TPU v7x, 512 devices: a whole 4x4x16 slice. The times are simulated.
512 devices in a mesh: men: 32 (over z_lo, y, core), women: 16 (over z_hi, x).
Axes of the slice: x: 4, y: 4, z: 16 (z_hi: 4, z_lo: 4; z = z_hi * 4 + z_lo), core: 2. Of those that a mesh axis runs over, the one named last changes fastest.
Arguments:
- men_embed: bfloat16 [65536, 128], P(('men', 'women')), may hold values from -4 to 4
- women_embed: bfloat16 [16384, 128], P(('women', 'men')), may hold values from -4 to 4
- men_count: int32 [65536], P('men'), may hold values from 1 to 297, as said below
- women_count: int32 [16384], P('women'), may hold values from 1 to 299
- women_root: float32 [16384], P('women'), may hold values from 0.5 to 6, as said below
- men_cotangent: float32 [65536], P('men'), may hold values from -300 to 300
- women_cotangent: float32 [16384], P('women'), may hold values from 24 to 864, as said below
Outputs:
- men_grad: float32 [65536, 128], P(('men', 'women'))
- women_grad: float32 [16384, 128], P(('women', 'men'))
Inputs may be any that keep to these rules, and one draw needn't show every extreme that they name: `men_count`: integer masses of the male types. `women_root`: positive. `women_cotangent`: positive.
All inputs are finite; a program needn't handle non-finite values.
Results may differ from a plain program's by a relative error of at most 0.0031.
Values may be sent and summed in bfloat16 or wider, within the bound.
No kernel may reach another device: no remote copies, remote signals or barrier semaphores. Data moves between devices by JAX's collectives and lax.ppermute only.
A program may use at most 64 MiB of HBM per device.

v0:
```python
import jax
import jax.numpy as jnp
from jax import lax
from jax.sharding import PartitionSpec as P


def kernel_tile(men_rows, women_block):
    surplus = lax.dot_general(
        men_rows, women_block, (((1,), (1,)), ((), ())), preferred_element_type=jnp.float32
    )
    return jnp.exp(0.5 * surplus)


def body(
    men_embed, women_embed, men_count, women_count, women_root, men_cotangent, women_cotangent
):
    men_rows = lax.all_gather(men_embed, "women", axis=0, tiled=True)
    women_rows = lax.all_gather(women_embed, "men", axis=0, tiled=True)
    men_mass = men_count.astype(jnp.float32)
    women_mass = women_count.astype(jnp.float32)
    stored = kernel_tile(men_rows, women_rows)

    def sweep(work):
        return work(stored, women_rows, 0)

    def first_work(kernel, women_block, col_start):
        weighted = kernel * women_root[None, :]
        product = jnp.dot(
            weighted.astype(jnp.bfloat16), women_block, preferred_element_type=jnp.float32
        )
        return ((jnp.sum(weighted, axis=1), product), ())

    row_partial, weighted_v = sweep(first_work)[0]
    row_mass = lax.psum(row_partial, "women")
    men_disc = jnp.sqrt(row_mass * row_mass + 4.0 * men_mass)
    men_root = 2.0 * men_mass / (row_mass + men_disc)

    def second_work(kernel, women_block, col_start):
        return ((), (jnp.sum(kernel * men_root[:, None], axis=0),))

    col_partial = sweep(second_work)[1][0]
    col_mass = lax.psum(col_partial, "men")
    women_disc = jnp.sqrt(col_mass * col_mass + 4.0 * women_mass)
    col_grad = -women_cotangent / women_disc

    def third_work(kernel, women_block, col_start):
        weighted = kernel * col_grad[None, :]
        product = jnp.dot(
            weighted.astype(jnp.bfloat16), women_block, preferred_element_type=jnp.float32
        )
        return ((jnp.sum(weighted, axis=1), product), ())

    row_back, direct_v = sweep(third_work)[0]
    row_cot = lax.psum(row_back, "women")
    row_grad = -(men_cotangent + men_root * row_cot) / men_disc
    men_term = 0.5 * (row_grad[:, None] * weighted_v + men_root[:, None] * direct_v)
    men_grad = lax.psum_scatter(men_term, "women", scatter_dimension=0, tiled=True)

    def fourth_work(kernel, women_block, col_start):
        tangent = (
            0.5
            * kernel
            * (row_grad[:, None] * women_root[None, :] + men_root[:, None] * col_grad[None, :])
        ).astype(jnp.bfloat16)
        return (
            (),
            (
                lax.dot_general(
                    tangent, men_rows, (((0,), (0,)), ((), ())), preferred_element_type=jnp.float32
                ),
            ),
        )

    women_terms = sweep(fourth_work)[1][0]
    women_grad = lax.psum_scatter(women_terms, "men", scatter_dimension=0, tiled=True)
    return (men_grad, women_grad)


def solution(mesh):
    return jax.shard_map(
        body,
        mesh=mesh,
        in_specs=(
            P(("men", "women"), None),
            P(("women", "men"), None),
            P("men"),
            P("women"),
            P("women"),
            P("men"),
            P("women"),
        ),
        out_specs=(P(("men", "women"), None), P(("women", "men"), None)),
        check_vma=False,
    )
```

profile of v0, /device:TPU:16, one launch (start us, length us, event | category | flops | bytes accessed | tf_op | source)
XLA Modules:
  0.0 561.4 jit_solution(11899115688756769913)
XLA Ops:
  7.2 0.0 copy-start.1
  7.2 0.0 reduce-scatter.5.cloned.1.call-start
  7.2 40.5 %all_gather.7 = bf16[1024,128]{1,0:T(8,128)(2,1)S(1)} all-gather(bf16[32,128]{1,0:T(8,128)(2,1)} %param.8), channel_id=1, replica_groups=mesh['men'=32,'women'=16] {'men'}, dimensions={0}, use_global_device_ids=true | all-gather | bytes 270336 | tf_op jit(solution)/shard_map/all_gather | solution.py:18
  47.8 60.0 %all_gather.6 = bf16[2048,128]{1,0:T(8,128)(2,1)S(1)} all-gather(bf16[128,128]{1,0:T(8,128)(2,1)} %param.7), channel_id=1, replica_groups=mesh['men'=32,'women'=16] {'women'}, dimensions={0}, use_global_device_ids=true | all-gather | bytes 557056 | tf_op jit(solution)/shard_map/all_gather | solution.py:17
  107.8 0.0 copy-start.3
  107.8 0.0 copy-start.4
  107.8 4.8 multiply_reduce_fusion.2
  112.6 46.8 %psum.21 = f32[2048]{0:T(1024)S(1)} all-reduce(f32[2048]{0:T(1024)S(1)} %get-tuple-element.2), channel_id=1, replica_groups=mesh['men'=32,'women'=16] {'women'}, use_global_device_ids=true, to_apply=%region_1.0 | all-reduce | flops 2048 | bytes 16384 | tf_op jit(solution)/shard_map/psum | solution.py:34
  159.4 0.0 copy-done.1
  159.4 0.0 copy-start.2
  159.5 0.0 copy-start
  159.5 4.0 multiply_reduce_fusion
  163.5 61.0 %psum.22 = f32[1024]{0:T(1024)S(1)} all-reduce(f32[1024]{0:T(1024)S(1)} %multiply_reduce_fusion), channel_id=1, replica_groups=mesh['men'=32,'women'=16] {'men'}, use_global_device_ids=true, to_apply=%region_3.0 | all-reduce | flops 1024 | bytes 8192 | tf_op jit(solution)/shard_map/psum | solution.py:42
  224.5 0.0 copy-done.3
  224.5 0.0 copy-done.4
  224.5 4.0 multiply_reduce_fusion.1
  228.5 48.8 %psum.23 = f32[2048]{0:T(1024)S(1)} all-reduce(f32[2048]{0:T(1024)S(1)} %multiply_reduce_fusion.1), channel_id=1, replica_groups=mesh['men'=32,'women'=16] {'women'}, use_global_device_ids=true, to_apply=%region_5.0 | all-reduce | flops 2048 | bytes 16384 | tf_op jit(solution)/shard_map/psum | solution.py:54
  277.3 0.0 copy-done.2
  277.4 0.0 copy-done
  277.4 5.9 %fusion.4 = f32[1024,128]{1,0:T(8,128)} fusion(bf16[2048,128]{1,0:T(8,128)(2,1)S(1)} %all_gather.6, f32[2048,1024]{0,1:T(8,128)} %get-tuple-element.3, f32[2048]{0:T(1024)S(1)} %negate_divide_fusion, f32[1024]{0:T(1024)S(1)} %rsqrt_multiply_fusion, f32[2048]{0:T(1024)S(1)} %add_divide_fusion, f32[1024]{0:T(1024)S(1)} %copy-done), kind=kOutput, calls=%fused_computation.11 | convolution fusion | flops 549453824 | bytes 9461760 | tf_op jit(solution)/shard_map/dot_general | solution.py:68
  283.3 0.0 reduce-scatter.5.cloned.1.call-update
  283.3 0.0 reduce-scatter.3.cloned.1.call-start
  283.3 5.0 fusion.5
  288.3 6.1 %fusion.8 = f32[2048,128]{1,0:T(8,128)} fusion(f32[2048,128]{1,0:T(8,128)S(1)} %fusion.5, bf16[1024,128]{1,0:T(8,128)(2,1)S(1)} %all_gather.7, f32[2048,1024]{0,1:T(8,128)} %get-tuple-element.3, f32[1024]{0:T(1024)S(1)} %copy-done, f32[2048]{0:T(1024)S(1)} %negate_divide_fusion), kind=kOutput, calls=%fused_computation.15 | convolution fusion | flops 541851648 | bytes 10760192 | tf_op jit(solution)/shard_map/dot_general | solution.py:28
  294.4 0.0 reduce-scatter.3.cloned.1.call-update
  294.4 132.8 %reduce-scatter.5.cloned.1.call-done = f32[32,128]{1,0:T(8,128)} async-done(((f32[1024,128]{1,0:T(8,128)}), f32[32,128]{1,0:T(8,128)}) %reduce-scatter.5.cloned.1.call-update) | async-done | bytes 16400 | tf_op jit(solution)/shard_map/reduce_scatter | solution.py:75
  427.2 127.3 %reduce-scatter.3.cloned.1.call-done = f32[128,128]{1,0:T(8,128)} async-done(((f32[2048,128]{1,0:T(8,128)}), f32[128,128]{1,0:T(8,128)}) %reduce-scatter.3.cloned.1.call-update) | async-done | bytes 65552 | tf_op jit(solution)/shard_map/reduce_scatter | solution.py:57
  (3 shorter events, 0.0 us)
Async XLA Ops:
  7.2 152.2 %copy-start.1 = (s32[2048]{0:T(1024)S(1)}, s32[2048]{0:T(1024)}, u32[]{:S(2)}) copy-start(s32[2048]{0:T(1024)} %param.9) | copy-start | bytes 24580
  7.2 420.1 %reduce-scatter.5.cloned.1.call-start = ((), (), s32[]{:S(2)}) async-start(), calls=%async_computation.3 | async-start | bytes 540672 | tf_op jit(solution)/shard_map/reduce_scatter | solution.py:75
  107.8 116.7 %copy-start.3 = (s32[1024]{0:T(1024)S(1)}, s32[1024]{0:T(1024)}, u32[]{:S(2)}) copy-start(s32[1024]{0:T(1024)} %param.10) | copy-start | bytes 12292
  107.8 116.7 %copy-start.4 = (f32[1024]{0:T(1024)S(1)}, f32[1024]{0:T(1024)}, u32[]{:S(2)}) copy-start(f32[1024]{0:T(1024)} %param.13) | copy-start | bytes 12292
  159.4 117.9 %copy-start.2 = (f32[2048]{0:T(1024)S(1)}, f32[2048]{0:T(1024)}, u32[]{:S(2)}) copy-start(f32[2048]{0:T(1024)} %param.12) | copy-start | bytes 24580
  159.5 117.9 %copy-start = (f32[1024]{0:T(1024)S(1)}, f32[1024]{0:T(1024)}, u32[]{:S(2)}) copy-start(f32[1024]{0:T(1024)} %param.11) | copy-start | bytes 12292
  283.3 271.2 %reduce-scatter.3.cloned.1.call-start = ((), (), s32[]{:S(2)}) async-start(), calls=%async_computation.2 | async-start | bytes 1114112 | tf_op jit(solution)/shard_map/reduce_scatter | solution.py:57
Sparse Core Ops, SparseCore 0:
  283.4 143.7 reduce-scatter.4
  431.9 122.5 reduce-scatter.2
where the time goes:
time: 562 us; the launch traced here: 561 us
  waiting for transfers between devices  260 us (46%)
  blocking collectives  257 us (46%)
  matrix products  21.8 us (4%)
  between operations  14.1 us (3%)
  other arithmetic  8.05 us (1%)
    reduce_scatter x1, waiting for transfers between devices, body(): lax.psum_scatter(women_terms, 'men', scatter_dimension=0, tiled=True)  133 us
    reduce_scatter x1, waiting for transfers between devices, body(): lax.psum_scatter(men_term, 'women', scatter_dimension=0, tiled=True)  127 us
    psum x1, blocking collectives, body(): col_mass = lax.psum(col_partial, 'men')  61 us
    all_gather x1, blocking collectives, body(): men_rows = lax.all_gather(men_embed, 'women', axis=0, tiled=True)  60 us
    psum x1, blocking collectives, body(): row_cot = lax.psum(row_back, 'women')  48.8 us
    psum x1, blocking collectives, body(): row_mass = lax.psum(row_partial, 'women')  46.8 us
    all_gather x1, blocking collectives, body(): women_rows = lax.all_gather(women_embed, 'men', axis=0, tiled=True)  40.5 us
  transfers between devices with their start and end apart: 2, of which 2 were waited for; matrix products, arithmetic and copies ran while one was open for 2% of the time, Pallas kernels for 0%

commit v1 on v0

v1 whole, which is shorter than its diff:
```python
import jax
import jax.numpy as jnp
from jax import lax
from jax.sharding import Mesh
from jax.sharding import PartitionSpec as P

MEN_AXES = ("zl", "y", "c")
WOMEN_AXES = ("zh", "x")
ALL_AXES = MEN_AXES + WOMEN_AXES


def kernel_tile(men_rows, women_block):
    surplus = lax.dot_general(
        men_rows, women_block, (((1,), (1,)), ((), ())), preferred_element_type=jnp.float32
    )
    return jnp.exp(0.5 * surplus)


def nested_psum(x, axes):
    for a in axes:
        x = lax.psum(x, a)
    return x


def nested_gather(x, axes):
    for a in reversed(axes):
        x = lax.all_gather(x, a, axis=0, tiled=True)
    return x


def halving_scatter(x, axes, sizes, order):
    rows = x.shape[0]
    block = rows
    for n in sizes:
        block //= n
    x = x.reshape(tuple(sizes) + (block,) + x.shape[1:])
    for a in order:
        d = axes.index(a)
        n = sizes[axes.index(a)]
        me = lax.axis_index(a)
        k = n // 2
        while k >= 1:
            width = x.shape[d] // 2
            bit = (me // k) % 2
            keep = lax.dynamic_slice_in_dim(x, bit * width, width, axis=d)
            send = lax.dynamic_slice_in_dim(x, (1 - bit) * width, width, axis=d)
            got = lax.ppermute(send, a, [(i, i ^ k) for i in range(n)])
            x = keep + got
            k //= 2
    return x.reshape((block,) + x.shape[len(sizes) + 1 :])


def make_body(men_sizes, women_sizes):
    def body(
        men_embed, women_embed, men_count, women_count, women_root, men_cotangent, women_cotangent
    ):
        men_rows = nested_gather(men_embed, WOMEN_AXES)
        women_rows = nested_gather(women_embed, MEN_AXES)
        men_mass = men_count.astype(jnp.float32)
        women_mass = women_count.astype(jnp.float32)
        kernel = kernel_tile(men_rows, women_rows)

        weighted = kernel * women_root[None, :]
        weighted_v = jnp.dot(
            weighted.astype(jnp.bfloat16), women_rows, preferred_element_type=jnp.float32
        )
        row_mass = nested_psum(jnp.sum(weighted, axis=1), ("x", "zh"))
        men_disc = jnp.sqrt(row_mass * row_mass + 4.0 * men_mass)
        men_root = 2.0 * men_mass / (row_mass + men_disc)

        col_partial = jnp.sum(kernel * men_root[:, None], axis=0)
        col_mass = nested_psum(col_partial, ("c", "y", "zl"))
        women_disc = jnp.sqrt(col_mass * col_mass + 4.0 * women_mass)
        col_grad = -women_cotangent / women_disc

        weighted = kernel * col_grad[None, :]
        direct_v = jnp.dot(
            weighted.astype(jnp.bfloat16), women_rows, preferred_element_type=jnp.float32
        )
        row_cot = nested_psum(jnp.sum(weighted, axis=1), ("x", "zh"))
        row_grad = -(men_cotangent + men_root * row_cot) / men_disc
        men_term = 0.5 * (row_grad[:, None] * weighted_v + men_root[:, None] * direct_v)

        tangent = (
            0.5
            * kernel
            * (row_grad[:, None] * women_root[None, :] + men_root[:, None] * col_grad[None, :])
        ).astype(jnp.bfloat16)
        women_terms = lax.dot_general(
            tangent, men_rows, (((0,), (0,)), ((), ())), preferred_element_type=jnp.float32
        )
        men_grad = halving_scatter(men_term, WOMEN_AXES, women_sizes, ("x", "zh"))
        women_grad = halving_scatter(women_terms, MEN_AXES, men_sizes, ("c", "y", "zl"))
        return (men_grad, women_grad)

    return body


def solution(mesh):
    men_n, women_n = mesh.shape["men"], mesh.shape["women"]
    women_sizes = (women_n // 4, 4)
    men_sizes = (men_n // 8, 4, 2)
    fine = Mesh(mesh.devices.reshape(men_sizes + women_sizes), ALL_AXES)
    return jax.shard_map(
        make_body(men_sizes, women_sizes),
        mesh=fine,
        in_specs=(
            P(ALL_AXES, None),
            P(WOMEN_AXES + MEN_AXES, None),
            P(MEN_AXES),
            P(WOMEN_AXES),
            P(WOMEN_AXES),
            P(MEN_AXES),
            P(WOMEN_AXES),
        ),
        out_specs=(P(ALL_AXES, None), P(WOMEN_AXES + MEN_AXES, None)),
        check_vma=False,
    )
```

time: 562 us -> 231 us (0.41)
  the two profiles are of different devices: /device:TPU:16 before, /device:TPU:2 now
where the time goes in v1:
time: 231 us; the launch traced here: 230 us
  blocking collectives  142 us (61%)
  waiting for transfers between devices  36.1 us (16%)
  starting transfers between devices  25.3 us (11%)
  matrix products  16 us (7%)
  other arithmetic  9.49 us (4%)
    all_gather x5, blocking collectives, nested_gather(): x = lax.all_gather(x, a, axis=0, tiled=True)  72.9 us
    psum x7, blocking collectives, nested_psum(): x = lax.psum(x, a)  69 us
    ppermute x9, waiting for transfers between devices, halving_scatter(): got = lax.ppermute(send, a, [(i, i ^ k) for i in range(n)])  36.1 us
    ppermute x9, starting transfers between devices, halving_scatter(): got = lax.ppermute(send, a, [(i, i ^ k) for i in range(n)])  25.3 us
    dot_general x2, matrix products, body(): jnp.dot(weighted.astype(jnp.bfloat16), women_rows, preferred_element_type...  6.66 us
    dot_general x1, matrix products, kernel_tile(): lax.dot_general(men_rows, women_block, (((1,), (1,)), ((), ())), preferre...  4.83 us
  transfers between devices with their start and end apart: 9, of which 5 were waited for; matrix products, arithmetic and copies ran while one was open for 3% of the time, Pallas kernels for 0%

profile of v1, /device:TPU:2, one launch (start us, length us, event | category | flops | bytes accessed | tf_op | source)
XLA Modules:
  0.0 230.3 jit_solution(14290723110834459367)
XLA Ops:
  0.6 0.0 copy-start.1
  0.7 2.0 all_gather.17
  2.7 12.4 %all_gather.18 = bf16[256,128]{1,0:T(8,128)(2,1)S(1)} all-gather(bf16[64,128]{1,0:T(8,128)(2,1)S(1)} %all_gather.17), channel_id=1, replica_groups=mesh['zl'=4,'y'=4,'c'=2,'zh'=4,'x'=4] {'y'}, dimensions={0}, use_global_device_ids=true | all-gather | bytes 81920 | tf_op jit(solution)/shard_map/all_gather | solution.py:27
  15.1 15.4 %all_gather.19 = bf16[1024,128]{1,0:T(8,128)(2,1)S(1)} all-gather(bf16[256,128]{1,0:T(8,128)(2,1)S(1)} %all_gather.18), channel_id=1, replica_groups=mesh['zl'=4,'y'=4,'c'=2,'zh'=4,'x'=4] {'zl'}, dimensions={0}, use_global_device_ids=true | all-gather | bytes 327680 | tf_op jit(solution)/shard_map/all_gather | solution.py:27
  30.4 13.0 %all_gather.15 = bf16[512,128]{1,0:T(8,128)(2,1)S(1)} all-gather(bf16[128,128]{1,0:T(8,128)(2,1)} %param.7), channel_id=1, replica_groups=mesh['zl'=4,'y'=4,'c'=2,'zh'=4,'x'=4] {'x'}, dimensions={0}, use_global_device_ids=true | all-gather | bytes 163840 | tf_op jit(solution)/shard_map/all_gather | solution.py:27
  43.4 30.2 %all_gather.16 = bf16[2048,128]{1,0:T(8,128)(2,1)S(1)} all-gather(bf16[512,128]{1,0:T(8,128)(2,1)S(1)} %all_gather.15), channel_id=1, replica_groups=mesh['zl'=4,'y'=4,'c'=2,'zh'=4,'x'=4] {'zh'}, dimensions={0}, use_global_device_ids=true | all-gather | bytes 655360 | tf_op jit(solution)/shard_map/all_gather | solution.py:27
  73.6 0.0 copy-start.3
  73.6 0.0 copy-start.4
  73.6 4.8 %multiply_reduce_fusion.2 = (f32[2048]{0:T(1024)S(1)}, f32[2048,1024]{0,1:T(8,128)}) fusion(f32[1024]{0:T(1024)} %param.11, bf16[2048,128]{1,0:T(8,128)(2,1)S(1)} %all_gather.16, bf16[1024,128]{1,0:T(8,128)(2,1)S(1)} %all_gather.19), kind=kOutput, calls=%fused_computation.6 | convolution fusion | flops 543160320 | bytes 9187328 | tf_op jit(solution)/shard_map/dot_general | solution.py:13
  78.4 8.4 %psum.49 = f32[2048]{0:T(1024)S(1)} all-reduce(f32[2048]{0:T(1024)S(1)} %get-tuple-element.2), channel_id=1, replica_groups=mesh['zl'=4,'y'=4,'c'=2,'zh'=4,'x'=4] {'x'}, use_global_device_ids=true, to_apply=%region_1.0 | all-reduce | flops 2048 | bytes 16384 | tf_op jit(solution)/shard_map/psum | solution.py:21
  86.8 12.5 %psum.50 = f32[2048]{0:T(1024)S(1)} all-reduce(f32[2048]{0:T(1024)S(1)} %psum.49), channel_id=1, replica_groups=mesh['zl'=4,'y'=4,'c'=2,'zh'=4,'x'=4] {'zh'}, use_global_device_ids=true, to_apply=%region_2.0 | all-reduce | flops 2048 | bytes 16384 | tf_op jit(solution)/shard_map/psum | solution.py:21
  99.3 0.0 copy-done.1
  99.3 0.0 copy-start.2
  99.3 0.0 copy-start
  99.3 4.0 %multiply_reduce_fusion = f32[1024]{0:T(1024)S(1)} fusion(f32[2048,1024]{0,1:T(8,128)} %get-tuple-element.3, f32[2048]{0:T(1024)S(1)} %add_divide_fusion), kind=kLoop, calls=%fused_computation.1 | loop fusion | flops 4193280 | bytes 8400896 | tf_op jit(solution)/shard_map/reduce_sum | solution.py:71
  103.4 2.5 %psum.51 = f32[1024]{0:T(1024)S(1)} all-reduce(f32[1024]{0:T(1024)S(1)} %multiply_reduce_fusion), channel_id=1, replica_groups=mesh['zl'=4,'y'=4,'c'=2,'zh'=4,'x'=4] {'c'}, use_global_device_ids=true, to_apply=%region_4.0 | all-reduce | flops 1024 | bytes 8192 | tf_op jit(solution)/shard_map/psum | solution.py:21
  105.8 10.2 %psum.52 = f32[1024]{0:T(1024)S(1)} all-reduce(f32[1024]{0:T(1024)S(1)} %psum.51), channel_id=1, replica_groups=mesh['zl'=4,'y'=4,'c'=2,'zh'=4,'x'=4] {'y'}, use_global_device_ids=true, to_apply=%region_5.0 | all-reduce | flops 1024 | bytes 8192 | tf_op jit(solution)/shard_map/psum | solution.py:21
  116.0 9.7 %psum.53 = f32[1024]{0:T(1024)S(1)} all-reduce(f32[1024]{0:T(1024)S(1)} %psum.52), channel_id=1, replica_groups=mesh['zl'=4,'y'=4,'c'=2,'zh'=4,'x'=4] {'zl'}, use_global_device_ids=true, to_apply=%region_6.0 | all-reduce | flops 1024 | bytes 8192 | tf_op jit(solution)/shard_map/psum | solution.py:21
  125.8 0.0 copy-done.3
  125.8 0.0 copy-done.4
  125.8 4.0 %multiply_reduce_fusion.1 = f32[2048]{0:T(1024)S(1)} fusion(f32[2048,1024]{0,1:T(8,128)} %get-tuple-element.3, f32[1024]{0:T(1024)S(1)} %rsqrt_multiply_fusion), kind=kLoop, calls=%fused_computation.4 | loop fusion | flops 4192256 | bytes 8400896 | tf_op jit(solution)/shard_map/reduce_sum | solution.py:80
  129.8 10.2 %psum.54 = f32[2048]{0:T(1024)S(1)} all-reduce(f32[2048]{0:T(1024)S(1)} %multiply_reduce_fusion.1), channel_id=1, replica_groups=mesh['zl'=4,'y'=4,'c'=2,'zh'=4,'x'=4] {'x'}, use_global_device_ids=true, to_apply=%region_8.0 | all-reduce | flops 2048 | bytes 16384 | tf_op jit(solution)/shard_map/psum | solution.py:21
  140.1 15.5 %psum.55 = f32[2048]{0:T(1024)S(1)} all-reduce(f32[2048]{0:T(1024)S(1)} %psum.54), channel_id=1, replica_groups=mesh['zl'=4,'y'=4,'c'=2,'zh'=4,'x'=4] {'zh'}, use_global_device_ids=true, to_apply=%region_9.0 | all-reduce | flops 2048 | bytes 16384 | tf_op jit(solution)/shard_map/psum | solution.py:21
  155.5 0.0 copy-done.2
  155.6 0.0 copy-done
  155.6 4.5 %fusion.4 = f32[1024,128]{1,0:T(8,128)S(1)} fusion(bf16[2048,128]{1,0:T(8,128)(2,1)S(1)} %all_gather.16, f32[2048,1024]{0,1:T(8,128)} %get-tuple-element.3, f32[2048]{0:T(1024)S(1)} %negate_divide_fusion, f32[1024]{0:T(1024)S(1)} %rsqrt_multiply_fusion, f32[2048]{0:T(1024)S(1)} %add_divide_fusion, f32[1024]{0:T(1024)S(1)} %copy-done), kind=kOutput, calls=%fused_computation.11 | convolution fusion | flops 549453824 | bytes 9461760 | tf_op jit(solution)/shard_map/dot_general | solution.py:89
  160.1 0.0 slice-start
  160.1 0.0 slice-start.1
  160.1 2.3 %collective-permute-start.4 = (f32[4,4,1,32,128]{4,3,2,1,0:T(8,128)S(1)}, f32[4,4,1,32,128]{4,3,2,1,0:T(8,128)S(1)}, u32[]{:S(2)}, u32[]{:S(2)}) collective-permute-start(f32[4,4,1,32,128]{4,3,2,1,0:T(8,128)S(1)} %constant_dynamic-slice_fusion.4), channel_id=1, source_target_pairs={{0,16},{16,0},{1,17},{17,1},{2,18},{18,2},{3,19},{19,3},{4,20},{20... | collective-permute-start | bytes 786440 | tf_op jit(solution)/shard_map/ppermute | solution.py:47
  162.4 5.1 %fusion.5 = f32[2048,128]{1,0:T(8,128)S(1)} fusion(bf16[1024,128]{1,0:T(8,128)(2,1)S(1)} %all_gather.19, f32[2048,1024]{0,1:T(8,128)} %get-tuple-element.3, f32[1024]{0:T(1024)S(1)} %rsqrt_multiply_fusion, f32[2048]{0:T(1024)S(1)} %add_divide_fusion), kind=kOutput, calls=%fused_computation.12 | convolution fusion | flops 541327360 | bytes 9711616 | tf_op jit(solution)/shard_map/dot_general | solution.py:77
  167.5 0.0 slice-done
  167.5 0.0 slice-done.1
  167.5 1.6 fusion.8
  169.2 2.8 %collective-permute-start = (f32[4,2,128,128]{3,2,1,0:T(8,128)S(1)}, f32[4,2,128,128]{3,2,1,0:T(8,128)S(1)}, u32[]{:S(2)}, u32[]{:S(2)}) collective-permute-start(f32[4,2,128,128]{3,2,1,0:T(8,128)S(1)} %constant_dynamic-slice_fusion.8), channel_id=1, source_target_pairs={{0,2},{1,3},{2,0},{3,1},{4,6},{5,7},{6,4},{7,5},{8,10},{9,11},{10,... | collective-permute-start | bytes 1572872 | tf_op jit(solution)/shard_map/ppermute | solution.py:47
  172.1 0.0 collective-permute-done.4
  172.1 2.8 %collective-permute-start.5 = (f32[4,2,1,32,128]{4,3,2,1,0:T(8,128)S(1)}, f32[4,2,1,32,128]{4,3,2,1,0:T(8,128)S(1)}, u32[]{:S(2)}, u32[]{:S(2)}) collective-permute-start(f32[4,2,1,32,128]{4,3,2,1,0:T(8,128)S(1)} %constant_dynamic-slice_fusion.3), channel_id=1, source_target_pairs={{0,64},{32,96},{64,0},{96,32},{1,65},{33,97},{65,1},{97,33},{2,66}... | collective-permute-start | bytes 393224 | tf_op jit(solution)/shard_map/ppermute | solution.py:47
  175.1 5.9 %collective-permute-done.5 = f32[4,2,1,32,128]{4,3,2,1,0:T(8,128)S(1)} collective-permute-done((f32[4,2,1,32,128]{4,3,2,1,0:T(8,128)S(1)}, f32[4,2,1,32,128]{4,3,2,1,0:T(8,128)S(1)}, u32[]{:S(2)}, u32[]{:S(2)}) %collective-permute-start.5) | collective-permute-done | bytes 131104 | tf_op jit(solution)/shard_map/ppermute | solution.py:47
  181.0 1.9 collective-permute-start.6
  182.9 3.8 %collective-permute-done = f32[4,2,128,128]{3,2,1,0:T(8,128)S(1)} collective-permute-done((f32[4,2,128,128]{3,2,1,0:T(8,128)S(1)}, f32[4,2,128,128]{3,2,1,0:T(8,128)S(1)}, u32[]{:S(2)}, u32[]{:S(2)}) %collective-permute-start) | collective-permute-done | bytes 524320 | tf_op jit(solution)/shard_map/ppermute | solution.py:47
  186.8 0.1 dynamic-slice_add_fusion
  186.8 1.9 collective-permute-start.1
  188.8 0.0 collective-permute-done.6
  188.8 1.9 collective-permute-start.7
  190.8 5.6 %collective-permute-done.1 = f32[4,1,128,128]{3,2,1,0:T(8,128)S(1)} collective-permute-done((f32[4,1,128,128]{3,2,1,0:T(8,128)S(1)}, f32[4,1,128,128]{3,2,1,0:T(8,128)S(1)}, u32[]{:S(2)}, u32[]{:S(2)}) %collective-permute-start.1) | collective-permute-done | bytes 262176 | tf_op jit(solution)/shard_map/ppermute | solution.py:47
  196.4 7.3 %collective-permute-start.2 = (f32[2,1,128,128]{3,2,1,0:T(8,128)S(1)}, f32[2,1,128,128]{3,2,1,0:T(8,128)S(1)}, u32[]{:S(2)}, u32[]{:S(2)}) collective-permute-start(f32[2,1,128,128]{3,2,1,0:T(8,128)S(1)} %constant_dynamic-slice_fusion.6), channel_id=1, source_target_pairs={{0,8},{4,12},{8,0},{12,4},{1,9},{5,13},{9,1},{13,5},{2,10},{6,14},... | collective-permute-start | bytes 393224 | tf_op jit(solution)/shard_map/ppermute | solution.py:47
  203.7 0.0 collective-permute-done.7
  203.8 1.9 collective-permute-start.8
  205.7 11.7 %collective-permute-done.2 = f32[2,1,128,128]{3,2,1,0:T(8,128)S(1)} collective-permute-done((f32[2,1,128,128]{3,2,1,0:T(8,128)S(1)}, f32[2,1,128,128]{3,2,1,0:T(8,128)S(1)}, u32[]{:S(2)}, u32[]{:S(2)}) %collective-permute-start.2) | collective-permute-done | bytes 131104 | tf_op jit(solution)/shard_map/ppermute | solution.py:47
  217.5 2.5 %collective-permute-start.3 = (f32[1,1,128,128]{3,2,1,0:T(8,128)S(1)}, f32[1,1,128,128]{3,2,1,0:T(8,128)S(1)}, u32[]{:S(2)}, u32[]{:S(2)}) collective-permute-start(f32[1,1,128,128]{3,2,1,0:T(8,128)S(1)} %constant_dynamic-slice_fusion.5), channel_id=1, source_target_pairs={{0,4},{4,0},{8,12},{12,8},{1,5},{5,1},{9,13},{13,9},{2,6},{6,2},{1... | collective-permute-start | bytes 196616 | tf_op jit(solution)/shard_map/ppermute | solution.py:47
  220.0 0.0 collective-permute-done.8
  220.0 0.6 add_bitcast_fusion.1
  220.6 9.0 %collective-permute-done.3 = f32[1,1,128,128]{3,2,1,0:T(8,128)S(1)} collective-permute-done((f32[1,1,128,128]{3,2,1,0:T(8,128)S(1)}, f32[1,1,128,128]{3,2,1,0:T(8,128)S(1)}, u32[]{:S(2)}, u32[]{:S(2)}) %collective-permute-start.3) | collective-permute-done | bytes 65568 | tf_op jit(solution)/shard_map/ppermute | solution.py:47
  229.7 0.6 add_bitcast_fusion
  (19 shorter events, 0.3 us)
Async XLA Ops:
  0.6 98.7 %copy-start.1 = (s32[2048]{0:T(1024)S(1)}, s32[2048]{0:T(1024)}, u32[]{:S(2)}) copy-start(s32[2048]{0:T(1024)} %param.9) | copy-start | bytes 24580
  73.6 52.2 %copy-start.3 = (s32[1024]{0:T(1024)S(1)}, s32[1024]{0:T(1024)}, u32[]{:S(2)}) copy-start(s32[1024]{0:T(1024)} %param.10) | copy-start | bytes 12292
  73.6 52.2 %copy-start.4 = (f32[1024]{0:T(1024)S(1)}, f32[1024]{0:T(1024)}, u32[]{:S(2)}) copy-start(f32[1024]{0:T(1024)} %param.13) | copy-start | bytes 12292
  99.3 56.2 %copy-start.2 = (f32[2048]{0:T(1024)S(1)}, f32[2048]{0:T(1024)}, u32[]{:S(2)}) copy-start(f32[2048]{0:T(1024)} %param.12) | copy-start | bytes 24580
  99.3 56.2 %copy-start = (f32[1024]{0:T(1024)S(1)}, f32[1024]{0:T(1024)}, u32[]{:S(2)}) copy-start(f32[1024]{0:T(1024)} %param.11) | copy-start | bytes 12292
  160.1 7.4 %slice-start = ((s8[8388608]{0:T(1024)(128)(4,1)}), s8[4194304]{0:T(1024)(128)(4,1)S(1)}, s32[]{:S(2)}) async-start(s8[8388608]{0:T(1024)(128)(4,1)} %bitcast.11), calls=%async_computation | async-start | bytes 8388608
  160.1 7.4 %slice-start.1 = ((s8[8388608]{0:T(1024)(128)(4,1)}), s8[4194304]{0:T(1024)(128)(4,1)S(1)}, s32[]{:S(2)}) async-start(s8[8388608]{0:T(1024)(128)(4,1)} %bitcast.11), calls=%async_computation.1 | async-start | bytes 8388608
  160.1 11.9 %collective-permute-start.4 = (f32[4,4,1,32,128]{4,3,2,1,0:T(8,128)S(1)}, f32[4,4,1,32,128]{4,3,2,1,0:T(8,128)S(1)}, u32[]{:S(2)}, u32[]{:S(2)}) collective-permute-start(f32[4,4,1,32,128]{4,3,2,1,0:T(8,128)S(1)} %constant_dynamic-slice_fusion.4), channel_id=1, source_target_pairs={{0,16},{16,0},{1,17},{17,1},{2,18},{18,2},{3,19},{19,3},{4,20},{20... | collective-permute-start | bytes 786440 | tf_op jit(solution)/shard_map/ppermute | solution.py:47
  169.2 17.5 %collective-permute-start = (f32[4,2,128,128]{3,2,1,0:T(8,128)S(1)}, f32[4,2,128,128]{3,2,1,0:T(8,128)S(1)}, u32[]{:S(2)}, u32[]{:S(2)}) collective-permute-start(f32[4,2,128,128]{3,2,1,0:T(8,128)S(1)} %constant_dynamic-slice_fusion.8), channel_id=1, source_target_pairs={{0,2},{1,3},{2,0},{3,1},{4,6},{5,7},{6,4},{7,5},{8,10},{9,11},{10,... | collective-permute-start | bytes 1572872 | tf_op jit(solution)/shard_map/ppermute | solution.py:47
  172.1 8.8 %collective-permute-start.5 = (f32[4,2,1,32,128]{4,3,2,1,0:T(8,128)S(1)}, f32[4,2,1,32,128]{4,3,2,1,0:T(8,128)S(1)}, u32[]{:S(2)}, u32[]{:S(2)}) collective-permute-start(f32[4,2,1,32,128]{4,3,2,1,0:T(8,128)S(1)} %constant_dynamic-slice_fusion.3), channel_id=1, source_target_pairs={{0,64},{32,96},{64,0},{96,32},{1,65},{33,97},{65,1},{97,33},{2,66}... | collective-permute-start | bytes 393224 | tf_op jit(solution)/shard_map/ppermute | solution.py:47
  181.0 7.8 %collective-permute-start.6 = (f32[4,1,1,32,128]{4,3,2,1,0:T(8,128)S(1)}, f32[4,1,1,32,128]{4,3,2,1,0:T(8,128)S(1)}, u32[]{:S(2)}, u32[]{:S(2)}) collective-permute-start(f32[4,1,1,32,128]{4,3,2,1,0:T(8,128)S(1)} %constant_dynamic-slice_fusion.2), channel_id=1, source_target_pairs={{0,32},{32,0},{64,96},{96,64},{1,33},{33,1},{65,97},{97,65},{2,34}... | collective-permute-start | bytes 196616 | tf_op jit(solution)/shard_map/ppermute | solution.py:47
  186.8 9.5 %collective-permute-start.1 = (f32[4,1,128,128]{3,2,1,0:T(8,128)S(1)}, f32[4,1,128,128]{3,2,1,0:T(8,128)S(1)}, u32[]{:S(2)}, u32[]{:S(2)}) collective-permute-start(f32[4,1,128,128]{3,2,1,0:T(8,128)S(1)} %constant_dynamic-slice_fusion.7), channel_id=1, source_target_pairs={{0,1},{1,0},{2,3},{3,2},{4,5},{5,4},{6,7},{7,6},{8,9},{9,8},{10,11... | collective-permute-start | bytes 786440 | tf_op jit(solution)/shard_map/ppermute | solution.py:47
  188.8 14.9 %collective-permute-start.7 = (f32[2,1,1,32,128]{4,3,2,1,0:T(8,128)S(1)}, f32[2,1,1,32,128]{4,3,2,1,0:T(8,128)S(1)}, u32[]{:S(2)}, u32[]{:S(2)}) collective-permute-start(f32[2,1,1,32,128]{4,3,2,1,0:T(8,128)S(1)} %constant_dynamic-slice_fusion.1), channel_id=1, source_target_pairs={{0,256},{128,384},{256,0},{384,128},{1,257},{129,385},{257,1},{385... | collective-permute-start | bytes 98312 | tf_op jit(solution)/shard_map/ppermute | solution.py:47
  196.4 21.0 %collective-permute-start.2 = (f32[2,1,128,128]{3,2,1,0:T(8,128)S(1)}, f32[2,1,128,128]{3,2,1,0:T(8,128)S(1)}, u32[]{:S(2)}, u32[]{:S(2)}) collective-permute-start(f32[2,1,128,128]{3,2,1,0:T(8,128)S(1)} %constant_dynamic-slice_fusion.6), channel_id=1, source_target_pairs={{0,8},{4,12},{8,0},{12,4},{1,9},{5,13},{9,1},{13,5},{2,10},{6,14},... | collective-permute-start | bytes 393224 | tf_op jit(solution)/shard_map/ppermute | solution.py:47
  203.8 16.2 %collective-permute-start.8 = (f32[1,1,1,32,128]{4,3,2,1,0:T(8,128)S(1)}, f32[1,1,1,32,128]{4,3,2,1,0:T(8,128)S(1)}, u32[]{:S(2)}, u32[]{:S(2)}) collective-permute-start(f32[1,1,1,32,128]{4,3,2,1,0:T(8,128)S(1)} %constant_dynamic-slice_fusion), channel_id=1, source_target_pairs={{0,128},{128,0},{256,384},{384,256},{1,129},{129,1},{257,385},{385... | collective-permute-start | bytes 49160 | tf_op jit(solution)/shard_map/ppermute | solution.py:47
  217.5 12.2 %collective-permute-start.3 = (f32[1,1,128,128]{3,2,1,0:T(8,128)S(1)}, f32[1,1,128,128]{3,2,1,0:T(8,128)S(1)}, u32[]{:S(2)}, u32[]{:S(2)}) collective-permute-start(f32[1,1,128,128]{3,2,1,0:T(8,128)S(1)} %constant_dynamic-slice_fusion.5), channel_id=1, source_target_pairs={{0,4},{4,0},{8,12},{12,8},{1,5},{5,1},{9,13},{13,9},{2,6},{6,2},{1... | collective-permute-start | bytes 196616 | tf_op jit(solution)/shard_map/ppermute | solution.py:47

commit v2 on v1

--- a/solution.py
+++ b/solution.py
@@ -22,10 +22,14 @@
     return x
 
 
-def nested_gather(x, axes):
-    for a in reversed(axes):
-        x = lax.all_gather(x, a, axis=0, tiled=True)
-    return x
+def ordered_gather(x, axes, order):
+    got = []
+    for a in order:
+        x = lax.all_gather(x, a, axis=0, tiled=False)
+        got.insert(0, a)
+    lead = len(axes)
+    x = jnp.transpose(x, [got.index(a) for a in axes] + list(range(lead, x.ndim)))
+    return x.reshape((-1,) + x.shape[lead + 1 :])
 
 
 def halving_scatter(x, axes, sizes, order):
@@ -54,8 +58,8 @@
     def body(
         men_embed, women_embed, men_count, women_count, women_root, men_cotangent, women_cotangent
     ):
-        men_rows = nested_gather(men_embed, WOMEN_AXES)
-        women_rows = nested_gather(women_embed, MEN_AXES)
+        men_rows = ordered_gather(men_embed, WOMEN_AXES, ("zh", "x"))
+        women_rows = ordered_gather(women_embed, MEN_AXES, ("zl", "y", "c"))
         men_mass = men_count.astype(jnp.float32)
         women_mass = women_count.astype(jnp.float32)
         kernel = kernel_tile(men_rows, women_rows)
@@ -80,6 +84,7 @@
         row_cot = nested_psum(jnp.sum(weighted, axis=1), ("x", "zh"))
         row_grad = -(men_cotangent + men_root * row_cot) / men_disc
         men_term = 0.5 * (row_grad[:, None] * weighted_v + men_root[:, None] * direct_v)
+        men_grad = halving_scatter(men_term, WOMEN_AXES, women_sizes, ("x", "zh"))
 
         tangent = (
             0.5
@@ -89,7 +94,6 @@
         women_terms = lax.dot_general(
             tangent, men_rows, (((0,), (0,)), ((), ())), preferred_element_type=jnp.float32
         )
-        men_grad = halving_scatter(men_term, WOMEN_AXES, women_sizes, ("x", "zh"))
         women_grad = halving_scatter(women_terms, MEN_AXES, men_sizes, ("c", "y", "zl"))
         return (men_grad, women_grad)
 

time: 231 us -> 228 us (0.987)
  waiting for transfers between devices: 36.1 us -> 28.2 us
  starting transfers between devices: 25.3 us -> 31.9 us
  blocking collectives: 142 us -> 136 us
  other arithmetic: 9.49 us -> 15.2 us
    ppermute x9, waiting for transfers between devices: 36.1 us -> 28.2 us  [halving_scatter(): got = lax.ppermute(send, a, [(i, i ^ k) for i in range(n)])]
    ppermute x9, starting transfers between devices: 25.3 us -> 31.9 us  [halving_scatter(): got = lax.ppermute(send, a, [(i, i ^ k) for i in range(n)])]
    all_gather x5, blocking collectives: 72.9 us -> 67.1 us  [ordered_gather(): x = lax.all_gather(x, a, axis=0, tiled=False)]
    convert_element_type x0 -> x1, other arithmetic: none -> 5.74 us  [body(): tangent = (0.5 * kernel * (row_grad[:, None] * women_root[None, :] + men_...]
where the time goes in v2:
time: 228 us
  blocking collectives  136 us (60%)
  starting transfers between devices  31.9 us (14%)
  waiting for transfers between devices  28.2 us (12%)
  other arithmetic  15.2 us (7%)
  matrix products  14.9 us (7%)
    psum x7, blocking collectives, nested_psum(): x = lax.psum(x, a)  68.7 us
    all_gather x5, blocking collectives, ordered_gather(): x = lax.all_gather(x, a, axis=0, tiled=False)  67.1 us
    ppermute x9, starting transfers between devices, halving_scatter(): got = lax.ppermute(send, a, [(i, i ^ k) for i in range(n)])  31.9 us
    ppermute x9, waiting for transfers between devices, halving_scatter(): got = lax.ppermute(send, a, [(i, i ^ k) for i in range(n)])  28.2 us
    dot_general x2, matrix products, body(): jnp.dot(weighted.astype(jnp.bfloat16), women_rows, preferred_element_type...  6.66 us
    convert_element_type x1, other arithmetic, body(): tangent = (0.5 * kernel * (row_grad[:, None] * women_root[None, :] + men_...  5.74 us
    dot_general x1, matrix products, kernel_tile(): lax.dot_general(men_rows, women_block, (((1,), (1,)), ((), ())), preferre...  4.82 us
  transfers between devices with their start and end apart: 9, of which 5 were waited for; matrix products, arithmetic and copies ran while one was open for 3% of the time, Pallas kernels for 0%

profile of v2, /device:TPU:2, one launch (start us, length us, event | category | flops | bytes accessed | tf_op | source)
XLA Modules:
  0.0 227.6 jit_solution(13019616032472987528)
XLA Ops:
  0.6 0.0 copy-start.1
  0.6 14.3 %all-gather.2 = bf16[128,128]{1,0:T(8,128)(2,1)S(1)} all-gather(bf16[32,128]{1,0:T(8,128)(2,1)} %param.8), channel_id=4, replica_groups=mesh['zl'=4,'y'=4,'c'=2,'zh'=4,'x'=4] {'zl'}, dimensions={0}, use_global_device_ids=true | all-gather | bytes 40960 | tf_op jit(solution)/shard_map/all_gather | solution.py:28
  14.9 12.5 %all-gather.3 = bf16[16,32,128]{2,1,0:T(8,128)(2,1)S(1)} all-gather(bf16[4,32,128]{2,1,0:T(8,128)(2,1)S(1)} %bitcast.45), channel_id=5, replica_groups=mesh['zl'=4,'y'=4,'c'=2,'zh'=4,'x'=4] {'y'}, dimensions={0}, use_global_device_ids=true | all-gather | bytes 163840 | tf_op jit(solution)/shard_map/all_gather | solution.py:28
  27.4 2.0 all-gather.4
  29.4 25.5 %all-gather = bf16[512,128]{1,0:T(8,128)(2,1)S(1)} all-gather(bf16[128,128]{1,0:T(8,128)(2,1)} %param.7), channel_id=2, replica_groups=mesh['zl'=4,'y'=4,'c'=2,'zh'=4,'x'=4] {'zh'}, dimensions={0}, use_global_device_ids=true | all-gather | bytes 163840 | tf_op jit(solution)/shard_map/all_gather | solution.py:28
  55.0 12.8 %all-gather.1 = bf16[16,128,128]{2,1,0:T(8,128)(2,1)S(1)} all-gather(bf16[4,128,128]{2,1,0:T(8,128)(2,1)S(1)} %bitcast.44), channel_id=3, replica_groups=mesh['zl'=4,'y'=4,'c'=2,'zh'=4,'x'=4] {'x'}, dimensions={0}, use_global_device_ids=true | all-gather | bytes 655360 | tf_op jit(solution)/shard_map/all_gather | solution.py:28
  67.8 0.0 copy-start.3
  67.8 0.0 copy-start.4
  67.9 4.8 %multiply_reduce_fusion.2 = (f32[2048]{0:T(1024)S(1)}, f32[2048,1024]{0,1:T(8,128)}) fusion(f32[1024]{0:T(1024)} %param.11, bf16[2048,128]{1,0:T(8,128)(2,1)S(1)} %bitcast.34, bf16[1024,128]{1,0:T(8,128)(2,1)S(1)} %bitcast.36), kind=kOutput, calls=%fused_computation.7 | convolution fusion | flops 543160320 | bytes 9187328 | tf_op jit(solution)/shard_map/dot_general | solution.py:13
  72.7 8.7 %psum.49 = f32[2048]{0:T(1024)S(1)} all-reduce(f32[2048]{0:T(1024)S(1)} %get-tuple-element.2), channel_id=1, replica_groups=mesh['zl'=4,'y'=4,'c'=2,'zh'=4,'x'=4] {'x'}, use_global_device_ids=true, to_apply=%region_1.0 | all-reduce | flops 2048 | bytes 16384 | tf_op jit(solution)/shard_map/psum | solution.py:21
  81.4 13.1 %psum.50 = f32[2048]{0:T(1024)S(1)} all-reduce(f32[2048]{0:T(1024)S(1)} %psum.49), channel_id=1, replica_groups=mesh['zl'=4,'y'=4,'c'=2,'zh'=4,'x'=4] {'zh'}, use_global_device_ids=true, to_apply=%region_2.0 | all-reduce | flops 2048 | bytes 16384 | tf_op jit(solution)/shard_map/psum | solution.py:21
  94.5 0.0 copy-done.1
  94.6 0.0 copy-start.2
  94.6 0.0 copy-start
  94.6 4.0 %multiply_reduce_fusion = f32[1024]{0:T(1024)S(1)} fusion(f32[2048,1024]{0,1:T(8,128)} %get-tuple-element.3, f32[2048]{0:T(1024)S(1)} %add_divide_fusion), kind=kLoop, calls=%fused_computation.2 | loop fusion | flops 4193280 | bytes 8400896 | tf_op jit(solution)/shard_map/reduce_sum | solution.py:75
  98.6 2.5 %psum.51 = f32[1024]{0:T(1024)S(1)} all-reduce(f32[1024]{0:T(1024)S(1)} %multiply_reduce_fusion), channel_id=1, replica_groups=mesh['zl'=4,'y'=4,'c'=2,'zh'=4,'x'=4] {'c'}, use_global_device_ids=true, to_apply=%region_4.0 | all-reduce | flops 1024 | bytes 8192 | tf_op jit(solution)/shard_map/psum | solution.py:21
  101.1 10.2 %psum.52 = f32[1024]{0:T(1024)S(1)} all-reduce(f32[1024]{0:T(1024)S(1)} %psum.51), channel_id=1, replica_groups=mesh['zl'=4,'y'=4,'c'=2,'zh'=4,'x'=4] {'y'}, use_global_device_ids=true, to_apply=%region_5.0 | all-reduce | flops 1024 | bytes 8192 | tf_op jit(solution)/shard_map/psum | solution.py:21
  111.3 10.4 %psum.53 = f32[1024]{0:T(1024)S(1)} all-reduce(f32[1024]{0:T(1024)S(1)} %psum.52), channel_id=1, replica_groups=mesh['zl'=4,'y'=4,'c'=2,'zh'=4,'x'=4] {'zl'}, use_global_device_ids=true, to_apply=%region_6.0 | all-reduce | flops 1024 | bytes 8192 | tf_op jit(solution)/shard_map/psum | solution.py:21
  121.7 0.0 copy-done.3
  121.7 0.0 copy-done.4
  121.7 4.0 %multiply_reduce_fusion.1 = f32[2048]{0:T(1024)S(1)} fusion(f32[2048,1024]{0,1:T(8,128)} %get-tuple-element.3, f32[1024]{0:T(1024)S(1)} %rsqrt_multiply_fusion), kind=kLoop, calls=%fused_computation.5 | loop fusion | flops 4192256 | bytes 8400896 | tf_op jit(solution)/shard_map/reduce_sum | solution.py:84
  125.7 9.7 %psum.54 = f32[2048]{0:T(1024)S(1)} all-reduce(f32[2048]{0:T(1024)S(1)} %multiply_reduce_fusion.1), channel_id=1, replica_groups=mesh['zl'=4,'y'=4,'c'=2,'zh'=4,'x'=4] {'x'}, use_global_device_ids=true, to_apply=%region_8.0 | all-reduce | flops 2048 | bytes 16384 | tf_op jit(solution)/shard_map/psum | solution.py:21
  135.5 14.1 %psum.55 = f32[2048]{0:T(1024)S(1)} all-reduce(f32[2048]{0:T(1024)S(1)} %psum.54), channel_id=1, replica_groups=mesh['zl'=4,'y'=4,'c'=2,'zh'=4,'x'=4] {'zh'}, use_global_device_ids=true, to_apply=%region_9.0 | all-reduce | flops 2048 | bytes 16384 | tf_op jit(solution)/shard_map/psum | solution.py:21
  149.6 0.0 copy-done.2
  149.6 0.0 copy-done
  149.6 5.7 %fusion = bf16[1024,2048]{1,0:T(8,128)(2,1)} fusion(f32[2048,1024]{0,1:T(8,128)} %get-tuple-element.3, f32[1024]{0:T(1024)S(1)} %rsqrt_multiply_fusion, f32[2048]{0:T(1024)S(1)} %add_divide_fusion, f32[1024]{0:T(1024)S(1)} %copy-done, f32[2048]{0:T(1024)S(1)} %negate_divide_fusion), kind=kLoop, calls=%fused_computation.1 | loop fusion | flops 12582912 | bytes 12607488 | tf_op jit(solution)/shard_map/convert_element_type | solution.py:93
  155.3 3.4 %fusion.9 = f32[4,4,2,32,128]{4,3,2,1,0:T(8,128)S(1)} fusion(bf16[4,4,2,32,2048]{4,3,2,1,0:T(8,128)(2,1)} %bitcast.33, bf16[2048,128,1,1,1]{1,0,4,3,2:T(8,128)(2,1)S(1)} %bitcast.35), kind=kOutput, calls=%fused_computation.38 | convolution fusion | flops 536870912 | bytes 5242880 | tf_op jit(solution)/shard_map/dot_general | solution.py:94
  158.8 0.0 slice-start
  158.8 0.0 slice-start.1
  158.8 2.3 %collective-permute-start.4 = (f32[4,4,1,32,128]{4,3,2,1,0:T(8,128)S(1)}, f32[4,4,1,32,128]{4,3,2,1,0:T(8,128)S(1)}, u32[]{:S(2)}, u32[]{:S(2)}) collective-permute-start(f32[4,4,1,32,128]{4,3,2,1,0:T(8,128)S(1)} %constant_dynamic-slice_fusion.4), channel_id=1, source_target_pairs={{0,16},{16,0},{1,17},{17,1},{2,18},{18,2},{3,19},{19,3},{4,20},{20... | collective-permute-start | bytes 786440 | tf_op jit(solution)/shard_map/ppermute | solution.py:51
  161.2 5.1 %fusion.5 = f32[2048,128]{1,0:T(8,128)S(1)} fusion(bf16[1024,128]{1,0:T(8,128)(2,1)S(1)} %bitcast.37, f32[2048,1024]{0,1:T(8,128)} %get-tuple-element.3, f32[1024]{0:T(1024)S(1)} %rsqrt_multiply_fusion, f32[2048]{0:T(1024)S(1)} %add_divide_fusion), kind=kOutput, calls=%fused_computation.12 | convolution fusion | flops 541327360 | bytes 9711616 | tf_op jit(solution)/shard_map/dot_general | solution.py:81
  166.2 0.0 slice-done
  166.2 0.0 slice-done.1
  166.3 1.6 fusion.8
  168.0 2.8 %collective-permute-start = (f32[4,2,128,128]{3,2,1,0:T(8,128)S(1)}, f32[4,2,128,128]{3,2,1,0:T(8,128)S(1)}, u32[]{:S(2)}, u32[]{:S(2)}) collective-permute-start(f32[4,2,128,128]{3,2,1,0:T(8,128)S(1)} %constant_dynamic-slice_fusion.8), channel_id=1, source_target_pairs={{0,2},{1,3},{2,0},{3,1},{4,6},{5,7},{6,4},{7,5},{8,10},{9,11},{10,... | collective-permute-start | bytes 1572872 | tf_op jit(solution)/shard_map/ppermute | solution.py:51
  170.8 0.0 collective-permute-done.4
  170.8 2.8 %collective-permute-start.5 = (f32[4,2,1,32,128]{4,3,2,1,0:T(8,128)S(1)}, f32[4,2,1,32,128]{4,3,2,1,0:T(8,128)S(1)}, u32[]{:S(2)}, u32[]{:S(2)}) collective-permute-start(f32[4,2,1,32,128]{4,3,2,1,0:T(8,128)S(1)} %constant_dynamic-slice_fusion.3), channel_id=1, source_target_pairs={{0,64},{32,96},{64,0},{96,32},{1,65},{33,97},{65,1},{97,33},{2,66}... | collective-permute-start | bytes 393224 | tf_op jit(solution)/shard_map/ppermute | solution.py:51
  173.8 5.9 %collective-permute-done.5 = f32[4,2,1,32,128]{4,3,2,1,0:T(8,128)S(1)} collective-permute-done((f32[4,2,1,32,128]{4,3,2,1,0:T(8,128)S(1)}, f32[4,2,1,32,128]{4,3,2,1,0:T(8,128)S(1)}, u32[]{:S(2)}, u32[]{:S(2)}) %collective-permute-start.5) | collective-permute-done | bytes 131104 | tf_op jit(solution)/shard_map/ppermute | solution.py:51
  179.7 1.9 collective-permute-start.6
  181.6 3.8 %collective-permute-done = f32[4,2,128,128]{3,2,1,0:T(8,128)S(1)} collective-permute-done((f32[4,2,128,128]{3,2,1,0:T(8,128)S(1)}, f32[4,2,128,128]{3,2,1,0:T(8,128)S(1)}, u32[]{:S(2)}, u32[]{:S(2)}) %collective-permute-start) | collective-permute-done | bytes 524320 | tf_op jit(solution)/shard_map/ppermute | solution.py:51
  185.5 0.1 dynamic-slice_add_fusion
  185.6 2.0 collective-permute-start.1
  187.6 0.0 collective-permute-done.6
  187.7 1.9 collective-permute-start.7
  189.6 5.5 %collective-permute-done.1 = f32[4,1,128,128]{3,2,1,0:T(8,128)S(1)} collective-permute-done((f32[4,1,128,128]{3,2,1,0:T(8,128)S(1)}, f32[4,1,128,128]{3,2,1,0:T(8,128)S(1)}, u32[]{:S(2)}, u32[]{:S(2)}) %collective-permute-start.1) | collective-permute-done | bytes 262176 | tf_op jit(solution)/shard_map/ppermute | solution.py:51
  195.2 7.3 %collective-permute-start.2 = (f32[2,1,128,128]{3,2,1,0:T(8,128)S(1)}, f32[2,1,128,128]{3,2,1,0:T(8,128)S(1)}, u32[]{:S(2)}, u32[]{:S(2)}) collective-permute-start(f32[2,1,128,128]{3,2,1,0:T(8,128)S(1)} %constant_dynamic-slice_fusion.6), channel_id=1, source_target_pairs={{0,8},{4,12},{8,0},{12,4},{1,9},{5,13},{9,1},{13,5},{2,10},{6,14},... | collective-permute-start | bytes 393224 | tf_op jit(solution)/shard_map/ppermute | solution.py:51
  202.4 0.0 collective-permute-done.7
  202.5 2.2 collective-permute-start.8
  204.7 9.3 %collective-permute-done.2 = f32[2,1,128,128]{3,2,1,0:T(8,128)S(1)} collective-permute-done((f32[2,1,128,128]{3,2,1,0:T(8,128)S(1)}, f32[2,1,128,128]{3,2,1,0:T(8,128)S(1)}, u32[]{:S(2)}, u32[]{:S(2)}) %collective-permute-start.2) | collective-permute-done | bytes 131104 | tf_op jit(solution)/shard_map/ppermute | solution.py:51
  214.1 8.7 %collective-permute-start.3 = (f32[1,1,128,128]{3,2,1,0:T(8,128)S(1)}, f32[1,1,128,128]{3,2,1,0:T(8,128)S(1)}, u32[]{:S(2)}, u32[]{:S(2)}) collective-permute-start(f32[1,1,128,128]{3,2,1,0:T(8,128)S(1)} %constant_dynamic-slice_fusion.5), channel_id=1, source_target_pairs={{0,4},{4,0},{8,12},{12,8},{1,5},{5,1},{9,13},{13,9},{2,6},{6,2},{1... | collective-permute-start | bytes 196616 | tf_op jit(solution)/shard_map/ppermute | solution.py:51
  222.7 0.0 collective-permute-done.8
  222.7 0.6 add_bitcast_fusion.1
  223.4 3.6 %collective-permute-done.3 = f32[1,1,128,128]{3,2,1,0:T(8,128)S(1)} collective-permute-done((f32[1,1,128,128]{3,2,1,0:T(8,128)S(1)}, f32[1,1,128,128]{3,2,1,0:T(8,128)S(1)}, u32[]{:S(2)}, u32[]{:S(2)}) %collective-permute-start.3) | collective-permute-done | bytes 65568 | tf_op jit(solution)/shard_map/ppermute | solution.py:51
  227.0 0.6 add_bitcast_fusion
  (21 shorter events, 0.4 us)
Async XLA Ops:
  0.6 93.9 %copy-start.1 = (s32[2048]{0:T(1024)S(1)}, s32[2048]{0:T(1024)}, u32[]{:S(2)}) copy-start(s32[2048]{0:T(1024)} %param.9) | copy-start | bytes 24580
  67.8 53.9 %copy-start.3 = (s32[1024]{0:T(1024)S(1)}, s32[1024]{0:T(1024)}, u32[]{:S(2)}) copy-start(s32[1024]{0:T(1024)} %param.10) | copy-start | bytes 12292
  67.8 53.9 %copy-start.4 = (f32[1024]{0:T(1024)S(1)}, f32[1024]{0:T(1024)}, u32[]{:S(2)}) copy-start(f32[1024]{0:T(1024)} %param.13) | copy-start | bytes 12292
  94.6 55.0 %copy-start.2 = (f32[2048]{0:T(1024)S(1)}, f32[2048]{0:T(1024)}, u32[]{:S(2)}) copy-start(f32[2048]{0:T(1024)} %param.12) | copy-start | bytes 24580
  94.6 55.0 %copy-start = (f32[1024]{0:T(1024)S(1)}, f32[1024]{0:T(1024)}, u32[]{:S(2)}) copy-start(f32[1024]{0:T(1024)} %param.11) | copy-start | bytes 12292
  158.8 7.4 %slice-start = ((s8[8388608]{0:T(1024)(128)(4,1)}), s8[4194304]{0:T(1024)(128)(4,1)S(1)}, s32[]{:S(2)}) async-start(s8[8388608]{0:T(1024)(128)(4,1)} %bitcast.31), calls=%async_computation | async-start | bytes 8388608
  158.8 7.4 %slice-start.1 = ((s8[8388608]{0:T(1024)(128)(4,1)}), s8[4194304]{0:T(1024)(128)(4,1)S(1)}, s32[]{:S(2)}) async-start(s8[8388608]{0:T(1024)(128)(4,1)} %bitcast.31), calls=%async_computation.1 | async-start | bytes 8388608
  158.8 11.9 %collective-permute-start.4 = (f32[4,4,1,32,128]{4,3,2,1,0:T(8,128)S(1)}, f32[4,4,1,32,128]{4,3,2,1,0:T(8,128)S(1)}, u32[]{:S(2)}, u32[]{:S(2)}) collective-permute-start(f32[4,4,1,32,128]{4,3,2,1,0:T(8,128)S(1)} %constant_dynamic-slice_fusion.4), channel_id=1, source_target_pairs={{0,16},{16,0},{1,17},{17,1},{2,18},{18,2},{3,19},{19,3},{4,20},{20... | collective-permute-start | bytes 786440 | tf_op jit(solution)/shard_map/ppermute | solution.py:51
  168.0 17.5 %collective-permute-start = (f32[4,2,128,128]{3,2,1,0:T(8,128)S(1)}, f32[4,2,128,128]{3,2,1,0:T(8,128)S(1)}, u32[]{:S(2)}, u32[]{:S(2)}) collective-permute-start(f32[4,2,128,128]{3,2,1,0:T(8,128)S(1)} %constant_dynamic-slice_fusion.8), channel_id=1, source_target_pairs={{0,2},{1,3},{2,0},{3,1},{4,6},{5,7},{6,4},{7,5},{8,10},{9,11},{10,... | collective-permute-start | bytes 1572872 | tf_op jit(solution)/shard_map/ppermute | solution.py:51
  170.8 8.8 %collective-permute-start.5 = (f32[4,2,1,32,128]{4,3,2,1,0:T(8,128)S(1)}, f32[4,2,1,32,128]{4,3,2,1,0:T(8,128)S(1)}, u32[]{:S(2)}, u32[]{:S(2)}) collective-permute-start(f32[4,2,1,32,128]{4,3,2,1,0:T(8,128)S(1)} %constant_dynamic-slice_fusion.3), channel_id=1, source_target_pairs={{0,64},{32,96},{64,0},{96,32},{1,65},{33,97},{65,1},{97,33},{2,66}... | collective-permute-start | bytes 393224 | tf_op jit(solution)/shard_map/ppermute | solution.py:51
  179.7 7.9 %collective-permute-start.6 = (f32[4,1,1,32,128]{4,3,2,1,0:T(8,128)S(1)}, f32[4,1,1,32,128]{4,3,2,1,0:T(8,128)S(1)}, u32[]{:S(2)}, u32[]{:S(2)}) collective-permute-start(f32[4,1,1,32,128]{4,3,2,1,0:T(8,128)S(1)} %constant_dynamic-slice_fusion.2), channel_id=1, source_target_pairs={{0,32},{32,0},{64,96},{96,64},{1,33},{33,1},{65,97},{97,65},{2,34}... | collective-permute-start | bytes 196616 | tf_op jit(solution)/shard_map/ppermute | solution.py:51
  185.6 9.5 %collective-permute-start.1 = (f32[4,1,128,128]{3,2,1,0:T(8,128)S(1)}, f32[4,1,128,128]{3,2,1,0:T(8,128)S(1)}, u32[]{:S(2)}, u32[]{:S(2)}) collective-permute-start(f32[4,1,128,128]{3,2,1,0:T(8,128)S(1)} %constant_dynamic-slice_fusion.7), channel_id=1, source_target_pairs={{0,1},{1,0},{2,3},{3,2},{4,5},{5,4},{6,7},{7,6},{8,9},{9,8},{10,11... | collective-permute-start | bytes 786440 | tf_op jit(solution)/shard_map/ppermute | solution.py:51
  187.7 14.8 %collective-permute-start.7 = (f32[2,1,1,32,128]{4,3,2,1,0:T(8,128)S(1)}, f32[2,1,1,32,128]{4,3,2,1,0:T(8,128)S(1)}, u32[]{:S(2)}, u32[]{:S(2)}) collective-permute-start(f32[2,1,1,32,128]{4,3,2,1,0:T(8,128)S(1)} %constant_dynamic-slice_fusion.1), channel_id=1, source_target_pairs={{0,256},{128,384},{256,0},{384,128},{1,257},{129,385},{257,1},{385... | collective-permute-start | bytes 98312 | tf_op jit(solution)/shard_map/ppermute | solution.py:51
  195.2 18.9 %collective-permute-start.2 = (f32[2,1,128,128]{3,2,1,0:T(8,128)S(1)}, f32[2,1,128,128]{3,2,1,0:T(8,128)S(1)}, u32[]{:S(2)}, u32[]{:S(2)}) collective-permute-start(f32[2,1,128,128]{3,2,1,0:T(8,128)S(1)} %constant_dynamic-slice_fusion.6), channel_id=1, source_target_pairs={{0,8},{4,12},{8,0},{12,4},{1,9},{5,13},{9,1},{13,5},{2,10},{6,14},... | collective-permute-start | bytes 393224 | tf_op jit(solution)/shard_map/ppermute | solution.py:51
  202.5 20.2 %collective-permute-start.8 = (f32[1,1,1,32,128]{4,3,2,1,0:T(8,128)S(1)}, f32[1,1,1,32,128]{4,3,2,1,0:T(8,128)S(1)}, u32[]{:S(2)}, u32[]{:S(2)}) collective-permute-start(f32[1,1,1,32,128]{4,3,2,1,0:T(8,128)S(1)} %constant_dynamic-slice_fusion), channel_id=1, source_target_pairs={{0,128},{128,0},{256,384},{384,256},{1,129},{129,1},{257,385},{385... | collective-permute-start | bytes 49160 | tf_op jit(solution)/shard_map/ppermute | solution.py:51
  214.1 12.9 %collective-permute-start.3 = (f32[1,1,128,128]{3,2,1,0:T(8,128)S(1)}, f32[1,1,128,128]{3,2,1,0:T(8,128)S(1)}, u32[]{:S(2)}, u32[]{:S(2)}) collective-permute-start(f32[1,1,128,128]{3,2,1,0:T(8,128)S(1)} %constant_dynamic-slice_fusion.5), channel_id=1, source_target_pairs={{0,4},{4,0},{8,12},{12,8},{1,5},{5,1},{9,13},{13,9},{2,6},{6,2},{1... | collective-permute-start | bytes 196616 | tf_op jit(solution)/shard_map/ppermute | solution.py:51

commit v3 on v2

--- a/solution.py
+++ b/solution.py
@@ -54,6 +54,15 @@
     return x.reshape((block,) + x.shape[len(sizes) + 1 :])
 
 
+def a2a_scatter(x, sizes, axes, order):
+    dims = list(axes)
+    for a in order:
+        d = dims.index(a)
+        x = jnp.sum(lax.all_to_all(x, a, d, 0, tiled=False), axis=0)
+        dims.pop(d)
+    return x
+
+
 def make_body(men_sizes, women_sizes):
     def body(
         men_embed, women_embed, men_count, women_count, women_root, men_cotangent, women_cotangent
@@ -84,7 +93,13 @@
         row_cot = nested_psum(jnp.sum(weighted, axis=1), ("x", "zh"))
         row_grad = -(men_cotangent + men_root * row_cot) / men_disc
         men_term = 0.5 * (row_grad[:, None] * weighted_v + men_root[:, None] * direct_v)
-        men_grad = halving_scatter(men_term, WOMEN_AXES, women_sizes, ("x", "zh"))
+        blk = men_term.shape[0] // (women_sizes[0] * women_sizes[1])
+        part = a2a_scatter(
+            men_term.reshape(women_sizes + (blk, men_term.shape[1])), women_sizes, WOMEN_AXES, ("x",)
+        )
+        men_grad = halving_scatter(
+            part.reshape(-1, part.shape[-1]), ("zh",), (women_sizes[0],), ("zh",)
+        )
 
         tangent = (
             0.5
@@ -94,7 +109,13 @@
         women_terms = lax.dot_general(
             tangent, men_rows, (((0,), (0,)), ((), ())), preferred_element_type=jnp.float32
         )
-        women_grad = halving_scatter(women_terms, MEN_AXES, men_sizes, ("c", "y", "zl"))
+        blk = women_terms.shape[0] // (men_sizes[0] * men_sizes[1] * men_sizes[2])
+        women_grad = a2a_scatter(
+            women_terms.reshape(men_sizes + (blk, women_terms.shape[1])),
+            men_sizes,
+            MEN_AXES,
+            ("c", "y", "zl"),
+        )
         return (men_grad, women_grad)
 
     return body

time: 228 us -> 228 us (level)
  the two profiles are of different devices: /device:TPU:2 before, /device:TPU:40 now
where the time goes in v3:
time: 228 us; the launch traced here: 227 us
  blocking collectives  132 us (58%)
  waiting for transfers between devices  34.2 us (15%)
  starting transfers between devices  27.3 us (12%)
  matrix products  16 us (7%)
  other arithmetic  14.6 us (6%)
  local copies, waits for them, and re-layouts  2.8 us (1%)
    psum x7, blocking collectives, nested_psum(): x = lax.psum(x, a)  66.2 us
    all_gather x5, blocking collectives, ordered_gather(): x = lax.all_gather(x, a, axis=0, tiled=False)  65.3 us
    ppermute x2, waiting for transfers between devices, halving_scatter(): got = lax.ppermute(send, a, [(i, i ^ k) for i in range(n)])  19 us
    all_to_all x4, starting transfers between devices, a2a_scatter(): x = jnp.sum(lax.all_to_all(x, a, d, 0, tiled=False), axis=0)  18.1 us
    all_to_all x4, waiting for transfers between devices, a2a_scatter(): x = jnp.sum(lax.all_to_all(x, a, d, 0, tiled=False), axis=0)  15.2 us
    dot_general x2, matrix products, body(): jnp.dot(weighted.astype(jnp.bfloat16), women_rows, preferred_element_type...  9.96 us
    ppermute x2, starting transfers between devices, halving_scatter(): got = lax.ppermute(send, a, [(i, i ^ k) for i in range(n)])  9.2 us
    dot_general x1, matrix products, kernel_tile(): lax.dot_general(men_rows, women_block, (((1,), (1,)), ((), ())), preferre...  4.82 us
  transfers between devices with their start and end apart: 6, of which 3 were waited for; matrix products, arithmetic and copies ran while one was open for 6% of the time, Pallas kernels for 0%

profile of v3, /device:TPU:40, one launch (start us, length us, event | category | flops | bytes accessed | tf_op | source)
XLA Modules:
  0.0 227.4 jit_solution(9170726571885241017)
XLA Ops:
  0.6 0.0 copy-start.1
  0.6 14.3 %all-gather.2 = bf16[128,128]{1,0:T(8,128)(2,1)S(1)} all-gather(bf16[32,128]{1,0:T(8,128)(2,1)} %param.8), channel_id=4, replica_groups=mesh['zl'=4,'y'=4,'c'=2,'zh'=4,'x'=4] {'zl'}, dimensions={0}, use_global_device_ids=true | all-gather | bytes 40960 | tf_op jit(solution)/shard_map/all_gather | solution.py:28
  14.9 12.2 %all-gather.3 = bf16[16,32,128]{2,1,0:T(8,128)(2,1)S(1)} all-gather(bf16[4,32,128]{2,1,0:T(8,128)(2,1)S(1)} %bitcast.44), channel_id=5, replica_groups=mesh['zl'=4,'y'=4,'c'=2,'zh'=4,'x'=4] {'y'}, dimensions={0}, use_global_device_ids=true | all-gather | bytes 163840 | tf_op jit(solution)/shard_map/all_gather | solution.py:28
  27.1 2.0 all-gather.4
  29.1 23.4 %all-gather = bf16[512,128]{1,0:T(8,128)(2,1)S(1)} all-gather(bf16[128,128]{1,0:T(8,128)(2,1)} %param.7), channel_id=2, replica_groups=mesh['zl'=4,'y'=4,'c'=2,'zh'=4,'x'=4] {'zh'}, dimensions={0}, use_global_device_ids=true | all-gather | bytes 163840 | tf_op jit(solution)/shard_map/all_gather | solution.py:28
  52.5 13.4 %all-gather.1 = bf16[16,128,128]{2,1,0:T(8,128)(2,1)S(1)} all-gather(bf16[4,128,128]{2,1,0:T(8,128)(2,1)S(1)} %bitcast.43), channel_id=3, replica_groups=mesh['zl'=4,'y'=4,'c'=2,'zh'=4,'x'=4] {'x'}, dimensions={0}, use_global_device_ids=true | all-gather | bytes 655360 | tf_op jit(solution)/shard_map/all_gather | solution.py:28
  66.0 0.0 copy-start.3
  66.0 0.0 copy-start.4
  66.0 4.8 %multiply_reduce_fusion.2 = (f32[2048]{0:T(1024)S(1)}, f32[2048,1024]{0,1:T(8,128)}) fusion(f32[1024]{0:T(1024)} %param.11, bf16[2048,128]{1,0:T(8,128)(2,1)S(1)} %bitcast.33, bf16[1024,128]{1,0:T(8,128)(2,1)S(1)} %bitcast.35), kind=kOutput, calls=%fused_computation.7 | convolution fusion | flops 543160320 | bytes 9187328 | tf_op jit(solution)/shard_map/dot_general | solution.py:13
  70.9 9.9 %psum.49 = f32[2048]{0:T(1024)S(1)} all-reduce(f32[2048]{0:T(1024)S(1)} %get-tuple-element.2), channel_id=1, replica_groups=mesh['zl'=4,'y'=4,'c'=2,'zh'=4,'x'=4] {'x'}, use_global_device_ids=true, to_apply=%region_1.0 | all-reduce | flops 2048 | bytes 16384 | tf_op jit(solution)/shard_map/psum | solution.py:21
  80.8 13.0 %psum.50 = f32[2048]{0:T(1024)S(1)} all-reduce(f32[2048]{0:T(1024)S(1)} %psum.49), channel_id=1, replica_groups=mesh['zl'=4,'y'=4,'c'=2,'zh'=4,'x'=4] {'zh'}, use_global_device_ids=true, to_apply=%region_2.0 | all-reduce | flops 2048 | bytes 16384 | tf_op jit(solution)/shard_map/psum | solution.py:21
  93.8 0.0 copy-done.1
  93.9 0.0 copy-start.2
  93.9 0.0 copy-start
  93.9 4.0 %multiply_reduce_fusion = f32[1024]{0:T(1024)S(1)} fusion(f32[2048,1024]{0,1:T(8,128)} %get-tuple-element.3, f32[2048]{0:T(1024)S(1)} %add_divide_fusion), kind=kLoop, calls=%fused_computation.2 | loop fusion | flops 4193280 | bytes 8400896 | tf_op jit(solution)/shard_map/reduce_sum | solution.py:84
  97.9 2.5 %psum.51 = f32[1024]{0:T(1024)S(1)} all-reduce(f32[1024]{0:T(1024)S(1)} %multiply_reduce_fusion), channel_id=1, replica_groups=mesh['zl'=4,'y'=4,'c'=2,'zh'=4,'x'=4] {'c'}, use_global_device_ids=true, to_apply=%region_4.0 | all-reduce | flops 1024 | bytes 8192 | tf_op jit(solution)/shard_map/psum | solution.py:21
  100.4 8.4 %psum.52 = f32[1024]{0:T(1024)S(1)} all-reduce(f32[1024]{0:T(1024)S(1)} %psum.51), channel_id=1, replica_groups=mesh['zl'=4,'y'=4,'c'=2,'zh'=4,'x'=4] {'y'}, use_global_device_ids=true, to_apply=%region_5.0 | all-reduce | flops 1024 | bytes 8192 | tf_op jit(solution)/shard_map/psum | solution.py:21
  108.8 10.4 %psum.53 = f32[1024]{0:T(1024)S(1)} all-reduce(f32[1024]{0:T(1024)S(1)} %psum.52), channel_id=1, replica_groups=mesh['zl'=4,'y'=4,'c'=2,'zh'=4,'x'=4] {'zl'}, use_global_device_ids=true, to_apply=%region_6.0 | all-reduce | flops 1024 | bytes 8192 | tf_op jit(solution)/shard_map/psum | solution.py:21
  119.2 0.0 copy-done.3
  119.2 0.0 copy-done.4
  119.2 4.0 %multiply_reduce_fusion.1 = f32[2048]{0:T(1024)S(1)} fusion(f32[2048,1024]{0,1:T(8,128)} %get-tuple-element.3, f32[1024]{0:T(1024)S(1)} %rsqrt_multiply_fusion), kind=kLoop, calls=%fused_computation.5 | loop fusion | flops 4192256 | bytes 8400896 | tf_op jit(solution)/shard_map/reduce_sum | solution.py:93
  123.2 7.8 %psum.54 = f32[2048]{0:T(1024)S(1)} all-reduce(f32[2048]{0:T(1024)S(1)} %multiply_reduce_fusion.1), channel_id=1, replica_groups=mesh['zl'=4,'y'=4,'c'=2,'zh'=4,'x'=4] {'x'}, use_global_device_ids=true, to_apply=%region_8.0 | all-reduce | flops 2048 | bytes 16384 | tf_op jit(solution)/shard_map/psum | solution.py:21
  131.1 14.2 %psum.55 = f32[2048]{0:T(1024)S(1)} all-reduce(f32[2048]{0:T(1024)S(1)} %psum.54), channel_id=1, replica_groups=mesh['zl'=4,'y'=4,'c'=2,'zh'=4,'x'=4] {'zh'}, use_global_device_ids=true, to_apply=%region_9.0 | all-reduce | flops 2048 | bytes 16384 | tf_op jit(solution)/shard_map/psum | solution.py:21
  145.2 0.0 copy-done.2
  145.3 0.0 copy-done
  145.3 4.5 %fusion = bf16[1024,2048]{1,0:T(8,128)(2,1)S(1)} fusion(f32[2048,1024]{0,1:T(8,128)} %get-tuple-element.3, f32[1024]{0:T(1024)S(1)} %rsqrt_multiply_fusion, f32[2048]{0:T(1024)S(1)} %add_divide_fusion, f32[1024]{0:T(1024)S(1)} %copy-done, f32[2048]{0:T(1024)S(1)} %negate_divide_fusion), kind=kLoop, calls=%fused_computation.1 | loop fusion | flops 12582912 | bytes 12607488 | tf_op jit(solution)/shard_map/convert_element_type | solution.py:108
  149.8 1.2 convolution_bitcast_fusion
  151.0 0.9 copy.24
  151.9 3.5 %all-to-all-start.1 = ((f32[1,4,4,2,32,128]{5,4,2,1,0,3:T(8,128)}), f32[1,4,4,2,32,128]{5,4,2,1,0,3:T(8,128)S(1)}, u32[]{:S(2)}, u32[]{:S(2)}) async-start(f32[1,4,4,2,32,128]{5,4,2,1,0,3:T(8,128)} %copy.24), calls=%async_computation.1 | async-start | bytes 1048576 | tf_op jit(solution)/shard_map/all_to_all | solution.py:61
  155.4 5.0 %fusion.5 = f32[2048,128]{1,0:T(8,128)S(1)} fusion(bf16[1024,128]{1,0:T(8,128)(2,1)S(1)} %bitcast.36, f32[2048,1024]{0,1:T(8,128)} %get-tuple-element.3, f32[1024]{0:T(1024)S(1)} %rsqrt_multiply_fusion, f32[2048]{0:T(1024)S(1)} %add_divide_fusion), kind=kOutput, calls=%fused_computation.12 | convolution fusion | flops 541327360 | bytes 9711616 | tf_op jit(solution)/shard_map/dot_general | solution.py:90
  160.4 5.0 %fusion.8 = f32[2048,128]{1,0:T(8,128)S(1)} fusion(f32[2048,128]{1,0:T(8,128)S(1)} %fusion.5, bf16[1024,128]{1,0:T(8,128)(2,1)S(1)} %bitcast.37, f32[2048,1024]{0,1:T(8,128)} %get-tuple-element.3, f32[1024]{0:T(1024)S(1)} %copy-done, f32[2048]{0:T(1024)S(1)} %negate_divide_fusion), kind=kOutput, calls=%fused_computation.15 | convolution fusion | flops 541851648 | bytes 10760192 | tf_op jit(solution)/shard_map/dot_general | solution.py:77
  165.4 1.1 copy.23
  166.5 0.0 all-to-all-done.1
  166.5 3.5 %all-to-all-start = ((f32[1,4,4,128,128]{4,3,1,0,2:T(8,128)}), f32[1,4,4,128,128]{4,3,1,0,2:T(8,128)S(1)}, u32[]{:S(2)}, u32[]{:S(2)}) async-start(f32[1,4,4,128,128]{4,3,1,0,2:T(8,128)} %copy.23), calls=%async_computation | async-start | bytes 2097152 | tf_op jit(solution)/shard_map/all_to_all | solution.py:61
  170.1 0.7 copy.25
  170.8 15.2 %all-to-all-done = f32[1,4,4,128,128]{4,3,1,0,2:T(8,128)S(1)} async-done(((f32[1,4,4,128,128]{4,3,1,0,2:T(8,128)}), f32[1,4,4,128,128]{4,3,1,0,2:T(8,128)S(1)}, u32[]{:S(2)}, u32[]{:S(2)}) %all-to-all-start) | async-done | bytes 1048608 | tf_op jit(solution)/shard_map/all_to_all | solution.py:61
  186.0 5.9 %all-to-all-start.2 = ((f32[1,4,4,32,128]{4,3,1,0,2:T(8,128)}), f32[1,4,4,32,128]{4,3,1,0,2:T(8,128)S(1)}, u32[]{:S(2)}, u32[]{:S(2)}) async-start(f32[1,4,4,32,128]{4,3,1,0,2:T(8,128)} %copy.25), calls=%async_computation.2 | async-start | bytes 524288 | tf_op jit(solution)/shard_map/all_to_all | solution.py:61
  191.8 0.1 reduce_sum.66
  191.9 7.3 %collective-permute-start = (f32[2,128,128]{2,1,0:T(8,128)S(1)}, f32[2,128,128]{2,1,0:T(8,128)S(1)}, u32[]{:S(2)}, u32[]{:S(2)}) collective-permute-start(f32[2,128,128]{2,1,0:T(8,128)S(1)} %constant_dynamic-slice_fusion.1), channel_id=1, source_target_pairs={{0,8},{4,12},{8,0},{12,4},{1,9},{5,13},{9,1},{13,5},{2,10},{6,14},... | collective-permute-start | bytes 393224 | tf_op jit(solution)/shard_map/ppermute | solution.py:51
  199.3 0.0 all-to-all-done.2
  199.3 0.6 reduce_sum.68
  199.9 5.2 %all-to-all-start.3 = ((f32[4,32,128]{2,1,0:T(8,128)}), f32[4,32,128]{2,1,0:T(8,128)S(1)}, u32[]{:S(2)}, u32[]{:S(2)}) async-start(f32[4,32,128]{2,1,0:T(8,128)} %reduce_sum.68), calls=%async_computation.3 | async-start | bytes 131072 | tf_op jit(solution)/shard_map/all_to_all | solution.py:61
  205.1 11.5 %collective-permute-done = f32[2,128,128]{2,1,0:T(8,128)S(1)} collective-permute-done((f32[2,128,128]{2,1,0:T(8,128)S(1)}, f32[2,128,128]{2,1,0:T(8,128)S(1)}, u32[]{:S(2)}, u32[]{:S(2)}) %collective-permute-start) | collective-permute-done | bytes 131104 | tf_op jit(solution)/shard_map/ppermute | solution.py:51
  216.7 1.9 collective-permute-start.1
  218.6 0.0 all-to-all-done.3
  218.6 0.6 reduce_sum.69
  219.2 7.5 %collective-permute-done.1 = f32[1,128,128]{2,1,0:T(8,128)S(1)} collective-permute-done((f32[1,128,128]{2,1,0:T(8,128)S(1)}, f32[1,128,128]{2,1,0:T(8,128)S(1)}, u32[]{:S(2)}, u32[]{:S(2)}) %collective-permute-start.1) | collective-permute-done | bytes 65568 | tf_op jit(solution)/shard_map/ppermute | solution.py:51
  226.7 0.6 add_bitcast_fusion
  (9 shorter events, 0.2 us)
Async XLA Ops:
  0.6 93.2 %copy-start.1 = (s32[2048]{0:T(1024)S(1)}, s32[2048]{0:T(1024)}, u32[]{:S(2)}) copy-start(s32[2048]{0:T(1024)} %param.9) | copy-start | bytes 24580
  66.0 53.1 %copy-start.3 = (s32[1024]{0:T(1024)S(1)}, s32[1024]{0:T(1024)}, u32[]{:S(2)}) copy-start(s32[1024]{0:T(1024)} %param.10) | copy-start | bytes 12292
  66.0 53.1 %copy-start.4 = (f32[1024]{0:T(1024)S(1)}, f32[1024]{0:T(1024)}, u32[]{:S(2)}) copy-start(f32[1024]{0:T(1024)} %param.13) | copy-start | bytes 12292
  93.9 51.4 %copy-start.2 = (f32[2048]{0:T(1024)S(1)}, f32[2048]{0:T(1024)}, u32[]{:S(2)}) copy-start(f32[2048]{0:T(1024)} %param.12) | copy-start | bytes 24580
  93.9 51.4 %copy-start = (f32[1024]{0:T(1024)S(1)}, f32[1024]{0:T(1024)}, u32[]{:S(2)}) copy-start(f32[1024]{0:T(1024)} %param.11) | copy-start | bytes 12292
  151.9 14.5 %all-to-all-start.1 = ((f32[1,4,4,2,32,128]{5,4,2,1,0,3:T(8,128)}), f32[1,4,4,2,32,128]{5,4,2,1,0,3:T(8,128)S(1)}, u32[]{:S(2)}, u32[]{:S(2)}) async-start(f32[1,4,4,2,32,128]{5,4,2,1,0,3:T(8,128)} %copy.24), calls=%async_computation.1 | async-start | bytes 1048576 | tf_op jit(solution)/shard_map/all_to_all | solution.py:61
  166.5 19.5 %all-to-all-start = ((f32[1,4,4,128,128]{4,3,1,0,2:T(8,128)}), f32[1,4,4,128,128]{4,3,1,0,2:T(8,128)S(1)}, u32[]{:S(2)}, u32[]{:S(2)}) async-start(f32[1,4,4,128,128]{4,3,1,0,2:T(8,128)} %copy.23), calls=%async_computation | async-start | bytes 2097152 | tf_op jit(solution)/shard_map/all_to_all | solution.py:61
  186.0 13.3 %all-to-all-start.2 = ((f32[1,4,4,32,128]{4,3,1,0,2:T(8,128)}), f32[1,4,4,32,128]{4,3,1,0,2:T(8,128)S(1)}, u32[]{:S(2)}, u32[]{:S(2)}) async-start(f32[1,4,4,32,128]{4,3,1,0,2:T(8,128)} %copy.25), calls=%async_computation.2 | async-start | bytes 524288 | tf_op jit(solution)/shard_map/all_to_all | solution.py:61
  191.9 24.7 %collective-permute-start = (f32[2,128,128]{2,1,0:T(8,128)S(1)}, f32[2,128,128]{2,1,0:T(8,128)S(1)}, u32[]{:S(2)}, u32[]{:S(2)}) collective-permute-start(f32[2,128,128]{2,1,0:T(8,128)S(1)} %constant_dynamic-slice_fusion.1), channel_id=1, source_target_pairs={{0,8},{4,12},{8,0},{12,4},{1,9},{5,13},{9,1},{13,5},{2,10},{6,14},... | collective-permute-start | bytes 393224 | tf_op jit(solution)/shard_map/ppermute | solution.py:51
  199.9 18.7 %all-to-all-start.3 = ((f32[4,32,128]{2,1,0:T(8,128)}), f32[4,32,128]{2,1,0:T(8,128)S(1)}, u32[]{:S(2)}, u32[]{:S(2)}) async-start(f32[4,32,128]{2,1,0:T(8,128)} %reduce_sum.68), calls=%async_computation.3 | async-start | bytes 131072 | tf_op jit(solution)/shard_map/all_to_all | solution.py:61
  216.7 10.1 %collective-permute-start.1 = (f32[1,128,128]{2,1,0:T(8,128)S(1)}, f32[1,128,128]{2,1,0:T(8,128)S(1)}, u32[]{:S(2)}, u32[]{:S(2)}) collective-permute-start(f32[1,128,128]{2,1,0:T(8,128)S(1)} %constant_dynamic-slice_fusion), channel_id=1, source_target_pairs={{0,4},{4,0},{8,12},{12,8},{1,5},{5,1},{9,13},{13,9},{2,6},{6,2},{1... | collective-permute-start | bytes 196616 | tf_op jit(solution)/shard_map/ppermute | solution.py:51

commit v4 on v3

--- a/solution.py
+++ b/solution.py
@@ -25,7 +25,8 @@
 def ordered_gather(x, axes, order):
     got = []
     for a in order:
-        x = lax.all_gather(x, a, axis=0, tiled=False)
+        n = lax.axis_size(a)
+        x = lax.all_to_all(jnp.broadcast_to(x[None], (n,) + x.shape), a, 0, 0, tiled=False)
         got.insert(0, a)
     lead = len(axes)
     x = jnp.transpose(x, [got.index(a) for a in axes] + list(range(lead, x.ndim)))

time: 228 us -> 224 us (0.982)
  the two profiles are of different devices: /device:TPU:40 before, /device:TPU:8 now
where the time goes in v4:
time: 224 us; the launch traced here: 223 us
  blocking collectives  123 us (55%)
  waiting for transfers between devices  37 us (17%)
  starting transfers between devices  29.7 us (13%)
  matrix products  16.2 us (7%)
  other arithmetic  11.2 us (5%)
  local copies, waits for them, and re-layouts  5.01 us (2%)
    psum x7, blocking collectives, nested_psum(): x = lax.psum(x, a)  66.7 us
    all_to_all x4, blocking collectives, ordered_gather(): lax.all_to_all(jnp.broadcast_to(x[None], (n,) + x.shape), a, 0, 0, tiled=...  51.8 us
    all_to_all x3, waiting for transfers between devices, a2a_scatter(): x = jnp.sum(lax.all_to_all(x, a, d, 0, tiled=False), axis=0)  14.8 us
    ppermute x2, waiting for transfers between devices, halving_scatter(): got = lax.ppermute(send, a, [(i, i ^ k) for i in range(n)])  14.2 us
    ppermute x2, starting transfers between devices, halving_scatter(): got = lax.ppermute(send, a, [(i, i ^ k) for i in range(n)])  14 us
    all_to_all x3, starting transfers between devices, a2a_scatter(): x = jnp.sum(lax.all_to_all(x, a, d, 0, tiled=False), axis=0)  11.3 us
    dot_general x2, matrix products, body(): jnp.dot(weighted.astype(jnp.bfloat16), women_rows, preferred_element_type...  10.1 us
    all_to_all x1, waiting for transfers between devices, ordered_gather(): lax.all_to_all(jnp.broadcast_to(x[None], (n,) + x.shape), a, 0, 0, tiled=...  8.06 us
  transfers between devices with their start and end apart: 6, of which 4 were waited for; matrix products, arithmetic and copies ran while one was open for 1% of the time, Pallas kernels for 0%

profile of v4, /device:TPU:8, one launch (start us, length us, event | category | flops | bytes accessed | tf_op | source)
XLA Modules:
  0.0 222.7 jit_solution(7307206107579980594)
XLA Ops:
  0.6 0.7 broadcast_in_dim.14
  1.3 11.3 %all_to_all.57 = bf16[4,32,128]{2,1,0:T(8,128)(2,1)S(1)} all-to-all(bf16[4,32,128]{2,1,0:T(8,128)(2,1)S(1)} %broadcast_in_dim.14), channel_id=1, replica_groups=mesh['zl'=4,'y'=4,'c'=2,'zh'=4,'x'=4] {'zl'}, dimensions={0} | all-to-all | bytes 65536 | tf_op jit(solution)/shard_map/all_to_all | solution.py:29
  12.7 9.4 %all_to_all.58 = bf16[4,4,32,128]{3,2,1,0:T(8,128)(2,1)S(1)} all-to-all(bf16[4,4,32,128]{3,2,1,0:T(8,128)(2,1)S(1)} %broadcast_in_dim.15), channel_id=1, replica_groups=mesh['zl'=4,'y'=4,'c'=2,'zh'=4,'x'=4] {'y'}, dimensions={0} | all-to-all | bytes 262144 | tf_op jit(solution)/shard_map/all_to_all | solution.py:29
  22.1 0.0 copy-start.2
  22.1 3.9 %all_to_all.59 = bf16[2,4,4,32,128]{4,3,1,2,0:T(8,128)(2,1)S(1)} all-to-all(bf16[2,4,4,32,128]{4,3,1,2,0:T(8,128)(2,1)S(1)} %broadcast_in_dim.16), channel_id=1, replica_groups=mesh['zl'=4,'y'=4,'c'=2,'zh'=4,'x'=4] {'c'}, dimensions={0} | all-to-all | bytes 524288 | tf_op jit(solution)/shard_map/all_to_all | solution.py:29
  26.1 0.8 broadcast_in_dim.12
  26.8 27.1 %all_to_all.60 = bf16[4,128,128]{2,1,0:T(8,128)(2,1)S(1)} all-to-all(bf16[4,128,128]{2,1,0:T(8,128)(2,1)S(1)} %broadcast_in_dim.12), channel_id=1, replica_groups=mesh['zl'=4,'y'=4,'c'=2,'zh'=4,'x'=4] {'zh'}, dimensions={0} | all-to-all | bytes 262144 | tf_op jit(solution)/shard_map/all_to_all | solution.py:29
  54.0 0.9 broadcast_in_dim.13
  54.9 4.3 %all-to-all-start.1 = ((bf16[4,4,128,128]{3,2,1,0:T(8,128)(2,1)}), bf16[4,4,128,128]{3,2,1,0:T(8,128)(2,1)S(1)}, u32[]{:S(2)}, u32[]{:S(2)}) async-start(bf16[4,4,128,128]{3,2,1,0:T(8,128)(2,1)} %broadcast_in_dim.13), calls=%async_computation.1 | async-start | bytes 1048576 | tf_op jit(solution)/shard_map/all_to_all | solution.py:29
  59.2 8.1 %all-to-all-done.1 = bf16[4,4,128,128]{3,2,1,0:T(8,128)(2,1)S(1)} async-done(((bf16[4,4,128,128]{3,2,1,0:T(8,128)(2,1)}), bf16[4,4,128,128]{3,2,1,0:T(8,128)(2,1)S(1)}, u32[]{:S(2)}, u32[]{:S(2)}) %all-to-all-start.1) | async-done | bytes 524320 | tf_op jit(solution)/shard_map/all_to_all | solution.py:29
  67.3 0.0 copy-start.4
  67.3 0.0 copy-start.5
  67.3 4.8 %multiply_reduce_fusion.2 = (f32[2048]{0:T(1024)S(1)}, f32[2048,1024]{0,1:T(8,128)}) fusion(f32[1024]{0:T(1024)} %param.11, bf16[2048,128]{1,0:T(8,128)(2,1)S(1)} %bitcast.27, bf16[1024,128]{1,0:T(8,128)(2,1)S(1)} %bitcast.29), kind=kOutput, calls=%fused_computation.7 | convolution fusion | flops 543160320 | bytes 9187328 | tf_op jit(solution)/shard_map/dot_general | solution.py:13
  72.1 9.0 %psum.49 = f32[2048]{0:T(1024)S(1)} all-reduce(f32[2048]{0:T(1024)S(1)} %get-tuple-element.2), channel_id=1, replica_groups=mesh['zl'=4,'y'=4,'c'=2,'zh'=4,'x'=4] {'x'}, use_global_device_ids=true, to_apply=%region_1.0 | all-reduce | flops 2048 | bytes 16384 | tf_op jit(solution)/shard_map/psum | solution.py:21
  81.1 13.1 %psum.50 = f32[2048]{0:T(1024)S(1)} all-reduce(f32[2048]{0:T(1024)S(1)} %psum.49), channel_id=1, replica_groups=mesh['zl'=4,'y'=4,'c'=2,'zh'=4,'x'=4] {'zh'}, use_global_device_ids=true, to_apply=%region_2.0 | all-reduce | flops 2048 | bytes 16384 | tf_op jit(solution)/shard_map/psum | solution.py:21
  94.2 0.0 copy-done.2
  94.2 4.0 %multiply_reduce_fusion = f32[1024]{0:T(1024)S(1)} fusion(f32[2048,1024]{0,1:T(8,128)} %get-tuple-element.3, f32[2048]{0:T(1024)S(1)} %add_divide_fusion), kind=kLoop, calls=%fused_computation.2 | loop fusion | flops 4193280 | bytes 8400896 | tf_op jit(solution)/shard_map/reduce_sum | solution.py:85
  98.2 2.5 %psum.51 = f32[1024]{0:T(1024)S(1)} all-reduce(f32[1024]{0:T(1024)S(1)} %multiply_reduce_fusion), channel_id=1, replica_groups=mesh['zl'=4,'y'=4,'c'=2,'zh'=4,'x'=4] {'c'}, use_global_device_ids=true, to_apply=%region_4.0 | all-reduce | flops 1024 | bytes 8192 | tf_op jit(solution)/shard_map/psum | solution.py:21
  100.7 9.2 %psum.52 = f32[1024]{0:T(1024)S(1)} all-reduce(f32[1024]{0:T(1024)S(1)} %psum.51), channel_id=1, replica_groups=mesh['zl'=4,'y'=4,'c'=2,'zh'=4,'x'=4] {'y'}, use_global_device_ids=true, to_apply=%region_5.0 | all-reduce | flops 1024 | bytes 8192 | tf_op jit(solution)/shard_map/psum | solution.py:21
  109.9 10.4 %psum.53 = f32[1024]{0:T(1024)S(1)} all-reduce(f32[1024]{0:T(1024)S(1)} %psum.52), channel_id=1, replica_groups=mesh['zl'=4,'y'=4,'c'=2,'zh'=4,'x'=4] {'zl'}, use_global_device_ids=true, to_apply=%region_6.0 | all-reduce | flops 1024 | bytes 8192 | tf_op jit(solution)/shard_map/psum | solution.py:21
  120.3 0.0 copy-done.4
  120.3 0.0 copy-done.5
  120.3 0.0 copy-start
  120.4 5.1 %fusion.5 = f32[2048,128]{1,0:T(8,128)S(1)} fusion(bf16[1024,128]{1,0:T(8,128)(2,1)S(1)} %bitcast.30, f32[2048,1024]{0,1:T(8,128)} %get-tuple-element.3, f32[1024]{0:T(1024)S(1)} %rsqrt_multiply_fusion, f32[2048]{0:T(1024)S(1)} %add_divide_fusion), kind=kOutput, calls=%fused_computation.12 | convolution fusion | flops 541327360 | bytes 9711616 | tf_op jit(solution)/shard_map/dot_general | solution.py:91
  125.5 0.6 copy-done
  126.1 0.0 copy-start.3
  126.1 0.0 copy-start.1
  126.1 0.6 multiply_reduce_fusion.1
  126.7 8.7 %psum.54 = f32[2048]{0:T(1024)S(1)} all-reduce(f32[2048]{0:T(1024)S(1)} %multiply_reduce_fusion.1), channel_id=1, replica_groups=mesh['zl'=4,'y'=4,'c'=2,'zh'=4,'x'=4] {'x'}, use_global_device_ids=true, to_apply=%region_8.0 | all-reduce | flops 2048 | bytes 16384 | tf_op jit(solution)/shard_map/psum | solution.py:21
  135.4 13.9 %psum.55 = f32[2048]{0:T(1024)S(1)} all-reduce(f32[2048]{0:T(1024)S(1)} %psum.54), channel_id=1, replica_groups=mesh['zl'=4,'y'=4,'c'=2,'zh'=4,'x'=4] {'zh'}, use_global_device_ids=true, to_apply=%region_9.0 | all-reduce | flops 2048 | bytes 16384 | tf_op jit(solution)/shard_map/psum | solution.py:21
  149.4 0.0 copy-done.3
  149.4 0.0 copy-done.1
  149.4 4.5 %fusion = bf16[1024,2048]{1,0:T(8,128)(2,1)S(1)} fusion(f32[2048,1024]{0,1:T(8,128)} %get-tuple-element.3, f32[1024]{0:T(1024)S(1)} %rsqrt_multiply_fusion, f32[2048]{0:T(1024)S(1)} %add_divide_fusion, f32[1024]{0:T(1024)S(1)} %copy-done.1, f32[2048]{0:T(1024)S(1)} %negate_divide_fusion), kind=kLoop, calls=%fused_computation.1 | loop fusion | flops 12582912 | bytes 12607488 | tf_op jit(solution)/shard_map/convert_element_type | solution.py:109
  153.9 5.0 %fusion.8 = f32[2048,128]{1,0:T(8,128)S(1)} fusion(f32[2048,128]{1,0:T(8,128)S(1)} %fusion.5, bf16[1024,128]{1,0:T(8,128)(2,1)S(1)} %bitcast.31, f32[2048,1024]{0,1:T(8,128)} %get-tuple-element.3, f32[1024]{0:T(1024)S(1)} %copy-done.1, f32[2048]{0:T(1024)S(1)} %negate_divide_fusion), kind=kOutput, calls=%fused_computation.15 | convolution fusion | flops 541851648 | bytes 10760192 | tf_op jit(solution)/shard_map/dot_general | solution.py:78
  158.9 1.1 copy.23
  159.9 1.2 convolution_bitcast_fusion
  161.2 4.2 %all_to_all.61 = f32[1,4,4,2,32,128]{5,4,2,1,0,3:T(8,128)S(1)} all-to-all(f32[1,4,4,2,32,128]{5,4,2,1,0,3:T(8,128)S(1)} %copy.24), channel_id=1, replica_groups=mesh['zl'=4,'y'=4,'c'=2,'zh'=4,'x'=4] {'c'}, dimensions={3} | all-to-all | bytes 1048576 | tf_op jit(solution)/shard_map/all_to_all | solution.py:62
  165.4 3.5 %all-to-all-start.5 = ((f32[1,4,4,128,128]{4,3,1,0,2:T(8,128)}), f32[1,4,4,128,128]{4,3,1,0,2:T(8,128)S(1)}, u32[]{:S(2)}, u32[]{:S(2)}) async-start(f32[1,4,4,128,128]{4,3,1,0,2:T(8,128)} %copy.23), calls=%async_computation.5 | async-start | bytes 2097152 | tf_op jit(solution)/shard_map/all_to_all | solution.py:62
  169.0 0.7 copy.25
  169.7 14.8 %all-to-all-done.5 = f32[1,4,4,128,128]{4,3,1,0,2:T(8,128)S(1)} async-done(((f32[1,4,4,128,128]{4,3,1,0,2:T(8,128)}), f32[1,4,4,128,128]{4,3,1,0,2:T(8,128)S(1)}, u32[]{:S(2)}, u32[]{:S(2)}) %all-to-all-start.5) | async-done | bytes 1048608 | tf_op jit(solution)/shard_map/all_to_all | solution.py:62
  184.5 4.5 %all-to-all-start.7 = ((f32[1,4,4,32,128]{4,3,1,0,2:T(8,128)}), f32[1,4,4,32,128]{4,3,1,0,2:T(8,128)S(1)}, u32[]{:S(2)}, u32[]{:S(2)}) async-start(f32[1,4,4,32,128]{4,3,1,0,2:T(8,128)} %copy.25), calls=%async_computation.7 | async-start | bytes 524288 | tf_op jit(solution)/shard_map/all_to_all | solution.py:62
  189.1 0.1 reduce_sum.66
  189.2 7.3 %collective-permute-start = (f32[2,128,128]{2,1,0:T(8,128)S(1)}, f32[2,128,128]{2,1,0:T(8,128)S(1)}, u32[]{:S(2)}, u32[]{:S(2)}) collective-permute-start(f32[2,128,128]{2,1,0:T(8,128)S(1)} %constant_dynamic-slice_fusion.1), channel_id=1, source_target_pairs={{0,8},{4,12},{8,0},{12,4},{1,9},{5,13},{9,1},{13,5},{2,10},{6,14},... | collective-permute-start | bytes 393224 | tf_op jit(solution)/shard_map/ppermute | solution.py:52
  196.5 0.0 all-to-all-done.7
  196.5 0.6 reduce_sum.68
  197.2 3.3 %all-to-all-start.8 = ((f32[4,32,128]{2,1,0:T(8,128)}), f32[4,32,128]{2,1,0:T(8,128)S(1)}, u32[]{:S(2)}, u32[]{:S(2)}) async-start(f32[4,32,128]{2,1,0:T(8,128)} %reduce_sum.68), calls=%async_computation.8 | async-start | bytes 131072 | tf_op jit(solution)/shard_map/all_to_all | solution.py:62
  200.5 10.8 %collective-permute-done = f32[2,128,128]{2,1,0:T(8,128)S(1)} collective-permute-done((f32[2,128,128]{2,1,0:T(8,128)S(1)}, f32[2,128,128]{2,1,0:T(8,128)S(1)}, u32[]{:S(2)}, u32[]{:S(2)}) %collective-permute-start) | collective-permute-done | bytes 131104 | tf_op jit(solution)/shard_map/ppermute | solution.py:52
  211.3 6.8 %collective-permute-start.1 = (f32[1,128,128]{2,1,0:T(8,128)S(1)}, f32[1,128,128]{2,1,0:T(8,128)S(1)}, u32[]{:S(2)}, u32[]{:S(2)}) collective-permute-start(f32[1,128,128]{2,1,0:T(8,128)S(1)} %constant_dynamic-slice_fusion), channel_id=1, source_target_pairs={{0,4},{4,0},{8,12},{12,8},{1,5},{5,1},{9,13},{13,9},{2,6},{6,2},{1... | collective-permute-start | bytes 196616 | tf_op jit(solution)/shard_map/ppermute | solution.py:52
  218.1 0.0 all-to-all-done.8
  218.1 0.6 reduce_sum.69
  218.7 3.4 %collective-permute-done.1 = f32[1,128,128]{2,1,0:T(8,128)S(1)} collective-permute-done((f32[1,128,128]{2,1,0:T(8,128)S(1)}, f32[1,128,128]{2,1,0:T(8,128)S(1)}, u32[]{:S(2)}, u32[]{:S(2)}) %collective-permute-start.1) | collective-permute-done | bytes 65568 | tf_op jit(solution)/shard_map/ppermute | solution.py:52
  222.1 0.6 add_bitcast_fusion
  (13 shorter events, 0.3 us)
Async XLA Ops:
  22.1 72.1 %copy-start.2 = (s32[2048]{0:T(1024)S(1)}, s32[2048]{0:T(1024)}, u32[]{:S(2)}) copy-start(s32[2048]{0:T(1024)} %param.9) | copy-start | bytes 24580
  54.9 12.4 %all-to-all-start.1 = ((bf16[4,4,128,128]{3,2,1,0:T(8,128)(2,1)}), bf16[4,4,128,128]{3,2,1,0:T(8,128)(2,1)S(1)}, u32[]{:S(2)}, u32[]{:S(2)}) async-start(bf16[4,4,128,128]{3,2,1,0:T(8,128)(2,1)} %broadcast_in_dim.13), calls=%async_computation.1 | async-start | bytes 1048576 | tf_op jit(solution)/shard_map/all_to_all | solution.py:29
  67.3 53.0 %copy-start.4 = (s32[1024]{0:T(1024)S(1)}, s32[1024]{0:T(1024)}, u32[]{:S(2)}) copy-start(s32[1024]{0:T(1024)} %param.10) | copy-start | bytes 12292
  67.3 53.0 %copy-start.5 = (f32[1024]{0:T(1024)S(1)}, f32[1024]{0:T(1024)}, u32[]{:S(2)}) copy-start(f32[1024]{0:T(1024)} %param.13) | copy-start | bytes 12292
  120.3 5.8 %copy-start = (f32[2048,1024]{0,1:T(8,128)S(1)}, f32[2048,1024]{0,1:T(8,128)}, u32[]{:S(2)}) copy-start(f32[2048,1024]{0,1:T(8,128)} %get-tuple-element.3) | copy-start | bytes 25165828
  126.1 23.2 %copy-start.3 = (f32[2048]{0:T(1024)S(1)}, f32[2048]{0:T(1024)}, u32[]{:S(2)}) copy-start(f32[2048]{0:T(1024)} %param.12) | copy-start | bytes 24580
  126.1 23.3 %copy-start.1 = (f32[1024]{0:T(1024)S(1)}, f32[1024]{0:T(1024)}, u32[]{:S(2)}) copy-start(f32[1024]{0:T(1024)} %param.11) | copy-start | bytes 12292
  165.4 19.2 %all-to-all-start.5 = ((f32[1,4,4,128,128]{4,3,1,0,2:T(8,128)}), f32[1,4,4,128,128]{4,3,1,0,2:T(8,128)S(1)}, u32[]{:S(2)}, u32[]{:S(2)}) async-start(f32[1,4,4,128,128]{4,3,1,0,2:T(8,128)} %copy.23), calls=%async_computation.5 | async-start | bytes 2097152 | tf_op jit(solution)/shard_map/all_to_all | solution.py:62
  184.5 12.0 %all-to-all-start.7 = ((f32[1,4,4,32,128]{4,3,1,0,2:T(8,128)}), f32[1,4,4,32,128]{4,3,1,0,2:T(8,128)S(1)}, u32[]{:S(2)}, u32[]{:S(2)}) async-start(f32[1,4,4,32,128]{4,3,1,0,2:T(8,128)} %copy.25), calls=%async_computation.7 | async-start | bytes 524288 | tf_op jit(solution)/shard_map/all_to_all | solution.py:62
  189.2 22.1 %collective-permute-start = (f32[2,128,128]{2,1,0:T(8,128)S(1)}, f32[2,128,128]{2,1,0:T(8,128)S(1)}, u32[]{:S(2)}, u32[]{:S(2)}) collective-permute-start(f32[2,128,128]{2,1,0:T(8,128)S(1)} %constant_dynamic-slice_fusion.1), channel_id=1, source_target_pairs={{0,8},{4,12},{8,0},{12,4},{1,9},{5,13},{9,1},{13,5},{2,10},{6,14},... | collective-permute-start | bytes 393224 | tf_op jit(solution)/shard_map/ppermute | solution.py:52
  197.2 20.9 %all-to-all-start.8 = ((f32[4,32,128]{2,1,0:T(8,128)}), f32[4,32,128]{2,1,0:T(8,128)S(1)}, u32[]{:S(2)}, u32[]{:S(2)}) async-start(f32[4,32,128]{2,1,0:T(8,128)} %reduce_sum.68), calls=%async_computation.8 | async-start | bytes 131072 | tf_op jit(solution)/shard_map/all_to_all | solution.py:62
  211.3 10.8 %collective-permute-start.1 = (f32[1,128,128]{2,1,0:T(8,128)S(1)}, f32[1,128,128]{2,1,0:T(8,128)S(1)}, u32[]{:S(2)}, u32[]{:S(2)}) collective-permute-start(f32[1,128,128]{2,1,0:T(8,128)S(1)} %constant_dynamic-slice_fusion), channel_id=1, source_target_pairs={{0,4},{4,0},{8,12},{12,8},{1,5},{5,1},{9,13},{13,9},{2,6},{6,2},{1... | collective-permute-start | bytes 196616 | tf_op jit(solution)/shard_map/ppermute | solution.py:52

commit v5 on v4

--- a/solution.py
+++ b/solution.py
@@ -31,6 +31,18 @@
     lead = len(axes)
     x = jnp.transpose(x, [got.index(a) for a in axes] + list(range(lead, x.ndim)))
     return x.reshape((-1,) + x.shape[lead + 1 :])
+
+
+def doubling_gather(x, axis, n):
+    me = lax.axis_index(axis)
+    x = x[None]
+    k = 1
+    while k < n:
+        got = lax.ppermute(x, axis, [(i, i ^ k) for i in range(n)])
+        low = (me // k) % 2 == 0
+        x = jnp.concatenate([jnp.where(low, x, got), jnp.where(low, got, x)], axis=0)
+        k *= 2
+    return x
 
 
 def halving_scatter(x, axes, sizes, order):
@@ -68,7 +80,10 @@
     def body(
         men_embed, women_embed, men_count, women_count, women_root, men_cotangent, women_cotangent
     ):
-        men_rows = ordered_gather(men_embed, WOMEN_AXES, ("zh", "x"))
+        part = doubling_gather(men_embed, "zh", women_sizes[0])
+        n = women_sizes[1]
+        part = lax.all_to_all(jnp.broadcast_to(part[None], (n,) + part.shape), "x", 0, 0, tiled=False)
+        men_rows = jnp.swapaxes(part, 0, 1).reshape((-1,) + men_embed.shape[1:])
         women_rows = ordered_gather(women_embed, MEN_AXES, ("zl", "y", "c"))
         men_mass = men_count.astype(jnp.float32)
         women_mass = women_count.astype(jnp.float32)

time: 224 us -> 224 us (level)
  the two profiles are of different devices: /device:TPU:8 before, /device:TPU:40 now
where the time goes in v5:
time: 224 us; the launch traced here: 223 us
  blocking collectives  74.1 us (33%)
  starting transfers between devices  59 us (26%)
  waiting for transfers between devices  55.3 us (25%)
  matrix products  16.2 us (7%)
  other arithmetic  12 us (5%)
  local copies, waits for them, and re-layouts  5.49 us (2%)
    psum x7, blocking collectives, nested_psum(): x = lax.psum(x, a)  66 us
    ppermute x2, starting transfers between devices, doubling_gather(): got = lax.ppermute(x, axis, [(i, i ^ k) for i in range(n)])  23.1 us
    ppermute x2, waiting for transfers between devices, halving_scatter(): got = lax.ppermute(send, a, [(i, i ^ k) for i in range(n)])  19.8 us
    all_to_all x3, waiting for transfers between devices, a2a_scatter(): x = jnp.sum(lax.all_to_all(x, a, d, 0, tiled=False), axis=0)  14.9 us
    all_to_all x3, starting transfers between devices, a2a_scatter(): x = jnp.sum(lax.all_to_all(x, a, d, 0, tiled=False), axis=0)  12.2 us
    all_to_all x2, starting transfers between devices, ordered_gather(): lax.all_to_all(jnp.broadcast_to(x[None], (n,) + x.shape), a, 0, 0, tiled=...  10.2 us
    dot_general x2, matrix products, body(): jnp.dot(weighted.astype(jnp.bfloat16), women_rows, preferred_element_type...  10.1 us
    all_to_all x1, waiting for transfers between devices, body(): lax.all_to_all(jnp.broadcast_to(part[None], (n,) + part.shape), 'x', 0, 0...  9.76 us
  transfers between devices with their start and end apart: 10, of which 7 were waited for; matrix products, arithmetic and copies ran while one was open for 2% of the time, Pallas kernels for 0%

profile of v5, /device:TPU:40, one launch (start us, length us, event | category | flops | bytes accessed | tf_op | source)
XLA Modules:
  0.0 223.0 jit_solution(324824727895681656)
XLA Ops:
  0.6 9.1 %collective-permute-start = (bf16[1,128,128]{2,1,0:T(8,128)(2,1)}, bf16[1,128,128]{2,1,0:T(8,128)(2,1)S(1)}, u32[]{:S(2)}, u32[]{:S(2)}) collective-permute-start(bf16[1,128,128]{2,1,0:T(8,128)(2,1)} %bitcast.38), channel_id=1, source_target_pairs={{0,4},{4,0},{8,12},{12,8},{1,5},{5,1},{9,13},{13,9},{2,6},{6,2},{1... | collective-permute-start | bytes 98312 | tf_op jit(solution)/shard_map/ppermute | solution.py:41
  9.7 2.1 collective-permute-done
  11.8 0.8 broadcast_select_fusion.3
  12.6 14.0 %collective-permute-start.1 = (bf16[2,128,128]{2,1,0:T(8,128)(2,1)S(1)}, bf16[2,128,128]{2,1,0:T(8,128)(2,1)S(1)}, u32[]{:S(2)}, u32[]{:S(2)}) collective-permute-start(bf16[2,128,128]{2,1,0:T(8,128)(2,1)S(1)} %pad_maximum_fusion.1), channel_id=1, source_target_pairs={{0,8},{4,12},{8,0},{12,4},{1,9},{5,13},{9,1},{13,5},{2,10},{6,14},... | collective-permute-start | bytes 196616 | tf_op jit(solution)/shard_map/ppermute | solution.py:41
  26.6 1.3 broadcast_in_dim.14
  28.0 5.3 %all-to-all-start.1 = ((bf16[4,32,128]{2,1,0:T(8,128)(2,1)}), bf16[4,32,128]{2,1,0:T(8,128)(2,1)S(1)}, u32[]{:S(2)}, u32[]{:S(2)}) async-start(bf16[4,32,128]{2,1,0:T(8,128)(2,1)} %broadcast_in_dim.14), calls=%async_computation.1 | async-start | bytes 65536 | tf_op jit(solution)/shard_map/all_to_all | solution.py:29
  33.3 0.0 collective-permute-done.1
  33.3 4.4 %all-to-all-done.1 = bf16[4,32,128]{2,1,0:T(8,128)(2,1)S(1)} async-done(((bf16[4,32,128]{2,1,0:T(8,128)(2,1)}), bf16[4,32,128]{2,1,0:T(8,128)(2,1)S(1)}, u32[]{:S(2)}, u32[]{:S(2)}) %all-to-all-start.1) | async-done | bytes 32800 | tf_op jit(solution)/shard_map/all_to_all | solution.py:29
  37.6 0.7 broadcast_in_dim.15
  38.3 4.9 %all-to-all-start.2 = ((bf16[4,4,32,128]{3,2,1,0:T(8,128)(2,1)}), bf16[4,4,32,128]{3,2,1,0:T(8,128)(2,1)S(1)}, u32[]{:S(2)}, u32[]{:S(2)}) async-start(bf16[4,4,32,128]{3,2,1,0:T(8,128)(2,1)} %broadcast_in_dim.15), calls=%async_computation.2 | async-start | bytes 262144 | tf_op jit(solution)/shard_map/all_to_all | solution.py:29
  43.2 4.5 %all-to-all-done.2 = bf16[4,4,32,128]{3,2,1,0:T(8,128)(2,1)S(1)} async-done(((bf16[4,4,32,128]{3,2,1,0:T(8,128)(2,1)}), bf16[4,4,32,128]{3,2,1,0:T(8,128)(2,1)S(1)}, u32[]{:S(2)}, u32[]{:S(2)}) %all-to-all-start.2) | async-done | bytes 131104 | tf_op jit(solution)/shard_map/all_to_all | solution.py:29
  47.7 0.0 copy-start.2
  47.8 3.9 %all_to_all.52 = bf16[2,4,4,32,128]{4,3,1,2,0:T(8,128)(2,1)S(1)} all-to-all(bf16[2,4,4,32,128]{4,3,1,2,0:T(8,128)(2,1)S(1)} %broadcast_in_dim.16), channel_id=1, replica_groups=mesh['zl'=4,'y'=4,'c'=2,'zh'=4,'x'=4] {'c'}, dimensions={0} | all-to-all | bytes 524288 | tf_op jit(solution)/shard_map/all_to_all | solution.py:29
  51.7 0.9 broadcast_in_dim.13
  52.6 4.3 %all-to-all-start = ((bf16[4,4,128,128]{3,2,1,0:T(8,128)(2,1)}), bf16[4,4,128,128]{3,2,1,0:T(8,128)(2,1)S(1)}, u32[]{:S(2)}, u32[]{:S(2)}) async-start(bf16[4,4,128,128]{3,2,1,0:T(8,128)(2,1)} %broadcast_in_dim.13), calls=%async_computation | async-start | bytes 1048576 | tf_op jit(solution)/shard_map/all_to_all | solution.py:85
  56.9 9.8 %all-to-all-done = bf16[4,4,128,128]{3,2,1,0:T(8,128)(2,1)S(1)} async-done(((bf16[4,4,128,128]{3,2,1,0:T(8,128)(2,1)}), bf16[4,4,128,128]{3,2,1,0:T(8,128)(2,1)S(1)}, u32[]{:S(2)}, u32[]{:S(2)}) %all-to-all-start) | async-done | bytes 524320 | tf_op jit(solution)/shard_map/all_to_all | solution.py:85
  66.8 0.0 copy-start.4
  66.8 0.0 copy-start.5
  66.8 4.8 %multiply_reduce_fusion.2 = (f32[2048]{0:T(1024)S(1)}, f32[2048,1024]{0,1:T(8,128)}) fusion(f32[1024]{0:T(1024)} %param.11, bf16[2048,128]{1,0:T(8,128)(2,1)S(1)} %bitcast.30, bf16[1024,128]{1,0:T(8,128)(2,1)S(1)} %bitcast.32), kind=kOutput, calls=%fused_computation.7 | convolution fusion | flops 543160320 | bytes 9187328 | tf_op jit(solution)/shard_map/dot_general | solution.py:13
  71.6 9.0 %psum.49 = f32[2048]{0:T(1024)S(1)} all-reduce(f32[2048]{0:T(1024)S(1)} %get-tuple-element.6), channel_id=1, replica_groups=mesh['zl'=4,'y'=4,'c'=2,'zh'=4,'x'=4] {'x'}, use_global_device_ids=true, to_apply=%region_1.2 | all-reduce | flops 2048 | bytes 16384 | tf_op jit(solution)/shard_map/psum | solution.py:21
  80.6 12.9 %psum.50 = f32[2048]{0:T(1024)S(1)} all-reduce(f32[2048]{0:T(1024)S(1)} %psum.49), channel_id=1, replica_groups=mesh['zl'=4,'y'=4,'c'=2,'zh'=4,'x'=4] {'zh'}, use_global_device_ids=true, to_apply=%region_2.3 | all-reduce | flops 2048 | bytes 16384 | tf_op jit(solution)/shard_map/psum | solution.py:21
  93.5 0.0 copy-done.2
  93.6 4.0 %multiply_reduce_fusion = f32[1024]{0:T(1024)S(1)} fusion(f32[2048,1024]{0,1:T(8,128)} %get-tuple-element.7, f32[2048]{0:T(1024)S(1)} %add_divide_fusion), kind=kLoop, calls=%fused_computation.2 | loop fusion | flops 4193280 | bytes 8400896 | tf_op jit(solution)/shard_map/reduce_sum | solution.py:100
  97.6 2.5 %psum.51 = f32[1024]{0:T(1024)S(1)} all-reduce(f32[1024]{0:T(1024)S(1)} %multiply_reduce_fusion), channel_id=1, replica_groups=mesh['zl'=4,'y'=4,'c'=2,'zh'=4,'x'=4] {'c'}, use_global_device_ids=true, to_apply=%region_4.5 | all-reduce | flops 1024 | bytes 8192 | tf_op jit(solution)/shard_map/psum | solution.py:21
  100.1 9.2 %psum.52 = f32[1024]{0:T(1024)S(1)} all-reduce(f32[1024]{0:T(1024)S(1)} %psum.51), channel_id=1, replica_groups=mesh['zl'=4,'y'=4,'c'=2,'zh'=4,'x'=4] {'y'}, use_global_device_ids=true, to_apply=%region_5.6 | all-reduce | flops 1024 | bytes 8192 | tf_op jit(solution)/shard_map/psum | solution.py:21
  109.2 9.5 %psum.53 = f32[1024]{0:T(1024)S(1)} all-reduce(f32[1024]{0:T(1024)S(1)} %psum.52), channel_id=1, replica_groups=mesh['zl'=4,'y'=4,'c'=2,'zh'=4,'x'=4] {'zl'}, use_global_device_ids=true, to_apply=%region_6.7 | all-reduce | flops 1024 | bytes 8192 | tf_op jit(solution)/shard_map/psum | solution.py:21
  118.7 0.0 copy-done.4
  118.7 0.0 copy-done.5
  118.7 0.0 copy-start
  118.8 5.1 %fusion.5 = f32[2048,128]{1,0:T(8,128)S(1)} fusion(bf16[1024,128]{1,0:T(8,128)(2,1)S(1)} %bitcast.33, f32[2048,1024]{0,1:T(8,128)} %get-tuple-element.7, f32[1024]{0:T(1024)S(1)} %rsqrt_multiply_fusion, f32[2048]{0:T(1024)S(1)} %add_divide_fusion), kind=kOutput, calls=%fused_computation.12 | convolution fusion | flops 541327360 | bytes 9711616 | tf_op jit(solution)/shard_map/dot_general | solution.py:106
  123.9 0.6 copy-done
  124.5 0.0 copy-start.3
  124.5 0.0 copy-start.1
  124.5 0.6 multiply_reduce_fusion.1
  125.1 8.7 %psum.54 = f32[2048]{0:T(1024)S(1)} all-reduce(f32[2048]{0:T(1024)S(1)} %multiply_reduce_fusion.1), channel_id=1, replica_groups=mesh['zl'=4,'y'=4,'c'=2,'zh'=4,'x'=4] {'x'}, use_global_device_ids=true, to_apply=%region_8.9 | all-reduce | flops 2048 | bytes 16384 | tf_op jit(solution)/shard_map/psum | solution.py:21
  133.9 14.2 %psum.55 = f32[2048]{0:T(1024)S(1)} all-reduce(f32[2048]{0:T(1024)S(1)} %psum.54), channel_id=1, replica_groups=mesh['zl'=4,'y'=4,'c'=2,'zh'=4,'x'=4] {'zh'}, use_global_device_ids=true, to_apply=%region_9.10 | all-reduce | flops 2048 | bytes 16384 | tf_op jit(solution)/shard_map/psum | solution.py:21
  148.1 0.0 copy-done.3
  148.1 0.0 copy-done.1
  148.1 4.5 %fusion = bf16[1024,2048]{1,0:T(8,128)(2,1)S(1)} fusion(f32[2048,1024]{0,1:T(8,128)} %get-tuple-element.7, f32[1024]{0:T(1024)S(1)} %rsqrt_multiply_fusion, f32[2048]{0:T(1024)S(1)} %add_divide_fusion, f32[1024]{0:T(1024)S(1)} %copy-done.1, f32[2048]{0:T(1024)S(1)} %negate_divide_fusion), kind=kLoop, calls=%fused_computation.1 | loop fusion | flops 12582912 | bytes 12607488 | tf_op jit(solution)/shard_map/convert_element_type | solution.py:124
  152.6 5.0 %fusion.8 = f32[2048,128]{1,0:T(8,128)S(1)} fusion(f32[2048,128]{1,0:T(8,128)S(1)} %fusion.5, bf16[1024,128]{1,0:T(8,128)(2,1)S(1)} %bitcast.34, f32[2048,1024]{0,1:T(8,128)} %get-tuple-element.7, f32[1024]{0:T(1024)S(1)} %copy-done.1, f32[2048]{0:T(1024)S(1)} %negate_divide_fusion), kind=kOutput, calls=%fused_computation.15 | convolution fusion | flops 541851648 | bytes 10760192 | tf_op jit(solution)/shard_map/dot_general | solution.py:93
  157.6 1.1 copy.23
  158.7 1.2 convolution_bitcast_fusion
  160.0 4.2 %all_to_all.53 = f32[1,4,4,2,32,128]{5,4,2,1,0,3:T(8,128)S(1)} all-to-all(f32[1,4,4,2,32,128]{5,4,2,1,0,3:T(8,128)S(1)} %copy.24), channel_id=1, replica_groups=mesh['zl'=4,'y'=4,'c'=2,'zh'=4,'x'=4] {'c'}, dimensions={3} | all-to-all | bytes 1048576 | tf_op jit(solution)/shard_map/all_to_all | solution.py:74
  164.1 3.5 %all-to-all-start.4 = ((f32[1,4,4,128,128]{4,3,1,0,2:T(8,128)}), f32[1,4,4,128,128]{4,3,1,0,2:T(8,128)S(1)}, u32[]{:S(2)}, u32[]{:S(2)}) async-start(f32[1,4,4,128,128]{4,3,1,0,2:T(8,128)} %copy.23), calls=%async_computation.4 | async-start | bytes 2097152 | tf_op jit(solution)/shard_map/all_to_all | solution.py:74
  167.7 0.7 copy.25
  168.4 14.8 %all-to-all-done.4 = f32[1,4,4,128,128]{4,3,1,0,2:T(8,128)S(1)} async-done(((f32[1,4,4,128,128]{4,3,1,0,2:T(8,128)}), f32[1,4,4,128,128]{4,3,1,0,2:T(8,128)S(1)}, u32[]{:S(2)}, u32[]{:S(2)}) %all-to-all-start.4) | async-done | bytes 1048608 | tf_op jit(solution)/shard_map/all_to_all | solution.py:74
  183.3 4.5 %all-to-all-start.6 = ((f32[1,4,4,32,128]{4,3,1,0,2:T(8,128)}), f32[1,4,4,32,128]{4,3,1,0,2:T(8,128)S(1)}, u32[]{:S(2)}, u32[]{:S(2)}) async-start(f32[1,4,4,32,128]{4,3,1,0,2:T(8,128)} %copy.25), calls=%async_computation.6 | async-start | bytes 524288 | tf_op jit(solution)/shard_map/all_to_all | solution.py:74
  187.8 0.1 reduce_sum.66
  187.9 7.3 %collective-permute-start.2 = (f32[2,128,128]{2,1,0:T(8,128)S(1)}, f32[2,128,128]{2,1,0:T(8,128)S(1)}, u32[]{:S(2)}, u32[]{:S(2)}) collective-permute-start(f32[2,128,128]{2,1,0:T(8,128)S(1)} %constant_dynamic-slice_fusion.1), channel_id=1, source_target_pairs={{0,8},{4,12},{8,0},{12,4},{1,9},{5,13},{9,1},{13,5},{2,10},{6,14},... | collective-permute-start | bytes 393224 | tf_op jit(solution)/shard_map/ppermute | solution.py:64
  195.2 0.0 all-to-all-done.6
  195.2 0.6 reduce_sum.68
  195.9 4.1 %all-to-all-start.7 = ((f32[4,32,128]{2,1,0:T(8,128)}), f32[4,32,128]{2,1,0:T(8,128)S(1)}, u32[]{:S(2)}, u32[]{:S(2)}) async-start(f32[4,32,128]{2,1,0:T(8,128)} %reduce_sum.68), calls=%async_computation.7 | async-start | bytes 131072 | tf_op jit(solution)/shard_map/all_to_all | solution.py:74
  200.0 12.3 %collective-permute-done.2 = f32[2,128,128]{2,1,0:T(8,128)S(1)} collective-permute-done((f32[2,128,128]{2,1,0:T(8,128)S(1)}, f32[2,128,128]{2,1,0:T(8,128)S(1)}, u32[]{:S(2)}, u32[]{:S(2)}) %collective-permute-start.2) | collective-permute-done | bytes 131104 | tf_op jit(solution)/shard_map/ppermute | solution.py:64
  212.3 1.9 collective-permute-start.3
  214.2 0.0 all-to-all-done.7
  214.2 0.6 reduce_sum.69
  214.8 7.5 %collective-permute-done.3 = f32[1,128,128]{2,1,0:T(8,128)S(1)} collective-permute-done((f32[1,128,128]{2,1,0:T(8,128)S(1)}, f32[1,128,128]{2,1,0:T(8,128)S(1)}, u32[]{:S(2)}, u32[]{:S(2)}) %collective-permute-start.3) | collective-permute-done | bytes 65568 | tf_op jit(solution)/shard_map/ppermute | solution.py:64
  222.3 0.6 add_bitcast_fusion
  (15 shorter events, 0.3 us)
Async XLA Ops:
  0.6 11.2 %collective-permute-start = (bf16[1,128,128]{2,1,0:T(8,128)(2,1)}, bf16[1,128,128]{2,1,0:T(8,128)(2,1)S(1)}, u32[]{:S(2)}, u32[]{:S(2)}) collective-permute-start(bf16[1,128,128]{2,1,0:T(8,128)(2,1)} %bitcast.38), channel_id=1, source_target_pairs={{0,4},{4,0},{8,12},{12,8},{1,5},{5,1},{9,13},{13,9},{2,6},{6,2},{1... | collective-permute-start | bytes 98312 | tf_op jit(solution)/shard_map/ppermute | solution.py:41
  12.6 20.7 %collective-permute-start.1 = (bf16[2,128,128]{2,1,0:T(8,128)(2,1)S(1)}, bf16[2,128,128]{2,1,0:T(8,128)(2,1)S(1)}, u32[]{:S(2)}, u32[]{:S(2)}) collective-permute-start(bf16[2,128,128]{2,1,0:T(8,128)(2,1)S(1)} %pad_maximum_fusion.1), channel_id=1, source_target_pairs={{0,8},{4,12},{8,0},{12,4},{1,9},{5,13},{9,1},{13,5},{2,10},{6,14},... | collective-permute-start | bytes 196616 | tf_op jit(solution)/shard_map/ppermute | solution.py:41
  28.0 9.7 %all-to-all-start.1 = ((bf16[4,32,128]{2,1,0:T(8,128)(2,1)}), bf16[4,32,128]{2,1,0:T(8,128)(2,1)S(1)}, u32[]{:S(2)}, u32[]{:S(2)}) async-start(bf16[4,32,128]{2,1,0:T(8,128)(2,1)} %broadcast_in_dim.14), calls=%async_computation.1 | async-start | bytes 65536 | tf_op jit(solution)/shard_map/all_to_all | solution.py:29
  38.3 9.4 %all-to-all-start.2 = ((bf16[4,4,32,128]{3,2,1,0:T(8,128)(2,1)}), bf16[4,4,32,128]{3,2,1,0:T(8,128)(2,1)S(1)}, u32[]{:S(2)}, u32[]{:S(2)}) async-start(bf16[4,4,32,128]{3,2,1,0:T(8,128)(2,1)} %broadcast_in_dim.15), calls=%async_computation.2 | async-start | bytes 262144 | tf_op jit(solution)/shard_map/all_to_all | solution.py:29
  47.7 45.8 %copy-start.2 = (s32[2048]{0:T(1024)S(1)}, s32[2048]{0:T(1024)}, u32[]{:S(2)}) copy-start(s32[2048]{0:T(1024)} %param.9) | copy-start | bytes 24580
  52.6 14.1 %all-to-all-start = ((bf16[4,4,128,128]{3,2,1,0:T(8,128)(2,1)}), bf16[4,4,128,128]{3,2,1,0:T(8,128)(2,1)S(1)}, u32[]{:S(2)}, u32[]{:S(2)}) async-start(bf16[4,4,128,128]{3,2,1,0:T(8,128)(2,1)} %broadcast_in_dim.13), calls=%async_computation | async-start | bytes 1048576 | tf_op jit(solution)/shard_map/all_to_all | solution.py:85
  66.8 52.0 %copy-start.4 = (s32[1024]{0:T(1024)S(1)}, s32[1024]{0:T(1024)}, u32[]{:S(2)}) copy-start(s32[1024]{0:T(1024)} %param.10) | copy-start | bytes 12292
  66.8 52.0 %copy-start.5 = (f32[1024]{0:T(1024)S(1)}, f32[1024]{0:T(1024)}, u32[]{:S(2)}) copy-start(f32[1024]{0:T(1024)} %param.13) | copy-start | bytes 12292
  118.7 5.8 %copy-start = (f32[2048,1024]{0,1:T(8,128)S(1)}, f32[2048,1024]{0,1:T(8,128)}, u32[]{:S(2)}) copy-start(f32[2048,1024]{0,1:T(8,128)} %get-tuple-element.7) | copy-start | bytes 25165828
  124.5 23.6 %copy-start.3 = (f32[2048]{0:T(1024)S(1)}, f32[2048]{0:T(1024)}, u32[]{:S(2)}) copy-start(f32[2048]{0:T(1024)} %param.12) | copy-start | bytes 24580
  124.5 23.6 %copy-start.1 = (f32[1024]{0:T(1024)S(1)}, f32[1024]{0:T(1024)}, u32[]{:S(2)}) copy-start(f32[1024]{0:T(1024)} %param.11) | copy-start | bytes 12292
  164.1 19.2 %all-to-all-start.4 = ((f32[1,4,4,128,128]{4,3,1,0,2:T(8,128)}), f32[1,4,4,128,128]{4,3,1,0,2:T(8,128)S(1)}, u32[]{:S(2)}, u32[]{:S(2)}) async-start(f32[1,4,4,128,128]{4,3,1,0,2:T(8,128)} %copy.23), calls=%async_computation.4 | async-start | bytes 2097152 | tf_op jit(solution)/shard_map/all_to_all | solution.py:74
  183.3 11.9 %all-to-all-start.6 = ((f32[1,4,4,32,128]{4,3,1,0,2:T(8,128)}), f32[1,4,4,32,128]{4,3,1,0,2:T(8,128)S(1)}, u32[]{:S(2)}, u32[]{:S(2)}) async-start(f32[1,4,4,32,128]{4,3,1,0,2:T(8,128)} %copy.25), calls=%async_computation.6 | async-start | bytes 524288 | tf_op jit(solution)/shard_map/all_to_all | solution.py:74
  187.9 24.3 %collective-permute-start.2 = (f32[2,128,128]{2,1,0:T(8,128)S(1)}, f32[2,128,128]{2,1,0:T(8,128)S(1)}, u32[]{:S(2)}, u32[]{:S(2)}) collective-permute-start(f32[2,128,128]{2,1,0:T(8,128)S(1)} %constant_dynamic-slice_fusion.1), channel_id=1, source_target_pairs={{0,8},{4,12},{8,0},{12,4},{1,9},{5,13},{9,1},{13,5},{2,10},{6,14},... | collective-permute-start | bytes 393224 | tf_op jit(solution)/shard_map/ppermute | solution.py:64
  195.9 18.3 %all-to-all-start.7 = ((f32[4,32,128]{2,1,0:T(8,128)}), f32[4,32,128]{2,1,0:T(8,128)S(1)}, u32[]{:S(2)}, u32[]{:S(2)}) async-start(f32[4,32,128]{2,1,0:T(8,128)} %reduce_sum.68), calls=%async_computation.7 | async-start | bytes 131072 | tf_op jit(solution)/shard_map/all_to_all | solution.py:74
  212.3 10.1 %collective-permute-start.3 = (f32[1,128,128]{2,1,0:T(8,128)S(1)}, f32[1,128,128]{2,1,0:T(8,128)S(1)}, u32[]{:S(2)}, u32[]{:S(2)}) collective-permute-start(f32[1,128,128]{2,1,0:T(8,128)S(1)} %constant_dynamic-slice_fusion), channel_id=1, source_target_pairs={{0,4},{4,0},{8,12},{12,8},{1,5},{5,1},{9,13},{13,9},{2,6},{6,2},{1... | collective-permute-start | bytes 196616 | tf_op jit(solution)/shard_map/ppermute | solution.py:64

commit v6 on v4

--- a/solution.py
+++ b/solution.py
@@ -78,6 +78,10 @@
         weighted_v = jnp.dot(
             weighted.astype(jnp.bfloat16), women_rows, preferred_element_type=jnp.float32
         )
+        blk = weighted_v.shape[0] // (women_sizes[0] * women_sizes[1])
+        wv_part = a2a_scatter(
+            weighted_v.reshape(women_sizes + (blk, weighted_v.shape[1])), women_sizes, WOMEN_AXES, ("x",)
+        )
         row_mass = nested_psum(jnp.sum(weighted, axis=1), ("x", "zh"))
         men_disc = jnp.sqrt(row_mass * row_mass + 4.0 * men_mass)
         men_root = 2.0 * men_mass / (row_mass + men_disc)
@@ -91,16 +95,18 @@
         direct_v = jnp.dot(
             weighted.astype(jnp.bfloat16), women_rows, preferred_element_type=jnp.float32
         )
+        dv_part = a2a_scatter(
+            direct_v.reshape(women_sizes + (blk, direct_v.shape[1])), women_sizes, WOMEN_AXES, ("x",)
+        )
         row_cot = nested_psum(jnp.sum(weighted, axis=1), ("x", "zh"))
         row_grad = -(men_cotangent + men_root * row_cot) / men_disc
-        men_term = 0.5 * (row_grad[:, None] * weighted_v + men_root[:, None] * direct_v)
-        blk = men_term.shape[0] // (women_sizes[0] * women_sizes[1])
-        part = a2a_scatter(
-            men_term.reshape(women_sizes + (blk, men_term.shape[1])), women_sizes, WOMEN_AXES, ("x",)
-        )
-        men_grad = halving_scatter(
-            part.reshape(-1, part.shape[-1]), ("zh",), (women_sizes[0],), ("zh",)
-        )
+        both = jnp.stack([wv_part, dv_part], axis=1)
+        both = halving_scatter(both.reshape(-1, both.shape[-1]), ("zh",), (women_sizes[0],), ("zh",))
+        both = both.reshape(2, blk, both.shape[-1])
+        start = (lax.axis_index("zh") * women_sizes[1] + lax.axis_index("x")) * blk
+        grad_blk = lax.dynamic_slice_in_dim(row_grad, start, blk)
+        root_blk = lax.dynamic_slice_in_dim(men_root, start, blk)
+        men_grad = 0.5 * (grad_blk[:, None] * both[0] + root_blk[:, None] * both[1])
 
         tangent = (
             0.5

time: 224 us -> 226 us (level)
  the two profiles are of different devices: /device:TPU:8 before, /device:TPU:2 now
where the time goes in v6:
time: 226 us; the launch traced here: 225 us
  blocking collectives  124 us (55%)
  starting transfers between devices  33.8 us (15%)
  waiting for transfers between devices  27.1 us (12%)
  other arithmetic  16 us (7%)
  local copies, waits for them, and re-layouts  12.2 us (5%)
  matrix products  10.9 us (5%)
    psum x7, blocking collectives, nested_psum(): x = lax.psum(x, a)  66.7 us
    all_to_all x4, blocking collectives, ordered_gather(): lax.all_to_all(jnp.broadcast_to(x[None], (n,) + x.shape), a, 0, 0, tiled=...  52.8 us
    all_to_all x4, starting transfers between devices, a2a_scatter(): x = jnp.sum(lax.all_to_all(x, a, d, 0, tiled=False), axis=0)  17.2 us
    ppermute x2, waiting for transfers between devices, halving_scatter(): got = lax.ppermute(send, a, [(i, i ^ k) for i in range(n)])  12.4 us
    ppermute x2, starting transfers between devices, halving_scatter(): got = lax.ppermute(send, a, [(i, i ^ k) for i in range(n)])  11.8 us
    all_to_all x4, waiting for transfers between devices, a2a_scatter(): x = jnp.sum(lax.all_to_all(x, a, d, 0, tiled=False), axis=0)  8.16 us
    all_to_all x1, waiting for transfers between devices, ordered_gather(): lax.all_to_all(jnp.broadcast_to(x[None], (n,) + x.shape), a, 0, 0, tiled=...  6.6 us
    convert_element_type x1, local copies, waits for them, and re-layouts, body(): tangent = (0.5 * kernel * (row_grad[:, None] * women_root[None, :] + men_...  6.49 us
  transfers between devices with their start and end apart: 7, of which 4 were waited for; matrix products, arithmetic and copies ran while one was open for 11% of the time, Pallas kernels for 0%

profile of v6, /device:TPU:2, one launch (start us, length us, event | category | flops | bytes accessed | tf_op | source)
XLA Modules:
  0.0 224.7 jit_solution(7718303587767725224)
XLA Ops:
  0.6 0.7 broadcast_in_dim.14
  1.3 11.3 %all_to_all.66 = bf16[4,32,128]{2,1,0:T(8,128)(2,1)S(1)} all-to-all(bf16[4,32,128]{2,1,0:T(8,128)(2,1)S(1)} %broadcast_in_dim.14), channel_id=1, replica_groups=mesh['zl'=4,'y'=4,'c'=2,'zh'=4,'x'=4] {'zl'}, dimensions={0} | all-to-all | bytes 65536 | tf_op jit(solution)/shard_map/all_to_all | solution.py:29
  12.7 10.2 %all_to_all.67 = bf16[4,4,32,128]{3,2,1,0:T(8,128)(2,1)S(1)} all-to-all(bf16[4,4,32,128]{3,2,1,0:T(8,128)(2,1)S(1)} %broadcast_in_dim.15), channel_id=1, replica_groups=mesh['zl'=4,'y'=4,'c'=2,'zh'=4,'x'=4] {'y'}, dimensions={0} | all-to-all | bytes 262144 | tf_op jit(solution)/shard_map/all_to_all | solution.py:29
  23.0 3.9 %all_to_all.68 = bf16[2,4,4,32,128]{4,3,1,2,0:T(8,128)(2,1)S(1)} all-to-all(bf16[2,4,4,32,128]{4,3,1,2,0:T(8,128)(2,1)S(1)} %broadcast_in_dim.16), channel_id=1, replica_groups=mesh['zl'=4,'y'=4,'c'=2,'zh'=4,'x'=4] {'c'}, dimensions={0} | all-to-all | bytes 524288 | tf_op jit(solution)/shard_map/all_to_all | solution.py:29
  26.9 0.8 broadcast_in_dim.12
  27.7 27.3 %all_to_all.69 = bf16[4,128,128]{2,1,0:T(8,128)(2,1)S(1)} all-to-all(bf16[4,128,128]{2,1,0:T(8,128)(2,1)S(1)} %broadcast_in_dim.12), channel_id=1, replica_groups=mesh['zl'=4,'y'=4,'c'=2,'zh'=4,'x'=4] {'zh'}, dimensions={0} | all-to-all | bytes 262144 | tf_op jit(solution)/shard_map/all_to_all | solution.py:29
  55.0 0.9 broadcast_in_dim.13
  55.9 4.8 %all-to-all-start.1 = ((bf16[4,4,128,128]{3,2,1,0:T(8,128)(2,1)}), bf16[4,4,128,128]{3,2,1,0:T(8,128)(2,1)S(1)}, u32[]{:S(2)}, u32[]{:S(2)}) async-start(bf16[4,4,128,128]{3,2,1,0:T(8,128)(2,1)} %broadcast_in_dim.13), calls=%async_computation.1 | async-start | bytes 1048576 | tf_op jit(solution)/shard_map/all_to_all | solution.py:29
  60.7 6.6 %all-to-all-done.1 = bf16[4,4,128,128]{3,2,1,0:T(8,128)(2,1)S(1)} async-done(((bf16[4,4,128,128]{3,2,1,0:T(8,128)(2,1)}), bf16[4,4,128,128]{3,2,1,0:T(8,128)(2,1)S(1)}, u32[]{:S(2)}, u32[]{:S(2)}) %all-to-all-start.1) | async-done | bytes 524320 | tf_op jit(solution)/shard_map/all_to_all | solution.py:29
  67.4 0.0 copy-start
  67.4 4.9 %multiply_convert_fusion.1 = (bf16[2048,1024]{1,0:T(8,128)(2,1)S(1)}, f32[2048]{0:T(1024)S(1)}, f32[2048,1024]{1,0:T(8,128)}) fusion(f32[1024]{0:T(1024)} %param.11, bf16[2048,128]{1,0:T(8,128)(2,1)S(1)} %bitcast.54, bf16[1024,128]{1,0:T(8,128)(2,1)S(1)} %bitcast.56), kind=kOutput, calls=%fused_computation.6 | convolution fusion | flops 545257472 | bytes 13381632 | tf_op jit(solution)/shard_map/dot_general | solution.py:13
  72.3 0.0 copy-start.3
  72.3 0.0 copy-start.4
  72.3 1.3 convolution_bitcast_fusion.1
  73.6 1.2 copy.29
  74.8 9.3 %psum.49 = f32[2048]{0:T(1024)S(1)} all-reduce(f32[2048]{0:T(1024)S(1)} %get-tuple-element.5), channel_id=1, replica_groups=mesh['zl'=4,'y'=4,'c'=2,'zh'=4,'x'=4] {'x'}, use_global_device_ids=true, to_apply=%region_1.0 | all-reduce | flops 2048 | bytes 16384 | tf_op jit(solution)/shard_map/psum | solution.py:21
  84.0 13.0 %psum.50 = f32[2048]{0:T(1024)S(1)} all-reduce(f32[2048]{0:T(1024)S(1)} %psum.49), channel_id=1, replica_groups=mesh['zl'=4,'y'=4,'c'=2,'zh'=4,'x'=4] {'zh'}, use_global_device_ids=true, to_apply=%region_2.0 | all-reduce | flops 2048 | bytes 16384 | tf_op jit(solution)/shard_map/psum | solution.py:21
  97.1 0.0 copy-done
  97.1 4.0 %multiply_reduce_fusion = f32[1024]{0:T(1024)S(1)} fusion(f32[2048,1024]{1,0:T(8,128)} %get-tuple-element.6, f32[2048]{0:T(1024)S(1)} %add_divide_fusion), kind=kLoop, calls=%fused_computation.2 | loop fusion | flops 4193280 | bytes 8400896 | tf_op jit(solution)/shard_map/reduce_sum | solution.py:89
  101.1 2.5 %psum.51 = f32[1024]{0:T(1024)S(1)} all-reduce(f32[1024]{0:T(1024)S(1)} %multiply_reduce_fusion), channel_id=1, replica_groups=mesh['zl'=4,'y'=4,'c'=2,'zh'=4,'x'=4] {'c'}, use_global_device_ids=true, to_apply=%region_4.0 | all-reduce | flops 1024 | bytes 8192 | tf_op jit(solution)/shard_map/psum | solution.py:21
  103.6 8.9 %psum.52 = f32[1024]{0:T(1024)S(1)} all-reduce(f32[1024]{0:T(1024)S(1)} %psum.51), channel_id=1, replica_groups=mesh['zl'=4,'y'=4,'c'=2,'zh'=4,'x'=4] {'y'}, use_global_device_ids=true, to_apply=%region_5.0 | all-reduce | flops 1024 | bytes 8192 | tf_op jit(solution)/shard_map/psum | solution.py:21
  112.4 10.5 %psum.53 = f32[1024]{0:T(1024)S(1)} all-reduce(f32[1024]{0:T(1024)S(1)} %psum.52), channel_id=1, replica_groups=mesh['zl'=4,'y'=4,'c'=2,'zh'=4,'x'=4] {'zl'}, use_global_device_ids=true, to_apply=%region_6.0 | all-reduce | flops 1024 | bytes 8192 | tf_op jit(solution)/shard_map/psum | solution.py:21
  122.9 4.7 %all-to-all-start.5 = ((f32[1,4,4,128,128]{4,3,1,0,2:T(8,128)}), f32[1,4,4,128,128]{4,3,1,0,2:T(8,128)S(1)}, u32[]{:S(2)}, u32[]{:S(2)}) async-start(f32[1,4,4,128,128]{4,3,1,0,2:T(8,128)} %copy.29), calls=%async_computation.5 | async-start | bytes 2097152 | tf_op jit(solution)/shard_map/all_to_all | solution.py:62
  127.6 0.0 copy-done.3
  127.6 0.0 copy-done.4
  127.6 0.0 copy-start.2
  127.6 0.0 copy-start.1
  127.6 4.2 %multiply_reduce_fusion.1 = (f32[2048]{0:T(1024)S(1)}, bf16[2048,1024]{1,0:T(8,128)(2,1)S(1)}) fusion(f32[2048,1024]{1,0:T(8,128)} %get-tuple-element.6, f32[1024]{0:T(1024)S(1)} %rsqrt_multiply_fusion), kind=kLoop, calls=%fused_computation.5 | loop fusion | flops 6289408 | bytes 12595200 | tf_op jit(solution)/shard_map/reduce_sum | solution.py:101
  131.8 1.3 convolution_bitcast_fusion
  133.1 1.1 copy.30
  134.2 8.7 %psum.54 = f32[2048]{0:T(1024)S(1)} all-reduce(f32[2048]{0:T(1024)S(1)} %get-tuple-element.2), channel_id=1, replica_groups=mesh['zl'=4,'y'=4,'c'=2,'zh'=4,'x'=4] {'x'}, use_global_device_ids=true, to_apply=%region_8.0 | all-reduce | flops 2048 | bytes 16384 | tf_op jit(solution)/shard_map/psum | solution.py:21
  142.9 13.9 %psum.55 = f32[2048]{0:T(1024)S(1)} all-reduce(f32[2048]{0:T(1024)S(1)} %psum.54), channel_id=1, replica_groups=mesh['zl'=4,'y'=4,'c'=2,'zh'=4,'x'=4] {'zh'}, use_global_device_ids=true, to_apply=%region_9.0 | all-reduce | flops 2048 | bytes 16384 | tf_op jit(solution)/shard_map/psum | solution.py:21
  156.8 0.0 copy-done.2
  156.8 0.0 all-to-all-done.5
  156.8 5.9 %all-to-all-start.6 = ((f32[1,4,4,128,128]{4,3,1,0,2:T(8,128)}), f32[1,4,4,128,128]{4,3,1,0,2:T(8,128)S(1)}, u32[]{:S(2)}, u32[]{:S(2)}) async-start(f32[1,4,4,128,128]{4,3,1,0,2:T(8,128)} %copy.30), calls=%async_computation.6 | async-start | bytes 2097152 | tf_op jit(solution)/shard_map/all_to_all | solution.py:62
  162.7 0.0 copy-done.1
  162.7 5.6 %fusion = bf16[1024,2048]{0,1:T(8,128)(2,1)} fusion(f32[2048,1024]{1,0:T(8,128)} %get-tuple-element.6, f32[1024]{0:T(1024)S(1)} %rsqrt_multiply_fusion, f32[2048]{0:T(1024)S(1)} %add_divide_fusion, f32[1024]{0:T(1024)S(1)} %copy-done.1, f32[2048]{0:T(1024)S(1)} %negate_divide_fusion), kind=kLoop, calls=%fused_computation.1 | loop fusion | flops 12582912 | bytes 12607488 | tf_op jit(solution)/shard_map/convert_element_type | solution.py:115
  168.3 6.5 %copy.31 = bf16[1024,2048]{1,0:T(8,128)(2,1)} copy(bf16[1024,2048]{0,1:T(8,128)(2,1)} %fusion) | data formatting | bytes 8388608 | tf_op jit(solution)/shard_map/convert_element_type | solution.py:115
  174.8 0.1 reduce_sum.75
  174.9 0.0 all-to-all-done.6
  174.9 0.1 reduce_sum.76
  175.0 7.3 %collective-permute-start = (f32[2,256,128]{2,1,0:T(8,128)S(1)}, f32[2,256,128]{2,1,0:T(8,128)S(1)}, u32[]{:S(2)}, u32[]{:S(2)}) collective-permute-start(f32[2,256,128]{2,1,0:T(8,128)S(1)} %constant_dynamic-slice_fusion.1), channel_id=1, source_target_pairs={{0,8},{4,12},{8,0},{12,4},{1,9},{5,13},{9,1},{13,5},{2,10},{6,14},... | collective-permute-start | bytes 786440 | tf_op jit(solution)/shard_map/ppermute | solution.py:52
  182.3 3.4 %convolution_bitcast_fusion.2 = f32[1,4,4,2,32,128]{5,4,3,2,1,0:T(8,128)S(1)} fusion(bf16[4,4,2,32,2048]{4,3,2,1,0:T(8,128)(2,1)} %bitcast.52, bf16[2048,128,1,1,1]{1,0,4,3,2:T(8,128)(2,1)S(1)} %bitcast.55), kind=kOutput, calls=%fused_computation.10 | convolution fusion | flops 536870912 | bytes 5242880 | tf_op jit(solution)/shard_map/dot_general | solution.py:116
  185.8 4.2 %all_to_all.70 = f32[1,4,4,2,32,128]{5,4,2,1,0,3:T(8,128)S(1)} all-to-all(f32[1,4,4,2,32,128]{5,4,2,1,0,3:T(8,128)S(1)} %copy.32), channel_id=1, replica_groups=mesh['zl'=4,'y'=4,'c'=2,'zh'=4,'x'=4] {'c'}, dimensions={3} | all-to-all | bytes 1048576 | tf_op jit(solution)/shard_map/all_to_all | solution.py:62
  190.0 0.7 copy.33
  190.7 3.4 %all-to-all-start.8 = ((f32[1,4,4,32,128]{4,3,1,0,2:T(8,128)}), f32[1,4,4,32,128]{4,3,1,0,2:T(8,128)S(1)}, u32[]{:S(2)}, u32[]{:S(2)}) async-start(f32[1,4,4,32,128]{4,3,1,0,2:T(8,128)} %copy.33), calls=%async_computation.8 | async-start | bytes 524288 | tf_op jit(solution)/shard_map/all_to_all | solution.py:62
  194.2 7.2 %all-to-all-done.8 = f32[1,4,4,32,128]{4,3,1,0,2:T(8,128)S(1)} async-done(((f32[1,4,4,32,128]{4,3,1,0,2:T(8,128)}), f32[1,4,4,32,128]{4,3,1,0,2:T(8,128)S(1)}, u32[]{:S(2)}, u32[]{:S(2)}) %all-to-all-start.8) | async-done | bytes 262176 | tf_op jit(solution)/shard_map/all_to_all | solution.py:62
  201.3 0.6 reduce_sum.78
  202.0 3.3 %all-to-all-start.9 = ((f32[4,32,128]{2,1,0:T(8,128)}), f32[4,32,128]{2,1,0:T(8,128)S(1)}, u32[]{:S(2)}, u32[]{:S(2)}) async-start(f32[4,32,128]{2,1,0:T(8,128)} %reduce_sum.78), calls=%async_computation.9 | async-start | bytes 131072 | tf_op jit(solution)/shard_map/all_to_all | solution.py:62
  205.3 0.0 collective-permute-done
  205.4 4.5 %collective-permute-start.1 = (f32[1,256,128]{2,1,0:T(8,128)S(1)}, f32[1,256,128]{2,1,0:T(8,128)S(1)}, u32[]{:S(2)}, u32[]{:S(2)}) collective-permute-start(f32[1,256,128]{2,1,0:T(8,128)S(1)} %constant_dynamic-slice_fusion), channel_id=1, source_target_pairs={{0,4},{4,0},{8,12},{12,8},{1,5},{5,1},{9,13},{13,9},{2,6},{6,2},{1... | collective-permute-start | bytes 393224 | tf_op jit(solution)/shard_map/ppermute | solution.py:52
  209.9 0.1 dynamic_slice.23
  210.0 0.1 dynamic_slice.18
  210.0 1.0 all-to-all-done.9
  211.0 0.6 reduce_sum.79
  211.6 12.4 %collective-permute-done.1 = f32[1,256,128]{2,1,0:T(8,128)S(1)} collective-permute-done((f32[1,256,128]{2,1,0:T(8,128)S(1)}, f32[1,256,128]{2,1,0:T(8,128)S(1)}, u32[]{:S(2)}, u32[]{:S(2)}) %collective-permute-start.1) | collective-permute-done | bytes 131104 | tf_op jit(solution)/shard_map/ppermute | solution.py:52
  224.0 0.7 fusion.3
  (15 shorter events, 0.4 us)
Async XLA Ops:
  55.9 11.4 %all-to-all-start.1 = ((bf16[4,4,128,128]{3,2,1,0:T(8,128)(2,1)}), bf16[4,4,128,128]{3,2,1,0:T(8,128)(2,1)S(1)}, u32[]{:S(2)}, u32[]{:S(2)}) async-start(bf16[4,4,128,128]{3,2,1,0:T(8,128)(2,1)} %broadcast_in_dim.13), calls=%async_computation.1 | async-start | bytes 1048576 | tf_op jit(solution)/shard_map/all_to_all | solution.py:29
  67.4 29.7 %copy-start = (s32[2048]{0:T(1024)S(1)}, s32[2048]{0:T(1024)}, u32[]{:S(2)}) copy-start(s32[2048]{0:T(1024)} %param.9) | copy-start | bytes 24580
  72.3 55.3 %copy-start.3 = (s32[1024]{0:T(1024)S(1)}, s32[1024]{0:T(1024)}, u32[]{:S(2)}) copy-start(s32[1024]{0:T(1024)} %param.10) | copy-start | bytes 12292
  72.3 55.3 %copy-start.4 = (f32[1024]{0:T(1024)S(1)}, f32[1024]{0:T(1024)}, u32[]{:S(2)}) copy-start(f32[1024]{0:T(1024)} %param.13) | copy-start | bytes 12292
  122.9 33.9 %all-to-all-start.5 = ((f32[1,4,4,128,128]{4,3,1,0,2:T(8,128)}), f32[1,4,4,128,128]{4,3,1,0,2:T(8,128)S(1)}, u32[]{:S(2)}, u32[]{:S(2)}) async-start(f32[1,4,4,128,128]{4,3,1,0,2:T(8,128)} %copy.29), calls=%async_computation.5 | async-start | bytes 2097152 | tf_op jit(solution)/shard_map/all_to_all | solution.py:62
  127.6 29.2 %copy-start.2 = (f32[2048]{0:T(1024)S(1)}, f32[2048]{0:T(1024)}, u32[]{:S(2)}) copy-start(f32[2048]{0:T(1024)} %param.12) | copy-start | bytes 24580
  127.6 35.1 %copy-start.1 = (f32[1024]{0:T(1024)S(1)}, f32[1024]{0:T(1024)}, u32[]{:S(2)}) copy-start(f32[1024]{0:T(1024)} %param.11) | copy-start | bytes 12292
  156.8 18.0 %all-to-all-start.6 = ((f32[1,4,4,128,128]{4,3,1,0,2:T(8,128)}), f32[1,4,4,128,128]{4,3,1,0,2:T(8,128)S(1)}, u32[]{:S(2)}, u32[]{:S(2)}) async-start(f32[1,4,4,128,128]{4,3,1,0,2:T(8,128)} %copy.30), calls=%async_computation.6 | async-start | bytes 2097152 | tf_op jit(solution)/shard_map/all_to_all | solution.py:62
  175.0 30.3 %collective-permute-start = (f32[2,256,128]{2,1,0:T(8,128)S(1)}, f32[2,256,128]{2,1,0:T(8,128)S(1)}, u32[]{:S(2)}, u32[]{:S(2)}) collective-permute-start(f32[2,256,128]{2,1,0:T(8,128)S(1)} %constant_dynamic-slice_fusion.1), channel_id=1, source_target_pairs={{0,8},{4,12},{8,0},{12,4},{1,9},{5,13},{9,1},{13,5},{2,10},{6,14},... | collective-permute-start | bytes 786440 | tf_op jit(solution)/shard_map/ppermute | solution.py:52
  190.7 10.6 %all-to-all-start.8 = ((f32[1,4,4,32,128]{4,3,1,0,2:T(8,128)}), f32[1,4,4,32,128]{4,3,1,0,2:T(8,128)S(1)}, u32[]{:S(2)}, u32[]{:S(2)}) async-start(f32[1,4,4,32,128]{4,3,1,0,2:T(8,128)} %copy.33), calls=%async_computation.8 | async-start | bytes 524288 | tf_op jit(solution)/shard_map/all_to_all | solution.py:62
  202.0 9.0 %all-to-all-start.9 = ((f32[4,32,128]{2,1,0:T(8,128)}), f32[4,32,128]{2,1,0:T(8,128)S(1)}, u32[]{:S(2)}, u32[]{:S(2)}) async-start(f32[4,32,128]{2,1,0:T(8,128)} %reduce_sum.78), calls=%async_computation.9 | async-start | bytes 131072 | tf_op jit(solution)/shard_map/all_to_all | solution.py:62
  205.4 18.6 %collective-permute-start.1 = (f32[1,256,128]{2,1,0:T(8,128)S(1)}, f32[1,256,128]{2,1,0:T(8,128)S(1)}, u32[]{:S(2)}, u32[]{:S(2)}) collective-permute-start(f32[1,256,128]{2,1,0:T(8,128)S(1)} %constant_dynamic-slice_fusion), channel_id=1, source_target_pairs={{0,4},{4,0},{8,12},{12,8},{1,5},{5,1},{9,13},{13,9},{2,6},{6,2},{1... | collective-permute-start | bytes 393224 | tf_op jit(solution)/shard_map/ppermute | solution.py:52

commit v7 on v4

--- a/solution.py
+++ b/solution.py
@@ -95,11 +95,11 @@
         row_grad = -(men_cotangent + men_root * row_cot) / men_disc
         men_term = 0.5 * (row_grad[:, None] * weighted_v + men_root[:, None] * direct_v)
         blk = men_term.shape[0] // (women_sizes[0] * women_sizes[1])
-        part = a2a_scatter(
-            men_term.reshape(women_sizes + (blk, men_term.shape[1])), women_sizes, WOMEN_AXES, ("x",)
-        )
-        men_grad = halving_scatter(
-            part.reshape(-1, part.shape[-1]), ("zh",), (women_sizes[0],), ("zh",)
+        men_grad = a2a_scatter(
+            men_term.reshape(women_sizes + (blk, men_term.shape[1])),
+            women_sizes,
+            WOMEN_AXES,
+            ("x", "zh"),
         )
 
         tangent = (

time: 224 us -> 225 us (level)
  waiting for transfers between devices: 37 us -> 45.2 us
  starting transfers between devices: 29.7 us -> 22.3 us
    all_to_all x3 -> x4, waiting for transfers between devices: 14.8 us -> 37.1 us  [a2a_scatter(): x = jnp.sum(lax.all_to_all(x, a, d, 0, tiled=False), axis=0)]
    ppermute x2 -> x0, waiting for transfers between devices: 14.2 us -> none  [halving_scatter(): got = lax.ppermute(send, a, [(i, i ^ k) for i in range(n)])]
    ppermute x2 -> x0, starting transfers between devices: 14 us -> none  [halving_scatter(): got = lax.ppermute(send, a, [(i, i ^ k) for i in range(n)])]
    all_to_all x3 -> x4, starting transfers between devices: 11.3 us -> 18 us  [a2a_scatter(): x = jnp.sum(lax.all_to_all(x, a, d, 0, tiled=False), axis=0)]
  transfers between devices with their start and end apart: 6 -> 5, of which waited for: 4 -> 4; matrix products, arithmetic and copies ran while one was open for 1% -> 4% of each run, Pallas kernels for 0% -> 0%
where the time goes in v7:
time: 225 us; the launch traced here: 224 us
  blocking collectives  123 us (55%)
  waiting for transfers between devices  45.2 us (20%)
  starting transfers between devices  22.3 us (10%)
  matrix products  16.2 us (7%)
  other arithmetic  11.8 us (5%)
  local copies, waits for them, and re-layouts  4.97 us (2%)
    psum x7, blocking collectives, nested_psum(): x = lax.psum(x, a)  66.7 us
    all_to_all x4, blocking collectives, ordered_gather(): lax.all_to_all(jnp.broadcast_to(x[None], (n,) + x.shape), a, 0, 0, tiled=...  51.8 us
    all_to_all x4, waiting for transfers between devices, a2a_scatter(): x = jnp.sum(lax.all_to_all(x, a, d, 0, tiled=False), axis=0)  37.1 us
    all_to_all x4, starting transfers between devices, a2a_scatter(): x = jnp.sum(lax.all_to_all(x, a, d, 0, tiled=False), axis=0)  18 us
    dot_general x2, matrix products, body(): jnp.dot(weighted.astype(jnp.bfloat16), women_rows, preferred_element_type...  10.1 us
    all_to_all x1, waiting for transfers between devices, ordered_gather(): lax.all_to_all(jnp.broadcast_to(x[None], (n,) + x.shape), a, 0, 0, tiled=...  8.06 us
    dot_general x1, matrix products, kernel_tile(): lax.dot_general(men_rows, women_block, (((1,), (1,)), ((), ())), preferre...  4.82 us
  transfers between devices with their start and end apart: 5, of which 4 were waited for; matrix products, arithmetic and copies ran while one was open for 4% of the time, Pallas kernels for 0%

profile of v7, /device:TPU:8, one launch (start us, length us, event | category | flops | bytes accessed | tf_op | source)
XLA Modules:
  0.0 223.9 jit_solution(14506467631193536341)
XLA Ops:
  0.6 0.7 broadcast_in_dim.14
  1.3 11.3 %all_to_all.62 = bf16[4,32,128]{2,1,0:T(8,128)(2,1)S(1)} all-to-all(bf16[4,32,128]{2,1,0:T(8,128)(2,1)S(1)} %broadcast_in_dim.14), channel_id=1, replica_groups=mesh['zl'=4,'y'=4,'c'=2,'zh'=4,'x'=4] {'zl'}, dimensions={0} | all-to-all | bytes 65536 | tf_op jit(solution)/shard_map/all_to_all | solution.py:29
  12.7 9.4 %all_to_all.63 = bf16[4,4,32,128]{3,2,1,0:T(8,128)(2,1)S(1)} all-to-all(bf16[4,4,32,128]{3,2,1,0:T(8,128)(2,1)S(1)} %broadcast_in_dim.15), channel_id=1, replica_groups=mesh['zl'=4,'y'=4,'c'=2,'zh'=4,'x'=4] {'y'}, dimensions={0} | all-to-all | bytes 262144 | tf_op jit(solution)/shard_map/all_to_all | solution.py:29
  22.1 0.0 copy-start.2
  22.1 3.9 %all_to_all.64 = bf16[2,4,4,32,128]{4,3,1,2,0:T(8,128)(2,1)S(1)} all-to-all(bf16[2,4,4,32,128]{4,3,1,2,0:T(8,128)(2,1)S(1)} %broadcast_in_dim.16), channel_id=1, replica_groups=mesh['zl'=4,'y'=4,'c'=2,'zh'=4,'x'=4] {'c'}, dimensions={0} | all-to-all | bytes 524288 | tf_op jit(solution)/shard_map/all_to_all | solution.py:29
  26.1 0.8 broadcast_in_dim.12
  26.8 27.1 %all_to_all.65 = bf16[4,128,128]{2,1,0:T(8,128)(2,1)S(1)} all-to-all(bf16[4,128,128]{2,1,0:T(8,128)(2,1)S(1)} %broadcast_in_dim.12), channel_id=1, replica_groups=mesh['zl'=4,'y'=4,'c'=2,'zh'=4,'x'=4] {'zh'}, dimensions={0} | all-to-all | bytes 262144 | tf_op jit(solution)/shard_map/all_to_all | solution.py:29
  54.0 0.9 broadcast_in_dim.13
  54.9 4.3 %all-to-all-start.1 = ((bf16[4,4,128,128]{3,2,1,0:T(8,128)(2,1)}), bf16[4,4,128,128]{3,2,1,0:T(8,128)(2,1)S(1)}, u32[]{:S(2)}, u32[]{:S(2)}) async-start(bf16[4,4,128,128]{3,2,1,0:T(8,128)(2,1)} %broadcast_in_dim.13), calls=%async_computation.1 | async-start | bytes 1048576 | tf_op jit(solution)/shard_map/all_to_all | solution.py:29
  59.2 8.1 %all-to-all-done.1 = bf16[4,4,128,128]{3,2,1,0:T(8,128)(2,1)S(1)} async-done(((bf16[4,4,128,128]{3,2,1,0:T(8,128)(2,1)}), bf16[4,4,128,128]{3,2,1,0:T(8,128)(2,1)S(1)}, u32[]{:S(2)}, u32[]{:S(2)}) %all-to-all-start.1) | async-done | bytes 524320 | tf_op jit(solution)/shard_map/all_to_all | solution.py:29
  67.3 0.0 copy-start.4
  67.3 0.0 copy-start.5
  67.3 4.8 %multiply_reduce_fusion.2 = (f32[2048]{0:T(1024)S(1)}, f32[2048,1024]{0,1:T(8,128)}) fusion(f32[1024]{0:T(1024)} %param.11, bf16[2048,128]{1,0:T(8,128)(2,1)S(1)} %bitcast.25, bf16[1024,128]{1,0:T(8,128)(2,1)S(1)} %bitcast.27), kind=kOutput, calls=%fused_computation.7 | convolution fusion | flops 543160320 | bytes 9187328 | tf_op jit(solution)/shard_map/dot_general | solution.py:13
  72.1 9.0 %psum.49 = f32[2048]{0:T(1024)S(1)} all-reduce(f32[2048]{0:T(1024)S(1)} %get-tuple-element.2), channel_id=1, replica_groups=mesh['zl'=4,'y'=4,'c'=2,'zh'=4,'x'=4] {'x'}, use_global_device_ids=true, to_apply=%region_1.0 | all-reduce | flops 2048 | bytes 16384 | tf_op jit(solution)/shard_map/psum | solution.py:21
  81.1 13.1 %psum.50 = f32[2048]{0:T(1024)S(1)} all-reduce(f32[2048]{0:T(1024)S(1)} %psum.49), channel_id=1, replica_groups=mesh['zl'=4,'y'=4,'c'=2,'zh'=4,'x'=4] {'zh'}, use_global_device_ids=true, to_apply=%region_2.0 | all-reduce | flops 2048 | bytes 16384 | tf_op jit(solution)/shard_map/psum | solution.py:21
  94.2 0.0 copy-done.2
  94.2 4.0 %multiply_reduce_fusion = f32[1024]{0:T(1024)S(1)} fusion(f32[2048,1024]{0,1:T(8,128)} %get-tuple-element.3, f32[2048]{0:T(1024)S(1)} %add_divide_fusion), kind=kLoop, calls=%fused_computation.2 | loop fusion | flops 4193280 | bytes 8400896 | tf_op jit(solution)/shard_map/reduce_sum | solution.py:85
  98.2 2.5 %psum.51 = f32[1024]{0:T(1024)S(1)} all-reduce(f32[1024]{0:T(1024)S(1)} %multiply_reduce_fusion), channel_id=1, replica_groups=mesh['zl'=4,'y'=4,'c'=2,'zh'=4,'x'=4] {'c'}, use_global_device_ids=true, to_apply=%region_4.0 | all-reduce | flops 1024 | bytes 8192 | tf_op jit(solution)/shard_map/psum | solution.py:21
  100.7 9.2 %psum.52 = f32[1024]{0:T(1024)S(1)} all-reduce(f32[1024]{0:T(1024)S(1)} %psum.51), channel_id=1, replica_groups=mesh['zl'=4,'y'=4,'c'=2,'zh'=4,'x'=4] {'y'}, use_global_device_ids=true, to_apply=%region_5.0 | all-reduce | flops 1024 | bytes 8192 | tf_op jit(solution)/shard_map/psum | solution.py:21
  109.9 10.4 %psum.53 = f32[1024]{0:T(1024)S(1)} all-reduce(f32[1024]{0:T(1024)S(1)} %psum.52), channel_id=1, replica_groups=mesh['zl'=4,'y'=4,'c'=2,'zh'=4,'x'=4] {'zl'}, use_global_device_ids=true, to_apply=%region_6.0 | all-reduce | flops 1024 | bytes 8192 | tf_op jit(solution)/shard_map/psum | solution.py:21
  120.3 0.0 copy-done.4
  120.3 0.0 copy-done.5
  120.3 0.0 copy-start
  120.4 5.1 %fusion.5 = f32[2048,128]{1,0:T(8,128)S(1)} fusion(bf16[1024,128]{1,0:T(8,128)(2,1)S(1)} %bitcast.28, f32[2048,1024]{0,1:T(8,128)} %get-tuple-element.3, f32[1024]{0:T(1024)S(1)} %rsqrt_multiply_fusion, f32[2048]{0:T(1024)S(1)} %add_divide_fusion), kind=kOutput, calls=%fused_computation.12 | convolution fusion | flops 541327360 | bytes 9711616 | tf_op jit(solution)/shard_map/dot_general | solution.py:91
  125.5 0.6 copy-done
  126.1 0.0 copy-start.3
  126.1 0.0 copy-start.1
  126.1 0.6 multiply_reduce_fusion.1
  126.7 8.7 %psum.54 = f32[2048]{0:T(1024)S(1)} all-reduce(f32[2048]{0:T(1024)S(1)} %multiply_reduce_fusion.1), channel_id=1, replica_groups=mesh['zl'=4,'y'=4,'c'=2,'zh'=4,'x'=4] {'x'}, use_global_device_ids=true, to_apply=%region_8.0 | all-reduce | flops 2048 | bytes 16384 | tf_op jit(solution)/shard_map/psum | solution.py:21
  135.4 13.9 %psum.55 = f32[2048]{0:T(1024)S(1)} all-reduce(f32[2048]{0:T(1024)S(1)} %psum.54), channel_id=1, replica_groups=mesh['zl'=4,'y'=4,'c'=2,'zh'=4,'x'=4] {'zh'}, use_global_device_ids=true, to_apply=%region_9.0 | all-reduce | flops 2048 | bytes 16384 | tf_op jit(solution)/shard_map/psum | solution.py:21
  149.4 0.0 copy-done.3
  149.4 0.0 copy-done.1
  149.4 4.5 %fusion = bf16[1024,2048]{1,0:T(8,128)(2,1)S(1)} fusion(f32[2048,1024]{0,1:T(8,128)} %get-tuple-element.3, f32[1024]{0:T(1024)S(1)} %rsqrt_multiply_fusion, f32[2048]{0:T(1024)S(1)} %add_divide_fusion, f32[1024]{0:T(1024)S(1)} %copy-done.1, f32[2048]{0:T(1024)S(1)} %negate_divide_fusion), kind=kLoop, calls=%fused_computation.1 | loop fusion | flops 12582912 | bytes 12607488 | tf_op jit(solution)/shard_map/convert_element_type | solution.py:109
  153.9 1.2 convolution_bitcast_fusion
  155.2 4.2 %all_to_all.66 = f32[1,4,4,2,32,128]{5,4,2,1,0,3:T(8,128)S(1)} all-to-all(f32[1,4,4,2,32,128]{5,4,2,1,0,3:T(8,128)S(1)} %copy.24), channel_id=1, replica_groups=mesh['zl'=4,'y'=4,'c'=2,'zh'=4,'x'=4] {'c'}, dimensions={3} | all-to-all | bytes 1048576 | tf_op jit(solution)/shard_map/all_to_all | solution.py:62
  159.4 0.7 copy.25
  160.1 4.5 %all-to-all-start.8 = ((f32[1,4,4,32,128]{4,3,1,0,2:T(8,128)}), f32[1,4,4,32,128]{4,3,1,0,2:T(8,128)S(1)}, u32[]{:S(2)}, u32[]{:S(2)}) async-start(f32[1,4,4,32,128]{4,3,1,0,2:T(8,128)} %copy.25), calls=%async_computation.8 | async-start | bytes 524288 | tf_op jit(solution)/shard_map/all_to_all | solution.py:62
  164.6 5.0 %fusion.8 = f32[2048,128]{1,0:T(8,128)S(1)} fusion(f32[2048,128]{1,0:T(8,128)S(1)} %fusion.5, bf16[1024,128]{1,0:T(8,128)(2,1)S(1)} %bitcast.29, f32[2048,1024]{0,1:T(8,128)} %get-tuple-element.3, f32[1024]{0:T(1024)S(1)} %copy-done.1, f32[2048]{0:T(1024)S(1)} %negate_divide_fusion), kind=kOutput, calls=%fused_computation.15 | convolution fusion | flops 541851648 | bytes 10760192 | tf_op jit(solution)/shard_map/dot_general | solution.py:78
  169.6 1.1 copy.23
  170.7 0.0 all-to-all-done.8
  170.7 3.5 %all-to-all-start.5 = ((f32[1,4,4,128,128]{4,3,1,0,2:T(8,128)}), f32[1,4,4,128,128]{4,3,1,0,2:T(8,128)S(1)}, u32[]{:S(2)}, u32[]{:S(2)}) async-start(f32[1,4,4,128,128]{4,3,1,0,2:T(8,128)} %copy.23), calls=%async_computation.5 | async-start | bytes 2097152 | tf_op jit(solution)/shard_map/all_to_all | solution.py:62
  174.2 0.6 reduce_sum.78
  174.9 14.7 %all-to-all-done.5 = f32[1,4,4,128,128]{4,3,1,0,2:T(8,128)S(1)} async-done(((f32[1,4,4,128,128]{4,3,1,0,2:T(8,128)}), f32[1,4,4,128,128]{4,3,1,0,2:T(8,128)S(1)}, u32[]{:S(2)}, u32[]{:S(2)}) %all-to-all-start.5) | async-done | bytes 1048608 | tf_op jit(solution)/shard_map/all_to_all | solution.py:62
  189.6 3.3 %all-to-all-start.9 = ((f32[4,32,128]{2,1,0:T(8,128)}), f32[4,32,128]{2,1,0:T(8,128)S(1)}, u32[]{:S(2)}, u32[]{:S(2)}) async-start(f32[4,32,128]{2,1,0:T(8,128)} %reduce_sum.78), calls=%async_computation.9 | async-start | bytes 131072 | tf_op jit(solution)/shard_map/all_to_all | solution.py:62
  192.9 0.8 reduce_sum.75
  193.6 4.9 %all-to-all-done.9 = f32[4,32,128]{2,1,0:T(8,128)S(1)} async-done(((f32[4,32,128]{2,1,0:T(8,128)}), f32[4,32,128]{2,1,0:T(8,128)S(1)}, u32[]{:S(2)}, u32[]{:S(2)}) %all-to-all-start.9) | async-done | bytes 65568 | tf_op jit(solution)/shard_map/all_to_all | solution.py:62
  198.6 6.6 %all-to-all-start.6 = ((f32[4,128,128]{2,1,0:T(8,128)}), f32[4,128,128]{2,1,0:T(8,128)S(1)}, u32[]{:S(2)}, u32[]{:S(2)}) async-start(f32[4,128,128]{2,1,0:T(8,128)} %reduce_sum.75), calls=%async_computation.6 | async-start | bytes 524288 | tf_op jit(solution)/shard_map/all_to_all | solution.py:62
  205.2 0.6 reduce_sum.79
  205.8 17.4 %all-to-all-done.6 = f32[4,128,128]{2,1,0:T(8,128)S(1)} async-done(((f32[4,128,128]{2,1,0:T(8,128)}), f32[4,128,128]{2,1,0:T(8,128)S(1)}, u32[]{:S(2)}, u32[]{:S(2)}) %all-to-all-start.6) | async-done | bytes 262176 | tf_op jit(solution)/shard_map/all_to_all | solution.py:62
  223.3 0.6 reduce_sum.76
  (10 shorter events, 0.2 us)
Async XLA Ops:
  22.1 72.1 %copy-start.2 = (s32[2048]{0:T(1024)S(1)}, s32[2048]{0:T(1024)}, u32[]{:S(2)}) copy-start(s32[2048]{0:T(1024)} %param.9) | copy-start | bytes 24580
  54.9 12.4 %all-to-all-start.1 = ((bf16[4,4,128,128]{3,2,1,0:T(8,128)(2,1)}), bf16[4,4,128,128]{3,2,1,0:T(8,128)(2,1)S(1)}, u32[]{:S(2)}, u32[]{:S(2)}) async-start(bf16[4,4,128,128]{3,2,1,0:T(8,128)(2,1)} %broadcast_in_dim.13), calls=%async_computation.1 | async-start | bytes 1048576 | tf_op jit(solution)/shard_map/all_to_all | solution.py:29
  67.3 53.0 %copy-start.4 = (s32[1024]{0:T(1024)S(1)}, s32[1024]{0:T(1024)}, u32[]{:S(2)}) copy-start(s32[1024]{0:T(1024)} %param.10) | copy-start | bytes 12292
  67.3 53.0 %copy-start.5 = (f32[1024]{0:T(1024)S(1)}, f32[1024]{0:T(1024)}, u32[]{:S(2)}) copy-start(f32[1024]{0:T(1024)} %param.13) | copy-start | bytes 12292
  120.3 5.8 %copy-start = (f32[2048,1024]{0,1:T(8,128)S(1)}, f32[2048,1024]{0,1:T(8,128)}, u32[]{:S(2)}) copy-start(f32[2048,1024]{0,1:T(8,128)} %get-tuple-element.3) | copy-start | bytes 25165828
  126.1 23.2 %copy-start.3 = (f32[2048]{0:T(1024)S(1)}, f32[2048]{0:T(1024)}, u32[]{:S(2)}) copy-start(f32[2048]{0:T(1024)} %param.12) | copy-start | bytes 24580
  126.1 23.3 %copy-start.1 = (f32[1024]{0:T(1024)S(1)}, f32[1024]{0:T(1024)}, u32[]{:S(2)}) copy-start(f32[1024]{0:T(1024)} %param.11) | copy-start | bytes 12292
  160.1 10.6 %all-to-all-start.8 = ((f32[1,4,4,32,128]{4,3,1,0,2:T(8,128)}), f32[1,4,4,32,128]{4,3,1,0,2:T(8,128)S(1)}, u32[]{:S(2)}, u32[]{:S(2)}) async-start(f32[1,4,4,32,128]{4,3,1,0,2:T(8,128)} %copy.25), calls=%async_computation.8 | async-start | bytes 524288 | tf_op jit(solution)/shard_map/all_to_all | solution.py:62
  170.7 18.9 %all-to-all-start.5 = ((f32[1,4,4,128,128]{4,3,1,0,2:T(8,128)}), f32[1,4,4,128,128]{4,3,1,0,2:T(8,128)S(1)}, u32[]{:S(2)}, u32[]{:S(2)}) async-start(f32[1,4,4,128,128]{4,3,1,0,2:T(8,128)} %copy.23), calls=%async_computation.5 | async-start | bytes 2097152 | tf_op jit(solution)/shard_map/all_to_all | solution.py:62
  189.6 9.0 %all-to-all-start.9 = ((f32[4,32,128]{2,1,0:T(8,128)}), f32[4,32,128]{2,1,0:T(8,128)S(1)}, u32[]{:S(2)}, u32[]{:S(2)}) async-start(f32[4,32,128]{2,1,0:T(8,128)} %reduce_sum.78), calls=%async_computation.9 | async-start | bytes 131072 | tf_op jit(solution)/shard_map/all_to_all | solution.py:62
  198.6 24.7 %all-to-all-start.6 = ((f32[4,128,128]{2,1,0:T(8,128)}), f32[4,128,128]{2,1,0:T(8,128)S(1)}, u32[]{:S(2)}, u32[]{:S(2)}) async-start(f32[4,128,128]{2,1,0:T(8,128)} %reduce_sum.75), calls=%async_computation.6 | async-start | bytes 524288 | tf_op jit(solution)/shard_map/all_to_all | solution.py:62

commit v8 on v3

--- a/solution.py
+++ b/solution.py
@@ -25,7 +25,11 @@
 def ordered_gather(x, axes, order):
     got = []
     for a in order:
-        x = lax.all_gather(x, a, axis=0, tiled=False)
+        if a == "zh":
+            x = lax.all_gather(x, a, axis=0, tiled=False)
+        else:
+            n = lax.axis_size(a)
+            x = lax.all_to_all(jnp.broadcast_to(x[None], (n,) + x.shape), a, 0, 0, tiled=False)
         got.insert(0, a)
     lead = len(axes)
     x = jnp.transpose(x, [got.index(a) for a in axes] + list(range(lead, x.ndim)))

time: 228 us -> 219 us (0.961)
  blocking collectives: 132 us -> 107 us
  waiting for transfers between devices: 34.2 us -> 44.8 us
  starting transfers between devices: 27.3 us -> 32.1 us
  other arithmetic: 14.6 us -> 11.2 us
    all_gather x5 -> x1, blocking collectives: 65.3 us -> 23.4 us  [ordered_gather(): x = lax.all_gather(x, a, axis=0, tiled=False)]
    all_to_all x0 -> x3, blocking collectives: none -> 18.3 us  [the longest x2 14.1 us: ordered_gather(): lax.all_to_all(jnp.broadcast_to(x[None], (n,) + x.shape), a, 0, 0, tiled=...]
    all_to_all x0 -> x2, starting transfers between devices: none -> 10 us  [ordered_gather(): lax.all_to_all(jnp.broadcast_to(x[None], (n,) + x.shape), a, 0, 0, tiled=...]
    all_to_all x0 -> x2, waiting for transfers between devices: none -> 9.77 us  [ordered_gather(): lax.all_to_all(jnp.broadcast_to(x[None], (n,) + x.shape), a, 0, 0, tiled=...]
    all_to_all x4 -> x3, starting transfers between devices: 18.1 us -> 12.9 us  [a2a_scatter(): x = jnp.sum(lax.all_to_all(x, a, d, 0, tiled=False), axis=0)]
    reduce_sum x1, other arithmetic: 4 us -> 0.62 us  [body(): row_cot = nested_psum(jnp.sum(weighted, axis=1), ('x', 'zh'))]
    broadcast_in_dim x0 -> x4, local copies, waits for them, and re-layouts: none -> 2.29 us  [ordered_gather(): jnp.broadcast_to(x[None], (n,) + x.shape)]
    all_to_all x4 -> x3, waiting for transfers between devices: 15.2 us -> 14.8 us  [a2a_scatter(): x = jnp.sum(lax.all_to_all(x, a, d, 0, tiled=False), axis=0)]
  transfers between devices with their start and end apart: 6 -> 7, of which waited for: 3 -> 4; matrix products, arithmetic and copies ran while one was open for 6% -> 1% of each run, Pallas kernels for 0% -> 0%
where the time goes in v8:
time: 219 us; the launch traced here: 218 us
  blocking collectives  107 us (49%)
  waiting for transfers between devices  44.8 us (20%)
  starting transfers between devices  32.1 us (15%)
  matrix products  16.2 us (7%)
  other arithmetic  11.2 us (5%)
  local copies, waits for them, and re-layouts  4.87 us (2%)
    psum x7, blocking collectives, nested_psum(): x = lax.psum(x, a)  65.8 us
    all_gather x1, blocking collectives, ordered_gather(): x = lax.all_gather(x, a, axis=0, tiled=False)  23.4 us
    ppermute x2, waiting for transfers between devices, halving_scatter(): got = lax.ppermute(send, a, [(i, i ^ k) for i in range(n)])  20.2 us
    all_to_all x3, waiting for transfers between devices, a2a_scatter(): x = jnp.sum(lax.all_to_all(x, a, d, 0, tiled=False), axis=0)  14.8 us
    all_to_all x2, blocking collectives, ordered_gather(): lax.all_to_all(jnp.broadcast_to(x[None], (n,) + x.shape), a, 0, 0, tiled=...  14.1 us
    all_to_all x3, starting transfers between devices, a2a_scatter(): x = jnp.sum(lax.all_to_all(x, a, d, 0, tiled=False), axis=0)  12.9 us
    dot_general x2, matrix products, body(): jnp.dot(weighted.astype(jnp.bfloat16), women_rows, preferred_element_type...  10.1 us
    all_to_all x2, starting transfers between devices, ordered_gather(): lax.all_to_all(jnp.broadcast_to(x[None], (n,) + x.shape), a, 0, 0, tiled=...  10 us
  transfers between devices with their start and end apart: 7, of which 4 were waited for; matrix products, arithmetic and copies ran while one was open for 1% of the time, Pallas kernels for 0%

profile of v8, /device:TPU:40, one launch (start us, length us, event | category | flops | bytes accessed | tf_op | source)
XLA Modules:
  0.0 217.6 jit_solution(14122023253395701139)
XLA Ops:
  0.6 0.7 broadcast_in_dim.11
  1.3 10.2 %all_to_all.52 = bf16[4,32,128]{2,1,0:T(8,128)(2,1)S(1)} all-to-all(bf16[4,32,128]{2,1,0:T(8,128)(2,1)S(1)} %broadcast_in_dim.11), channel_id=1, replica_groups=mesh['zl'=4,'y'=4,'c'=2,'zh'=4,'x'=4] {'zl'}, dimensions={0} | all-to-all | bytes 65536 | tf_op jit(solution)/shard_map/all_to_all | solution.py:32
  11.5 0.7 broadcast_in_dim.12
  12.1 5.7 %all-to-all-start.2 = ((bf16[4,4,32,128]{3,2,1,0:T(8,128)(2,1)}), bf16[4,4,32,128]{3,2,1,0:T(8,128)(2,1)S(1)}, u32[]{:S(2)}, u32[]{:S(2)}) async-start(bf16[4,4,32,128]{3,2,1,0:T(8,128)(2,1)} %broadcast_in_dim.12), calls=%async_computation.2 | async-start | bytes 262144 | tf_op jit(solution)/shard_map/all_to_all | solution.py:32
  17.9 23.4 %all-gather = bf16[512,128]{1,0:T(8,128)(2,1)S(1)} all-gather(bf16[128,128]{1,0:T(8,128)(2,1)} %param.7), channel_id=2, replica_groups=mesh['zl'=4,'y'=4,'c'=2,'zh'=4,'x'=4] {'zh'}, dimensions={0}, use_global_device_ids=true | all-gather | bytes 163840 | tf_op jit(solution)/shard_map/all_gather | solution.py:29
  41.3 0.0 all-to-all-done.2
  41.3 0.0 copy-start.2
  41.4 3.9 %all_to_all.53 = bf16[2,4,4,32,128]{4,3,1,2,0:T(8,128)(2,1)S(1)} all-to-all(bf16[2,4,4,32,128]{4,3,1,2,0:T(8,128)(2,1)S(1)} %broadcast_in_dim.13), channel_id=1, replica_groups=mesh['zl'=4,'y'=4,'c'=2,'zh'=4,'x'=4] {'c'}, dimensions={0} | all-to-all | bytes 524288 | tf_op jit(solution)/shard_map/all_to_all | solution.py:32
  45.3 0.9 broadcast_in_dim.10
  46.2 4.3 %all-to-all-start = ((bf16[4,4,128,128]{3,2,1,0:T(8,128)(2,1)}), bf16[4,4,128,128]{3,2,1,0:T(8,128)(2,1)S(1)}, u32[]{:S(2)}, u32[]{:S(2)}) async-start(bf16[4,4,128,128]{3,2,1,0:T(8,128)(2,1)} %broadcast_in_dim.10), calls=%async_computation | async-start | bytes 1048576 | tf_op jit(solution)/shard_map/all_to_all | solution.py:32
  50.5 9.8 %all-to-all-done = bf16[4,4,128,128]{3,2,1,0:T(8,128)(2,1)S(1)} async-done(((bf16[4,4,128,128]{3,2,1,0:T(8,128)(2,1)}), bf16[4,4,128,128]{3,2,1,0:T(8,128)(2,1)S(1)}, u32[]{:S(2)}, u32[]{:S(2)}) %all-to-all-start) | async-done | bytes 524320 | tf_op jit(solution)/shard_map/all_to_all | solution.py:32
  60.3 0.0 copy-start.4
  60.3 0.0 copy-start.5
  60.3 4.8 %multiply_reduce_fusion.2 = (f32[2048]{0:T(1024)S(1)}, f32[2048,1024]{0,1:T(8,128)}) fusion(f32[1024]{0:T(1024)} %param.11, bf16[2048,128]{1,0:T(8,128)(2,1)S(1)} %bitcast.28, bf16[1024,128]{1,0:T(8,128)(2,1)S(1)} %bitcast.30), kind=kOutput, calls=%fused_computation.7 | convolution fusion | flops 543160320 | bytes 9187328 | tf_op jit(solution)/shard_map/dot_general | solution.py:13
  65.2 9.0 %psum.49 = f32[2048]{0:T(1024)S(1)} all-reduce(f32[2048]{0:T(1024)S(1)} %get-tuple-element.2), channel_id=1, replica_groups=mesh['zl'=4,'y'=4,'c'=2,'zh'=4,'x'=4] {'x'}, use_global_device_ids=true, to_apply=%region_1.0 | all-reduce | flops 2048 | bytes 16384 | tf_op jit(solution)/shard_map/psum | solution.py:21
  74.2 13.0 %psum.50 = f32[2048]{0:T(1024)S(1)} all-reduce(f32[2048]{0:T(1024)S(1)} %psum.49), channel_id=1, replica_groups=mesh['zl'=4,'y'=4,'c'=2,'zh'=4,'x'=4] {'zh'}, use_global_device_ids=true, to_apply=%region_2.0 | all-reduce | flops 2048 | bytes 16384 | tf_op jit(solution)/shard_map/psum | solution.py:21
  87.1 0.0 copy-done.2
  87.2 4.0 %multiply_reduce_fusion = f32[1024]{0:T(1024)S(1)} fusion(f32[2048,1024]{0,1:T(8,128)} %get-tuple-element.3, f32[2048]{0:T(1024)S(1)} %add_divide_fusion), kind=kLoop, calls=%fused_computation.2 | loop fusion | flops 4193280 | bytes 8400896 | tf_op jit(solution)/shard_map/reduce_sum | solution.py:88
  91.2 2.5 %psum.51 = f32[1024]{0:T(1024)S(1)} all-reduce(f32[1024]{0:T(1024)S(1)} %multiply_reduce_fusion), channel_id=1, replica_groups=mesh['zl'=4,'y'=4,'c'=2,'zh'=4,'x'=4] {'c'}, use_global_device_ids=true, to_apply=%region_4.0 | all-reduce | flops 1024 | bytes 8192 | tf_op jit(solution)/shard_map/psum | solution.py:21
  93.6 8.6 %psum.52 = f32[1024]{0:T(1024)S(1)} all-reduce(f32[1024]{0:T(1024)S(1)} %psum.51), channel_id=1, replica_groups=mesh['zl'=4,'y'=4,'c'=2,'zh'=4,'x'=4] {'y'}, use_global_device_ids=true, to_apply=%region_5.0 | all-reduce | flops 1024 | bytes 8192 | tf_op jit(solution)/shard_map/psum | solution.py:21
  102.2 9.1 %psum.53 = f32[1024]{0:T(1024)S(1)} all-reduce(f32[1024]{0:T(1024)S(1)} %psum.52), channel_id=1, replica_groups=mesh['zl'=4,'y'=4,'c'=2,'zh'=4,'x'=4] {'zl'}, use_global_device_ids=true, to_apply=%region_6.0 | all-reduce | flops 1024 | bytes 8192 | tf_op jit(solution)/shard_map/psum | solution.py:21
  111.3 0.0 copy-done.4
  111.3 0.0 copy-done.5
  111.3 0.0 copy-start
  111.3 5.1 %fusion.5 = f32[2048,128]{1,0:T(8,128)S(1)} fusion(bf16[1024,128]{1,0:T(8,128)(2,1)S(1)} %bitcast.31, f32[2048,1024]{0,1:T(8,128)} %get-tuple-element.3, f32[1024]{0:T(1024)S(1)} %rsqrt_multiply_fusion, f32[2048]{0:T(1024)S(1)} %add_divide_fusion), kind=kOutput, calls=%fused_computation.12 | convolution fusion | flops 541327360 | bytes 9711616 | tf_op jit(solution)/shard_map/dot_general | solution.py:94
  116.4 0.6 copy-done
  117.0 0.0 copy-start.3
  117.0 0.0 copy-start.1
  117.1 0.6 multiply_reduce_fusion.1
  117.7 8.8 %psum.54 = f32[2048]{0:T(1024)S(1)} all-reduce(f32[2048]{0:T(1024)S(1)} %multiply_reduce_fusion.1), channel_id=1, replica_groups=mesh['zl'=4,'y'=4,'c'=2,'zh'=4,'x'=4] {'x'}, use_global_device_ids=true, to_apply=%region_8.0 | all-reduce | flops 2048 | bytes 16384 | tf_op jit(solution)/shard_map/psum | solution.py:21
  126.4 15.0 %psum.55 = f32[2048]{0:T(1024)S(1)} all-reduce(f32[2048]{0:T(1024)S(1)} %psum.54), channel_id=1, replica_groups=mesh['zl'=4,'y'=4,'c'=2,'zh'=4,'x'=4] {'zh'}, use_global_device_ids=true, to_apply=%region_9.0 | all-reduce | flops 2048 | bytes 16384 | tf_op jit(solution)/shard_map/psum | solution.py:21
  141.5 0.0 copy-done.3
  141.5 0.0 copy-done.1
  141.5 4.5 %fusion = bf16[1024,2048]{1,0:T(8,128)(2,1)S(1)} fusion(f32[2048,1024]{0,1:T(8,128)} %get-tuple-element.3, f32[1024]{0:T(1024)S(1)} %rsqrt_multiply_fusion, f32[2048]{0:T(1024)S(1)} %add_divide_fusion, f32[1024]{0:T(1024)S(1)} %copy-done.1, f32[2048]{0:T(1024)S(1)} %negate_divide_fusion), kind=kLoop, calls=%fused_computation.1 | loop fusion | flops 12582912 | bytes 12607488 | tf_op jit(solution)/shard_map/convert_element_type | solution.py:112
  146.0 5.0 %fusion.8 = f32[2048,128]{1,0:T(8,128)S(1)} fusion(f32[2048,128]{1,0:T(8,128)S(1)} %fusion.5, bf16[1024,128]{1,0:T(8,128)(2,1)S(1)} %bitcast.32, f32[2048,1024]{0,1:T(8,128)} %get-tuple-element.3, f32[1024]{0:T(1024)S(1)} %copy-done.1, f32[2048]{0:T(1024)S(1)} %negate_divide_fusion), kind=kOutput, calls=%fused_computation.15 | convolution fusion | flops 541851648 | bytes 10760192 | tf_op jit(solution)/shard_map/dot_general | solution.py:81
  151.0 1.1 copy.23
  152.1 1.2 convolution_bitcast_fusion
  153.3 4.2 %all_to_all.54 = f32[1,4,4,2,32,128]{5,4,2,1,0,3:T(8,128)S(1)} all-to-all(f32[1,4,4,2,32,128]{5,4,2,1,0,3:T(8,128)S(1)} %copy.24), channel_id=1, replica_groups=mesh['zl'=4,'y'=4,'c'=2,'zh'=4,'x'=4] {'c'}, dimensions={3} | all-to-all | bytes 1048576 | tf_op jit(solution)/shard_map/all_to_all | solution.py:65
  157.5 3.5 %all-to-all-start.4 = ((f32[1,4,4,128,128]{4,3,1,0,2:T(8,128)}), f32[1,4,4,128,128]{4,3,1,0,2:T(8,128)S(1)}, u32[]{:S(2)}, u32[]{:S(2)}) async-start(f32[1,4,4,128,128]{4,3,1,0,2:T(8,128)} %copy.23), calls=%async_computation.4 | async-start | bytes 2097152 | tf_op jit(solution)/shard_map/all_to_all | solution.py:65
  161.1 0.7 copy.25
  161.8 14.8 %all-to-all-done.4 = f32[1,4,4,128,128]{4,3,1,0,2:T(8,128)S(1)} async-done(((f32[1,4,4,128,128]{4,3,1,0,2:T(8,128)}), f32[1,4,4,128,128]{4,3,1,0,2:T(8,128)S(1)}, u32[]{:S(2)}, u32[]{:S(2)}) %all-to-all-start.4) | async-done | bytes 1048608 | tf_op jit(solution)/shard_map/all_to_all | solution.py:65
  176.7 5.8 %all-to-all-start.6 = ((f32[1,4,4,32,128]{4,3,1,0,2:T(8,128)}), f32[1,4,4,32,128]{4,3,1,0,2:T(8,128)S(1)}, u32[]{:S(2)}, u32[]{:S(2)}) async-start(f32[1,4,4,32,128]{4,3,1,0,2:T(8,128)} %copy.25), calls=%async_computation.6 | async-start | bytes 524288 | tf_op jit(solution)/shard_map/all_to_all | solution.py:65
  182.4 0.1 reduce_sum.66
  182.5 7.3 %collective-permute-start = (f32[2,128,128]{2,1,0:T(8,128)S(1)}, f32[2,128,128]{2,1,0:T(8,128)S(1)}, u32[]{:S(2)}, u32[]{:S(2)}) collective-permute-start(f32[2,128,128]{2,1,0:T(8,128)S(1)} %constant_dynamic-slice_fusion.1), channel_id=1, source_target_pairs={{0,8},{4,12},{8,0},{12,4},{1,9},{5,13},{9,1},{13,5},{2,10},{6,14},... | collective-permute-start | bytes 393224 | tf_op jit(solution)/shard_map/ppermute | solution.py:55
  189.8 0.0 all-to-all-done.6
  189.8 0.6 reduce_sum.68
  190.5 3.6 %all-to-all-start.7 = ((f32[4,32,128]{2,1,0:T(8,128)}), f32[4,32,128]{2,1,0:T(8,128)S(1)}, u32[]{:S(2)}, u32[]{:S(2)}) async-start(f32[4,32,128]{2,1,0:T(8,128)} %reduce_sum.68), calls=%async_computation.7 | async-start | bytes 131072 | tf_op jit(solution)/shard_map/all_to_all | solution.py:65
  194.1 12.7 %collective-permute-done = f32[2,128,128]{2,1,0:T(8,128)S(1)} collective-permute-done((f32[2,128,128]{2,1,0:T(8,128)S(1)}, f32[2,128,128]{2,1,0:T(8,128)S(1)}, u32[]{:S(2)}, u32[]{:S(2)}) %collective-permute-start) | collective-permute-done | bytes 131104 | tf_op jit(solution)/shard_map/ppermute | solution.py:55
  206.9 1.9 collective-permute-start.1
  208.8 0.0 all-to-all-done.7
  208.8 0.6 reduce_sum.69
  209.4 7.5 %collective-permute-done.1 = f32[1,128,128]{2,1,0:T(8,128)S(1)} collective-permute-done((f32[1,128,128]{2,1,0:T(8,128)S(1)}, f32[1,128,128]{2,1,0:T(8,128)S(1)}, u32[]{:S(2)}, u32[]{:S(2)}) %collective-permute-start.1) | collective-permute-done | bytes 65568 | tf_op jit(solution)/shard_map/ppermute | solution.py:55
  216.9 0.6 add_bitcast_fusion
  (12 shorter events, 0.3 us)
Async XLA Ops:
  12.1 29.1 %all-to-all-start.2 = ((bf16[4,4,32,128]{3,2,1,0:T(8,128)(2,1)}), bf16[4,4,32,128]{3,2,1,0:T(8,128)(2,1)S(1)}, u32[]{:S(2)}, u32[]{:S(2)}) async-start(bf16[4,4,32,128]{3,2,1,0:T(8,128)(2,1)} %broadcast_in_dim.12), calls=%async_computation.2 | async-start | bytes 262144 | tf_op jit(solution)/shard_map/all_to_all | solution.py:32
  41.3 45.8 %copy-start.2 = (s32[2048]{0:T(1024)S(1)}, s32[2048]{0:T(1024)}, u32[]{:S(2)}) copy-start(s32[2048]{0:T(1024)} %param.9) | copy-start | bytes 24580
  46.2 14.1 %all-to-all-start = ((bf16[4,4,128,128]{3,2,1,0:T(8,128)(2,1)}), bf16[4,4,128,128]{3,2,1,0:T(8,128)(2,1)S(1)}, u32[]{:S(2)}, u32[]{:S(2)}) async-start(bf16[4,4,128,128]{3,2,1,0:T(8,128)(2,1)} %broadcast_in_dim.10), calls=%async_computation | async-start | bytes 1048576 | tf_op jit(solution)/shard_map/all_to_all | solution.py:32
  60.3 50.9 %copy-start.4 = (s32[1024]{0:T(1024)S(1)}, s32[1024]{0:T(1024)}, u32[]{:S(2)}) copy-start(s32[1024]{0:T(1024)} %param.10) | copy-start | bytes 12292
  60.3 50.9 %copy-start.5 = (f32[1024]{0:T(1024)S(1)}, f32[1024]{0:T(1024)}, u32[]{:S(2)}) copy-start(f32[1024]{0:T(1024)} %param.13) | copy-start | bytes 12292
  111.3 5.8 %copy-start = (f32[2048,1024]{0,1:T(8,128)S(1)}, f32[2048,1024]{0,1:T(8,128)}, u32[]{:S(2)}) copy-start(f32[2048,1024]{0,1:T(8,128)} %get-tuple-element.3) | copy-start | bytes 25165828
  117.0 24.4 %copy-start.3 = (f32[2048]{0:T(1024)S(1)}, f32[2048]{0:T(1024)}, u32[]{:S(2)}) copy-start(f32[2048]{0:T(1024)} %param.12) | copy-start | bytes 24580
  117.0 24.5 %copy-start.1 = (f32[1024]{0:T(1024)S(1)}, f32[1024]{0:T(1024)}, u32[]{:S(2)}) copy-start(f32[1024]{0:T(1024)} %param.11) | copy-start | bytes 12292
  157.5 19.2 %all-to-all-start.4 = ((f32[1,4,4,128,128]{4,3,1,0,2:T(8,128)}), f32[1,4,4,128,128]{4,3,1,0,2:T(8,128)S(1)}, u32[]{:S(2)}, u32[]{:S(2)}) async-start(f32[1,4,4,128,128]{4,3,1,0,2:T(8,128)} %copy.23), calls=%async_computation.4 | async-start | bytes 2097152 | tf_op jit(solution)/shard_map/all_to_all | solution.py:65
  176.7 13.2 %all-to-all-start.6 = ((f32[1,4,4,32,128]{4,3,1,0,2:T(8,128)}), f32[1,4,4,32,128]{4,3,1,0,2:T(8,128)S(1)}, u32[]{:S(2)}, u32[]{:S(2)}) async-start(f32[1,4,4,32,128]{4,3,1,0,2:T(8,128)} %copy.25), calls=%async_computation.6 | async-start | bytes 524288 | tf_op jit(solution)/shard_map/all_to_all | solution.py:65
  182.5 24.3 %collective-permute-start = (f32[2,128,128]{2,1,0:T(8,128)S(1)}, f32[2,128,128]{2,1,0:T(8,128)S(1)}, u32[]{:S(2)}, u32[]{:S(2)}) collective-permute-start(f32[2,128,128]{2,1,0:T(8,128)S(1)} %constant_dynamic-slice_fusion.1), channel_id=1, source_target_pairs={{0,8},{4,12},{8,0},{12,4},{1,9},{5,13},{9,1},{13,5},{2,10},{6,14},... | collective-permute-start | bytes 393224 | tf_op jit(solution)/shard_map/ppermute | solution.py:55
  190.5 18.3 %all-to-all-start.7 = ((f32[4,32,128]{2,1,0:T(8,128)}), f32[4,32,128]{2,1,0:T(8,128)S(1)}, u32[]{:S(2)}, u32[]{:S(2)}) async-start(f32[4,32,128]{2,1,0:T(8,128)} %reduce_sum.68), calls=%async_computation.7 | async-start | bytes 131072 | tf_op jit(solution)/shard_map/all_to_all | solution.py:65
  206.9 10.1 %collective-permute-start.1 = (f32[1,128,128]{2,1,0:T(8,128)S(1)}, f32[1,128,128]{2,1,0:T(8,128)S(1)}, u32[]{:S(2)}, u32[]{:S(2)}) collective-permute-start(f32[1,128,128]{2,1,0:T(8,128)S(1)} %constant_dynamic-slice_fusion), channel_id=1, source_target_pairs={{0,4},{4,0},{8,12},{12,8},{1,5},{5,1},{9,13},{13,9},{2,6},{6,2},{1... | collective-permute-start | bytes 196616 | tf_op jit(solution)/shard_map/ppermute | solution.py:55

commit v9 on v8

--- a/solution.py
+++ b/solution.py
@@ -25,7 +25,7 @@
 def ordered_gather(x, axes, order):
     got = []
     for a in order:
-        if a == "zh":
+        if a in ("zh", "c"):
             x = lax.all_gather(x, a, axis=0, tiled=False)
         else:
             n = lax.axis_size(a)

time: 219 us -> 213 us (0.973)
  waiting for transfers between devices: 44.8 us -> 41.2 us
    all_to_all x2 -> x1, blocking collectives: 14.1 us -> 10.2 us  [ordered_gather(): lax.all_to_all(jnp.broadcast_to(x[None], (n,) + x.shape), a, 0, 0, tiled=...]
    all_to_all x2, waiting for transfers between devices: 9.77 us -> 6.08 us  [ordered_gather(): lax.all_to_all(jnp.broadcast_to(x[None], (n,) + x.shape), a, 0, 0, tiled=...]
    all_gather x1 -> x2, blocking collectives: 23.4 us -> 25.4 us  [ordered_gather(): x = lax.all_gather(x, a, axis=0, tiled=False)]
where the time goes in v9:
time: 213 us; the launch traced here: 212 us
  blocking collectives  105 us (49%)
  waiting for transfers between devices  41.2 us (19%)
  starting transfers between devices  32.1 us (15%)
  matrix products  16.2 us (8%)
  other arithmetic  11.2 us (5%)
  local copies, waits for them, and re-layouts  4.82 us (2%)
    psum x7, blocking collectives, nested_psum(): x = lax.psum(x, a)  65.8 us
    all_gather x2, blocking collectives, ordered_gather(): x = lax.all_gather(x, a, axis=0, tiled=False)  25.4 us
    ppermute x2, waiting for transfers between devices, halving_scatter(): got = lax.ppermute(send, a, [(i, i ^ k) for i in range(n)])  20.3 us
    all_to_all x3, waiting for transfers between devices, a2a_scatter(): x = jnp.sum(lax.all_to_all(x, a, d, 0, tiled=False), axis=0)  14.8 us
    all_to_all x3, starting transfers between devices, a2a_scatter(): x = jnp.sum(lax.all_to_all(x, a, d, 0, tiled=False), axis=0)  12.9 us
    all_to_all x1, blocking collectives, ordered_gather(): lax.all_to_all(jnp.broadcast_to(x[None], (n,) + x.shape), a, 0, 0, tiled=...  10.2 us
    dot_general x2, matrix products, body(): jnp.dot(weighted.astype(jnp.bfloat16), women_rows, preferred_element_type...  10.1 us
    all_to_all x2, starting transfers between devices, ordered_gather(): lax.all_to_all(jnp.broadcast_to(x[None], (n,) + x.shape), a, 0, 0, tiled=...  10 us
  transfers between devices with their start and end apart: 7, of which 4 were waited for; matrix products, arithmetic and copies ran while one was open for 1% of the time, Pallas kernels for 0%

profile of v9, /device:TPU:40, one launch (start us, length us, event | category | flops | bytes accessed | tf_op | source)
XLA Modules:
  0.0 211.8 jit_solution(3909143856578944285)
XLA Ops:
  0.6 0.7 broadcast_in_dim.9
  1.3 10.2 %all_to_all.47 = bf16[4,32,128]{2,1,0:T(8,128)(2,1)S(1)} all-to-all(bf16[4,32,128]{2,1,0:T(8,128)(2,1)S(1)} %broadcast_in_dim.9), channel_id=1, replica_groups=mesh['zl'=4,'y'=4,'c'=2,'zh'=4,'x'=4] {'zl'}, dimensions={0} | all-to-all | bytes 65536 | tf_op jit(solution)/shard_map/all_to_all | solution.py:32
  11.5 0.0 copy-start.2
  11.5 0.7 broadcast_in_dim.10
  12.2 5.7 %all-to-all-start.2 = ((bf16[4,4,32,128]{3,2,1,0:T(8,128)(2,1)}), bf16[4,4,32,128]{3,2,1,0:T(8,128)(2,1)S(1)}, u32[]{:S(2)}, u32[]{:S(2)}) async-start(bf16[4,4,32,128]{3,2,1,0:T(8,128)(2,1)} %broadcast_in_dim.10), calls=%async_computation.2 | async-start | bytes 262144 | tf_op jit(solution)/shard_map/all_to_all | solution.py:32
  17.9 23.4 %all-gather = bf16[512,128]{1,0:T(8,128)(2,1)S(1)} all-gather(bf16[128,128]{1,0:T(8,128)(2,1)} %param.7), channel_id=2, replica_groups=mesh['zl'=4,'y'=4,'c'=2,'zh'=4,'x'=4] {'zh'}, dimensions={0}, use_global_device_ids=true | all-gather | bytes 163840 | tf_op jit(solution)/shard_map/all_gather | solution.py:29
  41.3 0.0 all-to-all-done.2
  41.3 0.9 broadcast_in_dim.8
  42.2 4.3 %all-to-all-start = ((bf16[4,4,128,128]{3,2,1,0:T(8,128)(2,1)}), bf16[4,4,128,128]{3,2,1,0:T(8,128)(2,1)S(1)}, u32[]{:S(2)}, u32[]{:S(2)}) async-start(bf16[4,4,128,128]{3,2,1,0:T(8,128)(2,1)} %broadcast_in_dim.8), calls=%async_computation | async-start | bytes 1048576 | tf_op jit(solution)/shard_map/all_to_all | solution.py:32
  46.5 2.0 all-gather.1
  48.5 6.1 %all-to-all-done = bf16[4,4,128,128]{3,2,1,0:T(8,128)(2,1)S(1)} async-done(((bf16[4,4,128,128]{3,2,1,0:T(8,128)(2,1)}), bf16[4,4,128,128]{3,2,1,0:T(8,128)(2,1)S(1)}, u32[]{:S(2)}, u32[]{:S(2)}) %all-to-all-start) | async-done | bytes 524320 | tf_op jit(solution)/shard_map/all_to_all | solution.py:32
  54.6 0.0 copy-start.4
  54.6 0.0 copy-start.5
  54.6 4.8 %multiply_reduce_fusion.2 = (f32[2048]{0:T(1024)S(1)}, f32[2048,1024]{0,1:T(8,128)}) fusion(f32[1024]{0:T(1024)} %param.11, bf16[2048,128]{1,0:T(8,128)(2,1)S(1)} %bitcast.29, bf16[1024,128]{1,0:T(8,128)(2,1)S(1)} %bitcast.31), kind=kOutput, calls=%fused_computation.7 | convolution fusion | flops 543160320 | bytes 9187328 | tf_op jit(solution)/shard_map/dot_general | solution.py:13
  59.5 9.0 %psum.49 = f32[2048]{0:T(1024)S(1)} all-reduce(f32[2048]{0:T(1024)S(1)} %get-tuple-element.2), channel_id=1, replica_groups=mesh['zl'=4,'y'=4,'c'=2,'zh'=4,'x'=4] {'x'}, use_global_device_ids=true, to_apply=%region_1.0 | all-reduce | flops 2048 | bytes 16384 | tf_op jit(solution)/shard_map/psum | solution.py:21
  68.4 13.0 %psum.50 = f32[2048]{0:T(1024)S(1)} all-reduce(f32[2048]{0:T(1024)S(1)} %psum.49), channel_id=1, replica_groups=mesh['zl'=4,'y'=4,'c'=2,'zh'=4,'x'=4] {'zh'}, use_global_device_ids=true, to_apply=%region_2.0 | all-reduce | flops 2048 | bytes 16384 | tf_op jit(solution)/shard_map/psum | solution.py:21
  81.4 0.0 copy-done.2
  81.4 4.0 %multiply_reduce_fusion = f32[1024]{0:T(1024)S(1)} fusion(f32[2048,1024]{0,1:T(8,128)} %get-tuple-element.3, f32[2048]{0:T(1024)S(1)} %add_divide_fusion), kind=kLoop, calls=%fused_computation.2 | loop fusion | flops 4193280 | bytes 8400896 | tf_op jit(solution)/shard_map/reduce_sum | solution.py:88
  85.4 2.5 %psum.51 = f32[1024]{0:T(1024)S(1)} all-reduce(f32[1024]{0:T(1024)S(1)} %multiply_reduce_fusion), channel_id=1, replica_groups=mesh['zl'=4,'y'=4,'c'=2,'zh'=4,'x'=4] {'c'}, use_global_device_ids=true, to_apply=%region_4.0 | all-reduce | flops 1024 | bytes 8192 | tf_op jit(solution)/shard_map/psum | solution.py:21
  87.9 8.6 %psum.52 = f32[1024]{0:T(1024)S(1)} all-reduce(f32[1024]{0:T(1024)S(1)} %psum.51), channel_id=1, replica_groups=mesh['zl'=4,'y'=4,'c'=2,'zh'=4,'x'=4] {'y'}, use_global_device_ids=true, to_apply=%region_5.0 | all-reduce | flops 1024 | bytes 8192 | tf_op jit(solution)/shard_map/psum | solution.py:21
  96.5 9.1 %psum.53 = f32[1024]{0:T(1024)S(1)} all-reduce(f32[1024]{0:T(1024)S(1)} %psum.52), channel_id=1, replica_groups=mesh['zl'=4,'y'=4,'c'=2,'zh'=4,'x'=4] {'zl'}, use_global_device_ids=true, to_apply=%region_6.0 | all-reduce | flops 1024 | bytes 8192 | tf_op jit(solution)/shard_map/psum | solution.py:21
  105.5 0.0 copy-done.4
  105.5 0.0 copy-done.5
  105.6 0.0 copy-start
  105.6 5.1 %fusion.5 = f32[2048,128]{1,0:T(8,128)S(1)} fusion(bf16[1024,128]{1,0:T(8,128)(2,1)S(1)} %bitcast.32, f32[2048,1024]{0,1:T(8,128)} %get-tuple-element.3, f32[1024]{0:T(1024)S(1)} %rsqrt_multiply_fusion, f32[2048]{0:T(1024)S(1)} %add_divide_fusion), kind=kOutput, calls=%fused_computation.12 | convolution fusion | flops 541327360 | bytes 9711616 | tf_op jit(solution)/shard_map/dot_general | solution.py:94
  110.7 0.6 copy-done
  111.3 0.0 copy-start.3
  111.3 0.0 copy-start.1
  111.3 0.6 multiply_reduce_fusion.1
  112.0 8.7 %psum.54 = f32[2048]{0:T(1024)S(1)} all-reduce(f32[2048]{0:T(1024)S(1)} %multiply_reduce_fusion.1), channel_id=1, replica_groups=mesh['zl'=4,'y'=4,'c'=2,'zh'=4,'x'=4] {'x'}, use_global_device_ids=true, to_apply=%region_8.0 | all-reduce | flops 2048 | bytes 16384 | tf_op jit(solution)/shard_map/psum | solution.py:21
  120.7 15.0 %psum.55 = f32[2048]{0:T(1024)S(1)} all-reduce(f32[2048]{0:T(1024)S(1)} %psum.54), channel_id=1, replica_groups=mesh['zl'=4,'y'=4,'c'=2,'zh'=4,'x'=4] {'zh'}, use_global_device_ids=true, to_apply=%region_9.0 | all-reduce | flops 2048 | bytes 16384 | tf_op jit(solution)/shard_map/psum | solution.py:21
  135.7 0.0 copy-done.3
  135.7 0.0 copy-done.1
  135.7 4.5 %fusion = bf16[1024,2048]{1,0:T(8,128)(2,1)S(1)} fusion(f32[2048,1024]{0,1:T(8,128)} %get-tuple-element.3, f32[1024]{0:T(1024)S(1)} %rsqrt_multiply_fusion, f32[2048]{0:T(1024)S(1)} %add_divide_fusion, f32[1024]{0:T(1024)S(1)} %copy-done.1, f32[2048]{0:T(1024)S(1)} %negate_divide_fusion), kind=kLoop, calls=%fused_computation.1 | loop fusion | flops 12582912 | bytes 12607488 | tf_op jit(solution)/shard_map/convert_element_type | solution.py:112
  140.2 5.0 %fusion.8 = f32[2048,128]{1,0:T(8,128)S(1)} fusion(f32[2048,128]{1,0:T(8,128)S(1)} %fusion.5, bf16[1024,128]{1,0:T(8,128)(2,1)S(1)} %bitcast.33, f32[2048,1024]{0,1:T(8,128)} %get-tuple-element.3, f32[1024]{0:T(1024)S(1)} %copy-done.1, f32[2048]{0:T(1024)S(1)} %negate_divide_fusion), kind=kOutput, calls=%fused_computation.15 | convolution fusion | flops 541851648 | bytes 10760192 | tf_op jit(solution)/shard_map/dot_general | solution.py:81
  145.2 1.1 copy.21
  146.3 1.2 convolution_bitcast_fusion
  147.6 4.2 %all_to_all.48 = f32[1,4,4,2,32,128]{5,4,2,1,0,3:T(8,128)S(1)} all-to-all(f32[1,4,4,2,32,128]{5,4,2,1,0,3:T(8,128)S(1)} %copy.22), channel_id=1, replica_groups=mesh['zl'=4,'y'=4,'c'=2,'zh'=4,'x'=4] {'c'}, dimensions={3} | all-to-all | bytes 1048576 | tf_op jit(solution)/shard_map/all_to_all | solution.py:65
  151.7 3.5 %all-to-all-start.3 = ((f32[1,4,4,128,128]{4,3,1,0,2:T(8,128)}), f32[1,4,4,128,128]{4,3,1,0,2:T(8,128)S(1)}, u32[]{:S(2)}, u32[]{:S(2)}) async-start(f32[1,4,4,128,128]{4,3,1,0,2:T(8,128)} %copy.21), calls=%async_computation.3 | async-start | bytes 2097152 | tf_op jit(solution)/shard_map/all_to_all | solution.py:65
  155.3 0.7 copy.23
  156.1 14.8 %all-to-all-done.3 = f32[1,4,4,128,128]{4,3,1,0,2:T(8,128)S(1)} async-done(((f32[1,4,4,128,128]{4,3,1,0,2:T(8,128)}), f32[1,4,4,128,128]{4,3,1,0,2:T(8,128)S(1)}, u32[]{:S(2)}, u32[]{:S(2)}) %all-to-all-start.3) | async-done | bytes 1048608 | tf_op jit(solution)/shard_map/all_to_all | solution.py:65
  170.9 5.8 %all-to-all-start.5 = ((f32[1,4,4,32,128]{4,3,1,0,2:T(8,128)}), f32[1,4,4,32,128]{4,3,1,0,2:T(8,128)S(1)}, u32[]{:S(2)}, u32[]{:S(2)}) async-start(f32[1,4,4,32,128]{4,3,1,0,2:T(8,128)} %copy.23), calls=%async_computation.5 | async-start | bytes 524288 | tf_op jit(solution)/shard_map/all_to_all | solution.py:65
  176.6 0.1 reduce_sum.66
  176.7 7.3 %collective-permute-start = (f32[2,128,128]{2,1,0:T(8,128)S(1)}, f32[2,128,128]{2,1,0:T(8,128)S(1)}, u32[]{:S(2)}, u32[]{:S(2)}) collective-permute-start(f32[2,128,128]{2,1,0:T(8,128)S(1)} %constant_dynamic-slice_fusion.1), channel_id=1, source_target_pairs={{0,8},{4,12},{8,0},{12,4},{1,9},{5,13},{9,1},{13,5},{2,10},{6,14},... | collective-permute-start | bytes 393224 | tf_op jit(solution)/shard_map/ppermute | solution.py:55
  184.0 0.0 all-to-all-done.5
  184.1 0.6 reduce_sum.68
  184.7 3.6 %all-to-all-start.6 = ((f32[4,32,128]{2,1,0:T(8,128)}), f32[4,32,128]{2,1,0:T(8,128)S(1)}, u32[]{:S(2)}, u32[]{:S(2)}) async-start(f32[4,32,128]{2,1,0:T(8,128)} %reduce_sum.68), calls=%async_computation.6 | async-start | bytes 131072 | tf_op jit(solution)/shard_map/all_to_all | solution.py:65
  188.3 12.7 %collective-permute-done = f32[2,128,128]{2,1,0:T(8,128)S(1)} collective-permute-done((f32[2,128,128]{2,1,0:T(8,128)S(1)}, f32[2,128,128]{2,1,0:T(8,128)S(1)}, u32[]{:S(2)}, u32[]{:S(2)}) %collective-permute-start) | collective-permute-done | bytes 131104 | tf_op jit(solution)/shard_map/ppermute | solution.py:55
  201.1 1.9 collective-permute-start.1
  203.0 0.0 all-to-all-done.6
  203.0 0.6 reduce_sum.69
  203.7 7.5 %collective-permute-done.1 = f32[1,128,128]{2,1,0:T(8,128)S(1)} collective-permute-done((f32[1,128,128]{2,1,0:T(8,128)S(1)}, f32[1,128,128]{2,1,0:T(8,128)S(1)}, u32[]{:S(2)}, u32[]{:S(2)}) %collective-permute-start.1) | collective-permute-done | bytes 65568 | tf_op jit(solution)/shard_map/ppermute | solution.py:55
  211.2 0.6 add_bitcast_fusion
  (10 shorter events, 0.2 us)
Async XLA Ops:
  11.5 69.9 %copy-start.2 = (s32[2048]{0:T(1024)S(1)}, s32[2048]{0:T(1024)}, u32[]{:S(2)}) copy-start(s32[2048]{0:T(1024)} %param.9) | copy-start | bytes 24580
  12.2 29.1 %all-to-all-start.2 = ((bf16[4,4,32,128]{3,2,1,0:T(8,128)(2,1)}), bf16[4,4,32,128]{3,2,1,0:T(8,128)(2,1)S(1)}, u32[]{:S(2)}, u32[]{:S(2)}) async-start(bf16[4,4,32,128]{3,2,1,0:T(8,128)(2,1)} %broadcast_in_dim.10), calls=%async_computation.2 | async-start | bytes 262144 | tf_op jit(solution)/shard_map/all_to_all | solution.py:32
  42.2 12.4 %all-to-all-start = ((bf16[4,4,128,128]{3,2,1,0:T(8,128)(2,1)}), bf16[4,4,128,128]{3,2,1,0:T(8,128)(2,1)S(1)}, u32[]{:S(2)}, u32[]{:S(2)}) async-start(bf16[4,4,128,128]{3,2,1,0:T(8,128)(2,1)} %broadcast_in_dim.8), calls=%async_computation | async-start | bytes 1048576 | tf_op jit(solution)/shard_map/all_to_all | solution.py:32
  54.6 50.9 %copy-start.4 = (s32[1024]{0:T(1024)S(1)}, s32[1024]{0:T(1024)}, u32[]{:S(2)}) copy-start(s32[1024]{0:T(1024)} %param.10) | copy-start | bytes 12292
  54.6 50.9 %copy-start.5 = (f32[1024]{0:T(1024)S(1)}, f32[1024]{0:T(1024)}, u32[]{:S(2)}) copy-start(f32[1024]{0:T(1024)} %param.13) | copy-start | bytes 12292
  105.6 5.8 %copy-start = (f32[2048,1024]{0,1:T(8,128)S(1)}, f32[2048,1024]{0,1:T(8,128)}, u32[]{:S(2)}) copy-start(f32[2048,1024]{0,1:T(8,128)} %get-tuple-element.3) | copy-start | bytes 25165828
  111.3 24.4 %copy-start.3 = (f32[2048]{0:T(1024)S(1)}, f32[2048]{0:T(1024)}, u32[]{:S(2)}) copy-start(f32[2048]{0:T(1024)} %param.12) | copy-start | bytes 24580
  111.3 24.4 %copy-start.1 = (f32[1024]{0:T(1024)S(1)}, f32[1024]{0:T(1024)}, u32[]{:S(2)}) copy-start(f32[1024]{0:T(1024)} %param.11) | copy-start | bytes 12292
  151.7 19.2 %all-to-all-start.3 = ((f32[1,4,4,128,128]{4,3,1,0,2:T(8,128)}), f32[1,4,4,128,128]{4,3,1,0,2:T(8,128)S(1)}, u32[]{:S(2)}, u32[]{:S(2)}) async-start(f32[1,4,4,128,128]{4,3,1,0,2:T(8,128)} %copy.21), calls=%async_computation.3 | async-start | bytes 2097152 | tf_op jit(solution)/shard_map/all_to_all | solution.py:65
  170.9 13.2 %all-to-all-start.5 = ((f32[1,4,4,32,128]{4,3,1,0,2:T(8,128)}), f32[1,4,4,32,128]{4,3,1,0,2:T(8,128)S(1)}, u32[]{:S(2)}, u32[]{:S(2)}) async-start(f32[1,4,4,32,128]{4,3,1,0,2:T(8,128)} %copy.23), calls=%async_computation.5 | async-start | bytes 524288 | tf_op jit(solution)/shard_map/all_to_all | solution.py:65
  176.7 24.3 %collective-permute-start = (f32[2,128,128]{2,1,0:T(8,128)S(1)}, f32[2,128,128]{2,1,0:T(8,128)S(1)}, u32[]{:S(2)}, u32[]{:S(2)}) collective-permute-start(f32[2,128,128]{2,1,0:T(8,128)S(1)} %constant_dynamic-slice_fusion.1), channel_id=1, source_target_pairs={{0,8},{4,12},{8,0},{12,4},{1,9},{5,13},{9,1},{13,5},{2,10},{6,14},... | collective-permute-start | bytes 393224 | tf_op jit(solution)/shard_map/ppermute | solution.py:55
  184.7 18.3 %all-to-all-start.6 = ((f32[4,32,128]{2,1,0:T(8,128)}), f32[4,32,128]{2,1,0:T(8,128)S(1)}, u32[]{:S(2)}, u32[]{:S(2)}) async-start(f32[4,32,128]{2,1,0:T(8,128)} %reduce_sum.68), calls=%async_computation.6 | async-start | bytes 131072 | tf_op jit(solution)/shard_map/all_to_all | solution.py:65
  201.1 10.1 %collective-permute-start.1 = (f32[1,128,128]{2,1,0:T(8,128)S(1)}, f32[1,128,128]{2,1,0:T(8,128)S(1)}, u32[]{:S(2)}, u32[]{:S(2)}) collective-permute-start(f32[1,128,128]{2,1,0:T(8,128)S(1)} %constant_dynamic-slice_fusion), channel_id=1, source_target_pairs={{0,4},{4,0},{8,12},{12,8},{1,5},{5,1},{9,13},{13,9},{2,6},{6,2},{1... | collective-permute-start | bytes 196616 | tf_op jit(solution)/shard_map/ppermute | solution.py:55

commit v10 on v9

--- a/solution.py
+++ b/solution.py
@@ -114,12 +114,12 @@
             tangent, men_rows, (((0,), (0,)), ((), ())), preferred_element_type=jnp.float32
         )
         blk = women_terms.shape[0] // (men_sizes[0] * men_sizes[1] * men_sizes[2])
-        women_grad = a2a_scatter(
-            women_terms.reshape(men_sizes + (blk, women_terms.shape[1])),
-            men_sizes,
-            MEN_AXES,
-            ("c", "y", "zl"),
-        )
+        part = women_terms.reshape(men_sizes + (blk, women_terms.shape[1]))
+        bit = lax.axis_index("c")
+        keep = lax.dynamic_index_in_dim(part, bit, axis=2, keepdims=False)
+        send = lax.dynamic_index_in_dim(part, 1 - bit, axis=2, keepdims=False)
+        part = keep + lax.ppermute(send, "c", [(0, 1), (1, 0)])
+        women_grad = a2a_scatter(part, men_sizes[:2], MEN_AXES[:2], ("y", "zl"))
         return (men_grad, women_grad)
 
     return body

time: 213 us -> 202 us (0.948)
  the two profiles are of different devices: /device:TPU:40 before, /device:TPU:42 now
where the time goes in v10:
time: 202 us; the launch traced here: 201 us
  blocking collectives  103 us (51%)
  starting transfers between devices  34.5 us (17%)
  waiting for transfers between devices  27.2 us (13%)
  matrix products  18.4 us (9%)
  other arithmetic  12.4 us (6%)
  local copies, waits for them, and re-layouts  4.82 us (2%)
    psum x7, blocking collectives, nested_psum(): x = lax.psum(x, a)  66.4 us
    all_gather x2, blocking collectives, ordered_gather(): x = lax.all_gather(x, a, axis=0, tiled=False)  26.2 us
    ppermute x2, waiting for transfers between devices, halving_scatter(): got = lax.ppermute(send, a, [(i, i ^ k) for i in range(n)])  19.3 us
    all_to_all x3, starting transfers between devices, a2a_scatter(): x = jnp.sum(lax.all_to_all(x, a, d, 0, tiled=False), axis=0)  13.7 us
    all_to_all x1, blocking collectives, ordered_gather(): lax.all_to_all(jnp.broadcast_to(x[None], (n,) + x.shape), a, 0, 0, tiled=...  10.2 us
    dot_general x2, matrix products, body(): jnp.dot(weighted.astype(jnp.bfloat16), women_rows, preferred_element_type...  10.1 us
    all_to_all x2, starting transfers between devices, ordered_gather(): lax.all_to_all(jnp.broadcast_to(x[None], (n,) + x.shape), a, 0, 0, tiled=...  9.73 us
    ppermute x2, starting transfers between devices, halving_scatter(): got = lax.ppermute(send, a, [(i, i ^ k) for i in range(n)])  9.2 us
  transfers between devices with their start and end apart: 8, of which 5 were waited for; matrix products, arithmetic and copies ran while one was open for 3% of the time, Pallas kernels for 0%

profile of v10, /device:TPU:42, one launch (start us, length us, event | category | flops | bytes accessed | tf_op | source)
XLA Modules:
  0.0 201.0 jit_solution(9942290556441674966)
XLA Ops:
  0.6 0.7 broadcast_in_dim.9
  1.3 10.2 %all_to_all.38 = bf16[4,32,128]{2,1,0:T(8,128)(2,1)S(1)} all-to-all(bf16[4,32,128]{2,1,0:T(8,128)(2,1)S(1)} %broadcast_in_dim.9), channel_id=1, replica_groups=mesh['zl'=4,'y'=4,'c'=2,'zh'=4,'x'=4] {'zl'}, dimensions={0} | all-to-all | bytes 65536 | tf_op jit(solution)/shard_map/all_to_all | solution.py:32
  11.5 0.0 copy-start.2
  11.5 0.7 broadcast_in_dim.10
  12.2 4.9 %all-to-all-start.2 = ((bf16[4,4,32,128]{3,2,1,0:T(8,128)(2,1)}), bf16[4,4,32,128]{3,2,1,0:T(8,128)(2,1)S(1)}, u32[]{:S(2)}, u32[]{:S(2)}) async-start(bf16[4,4,32,128]{3,2,1,0:T(8,128)(2,1)} %broadcast_in_dim.10), calls=%async_computation.2 | async-start | bytes 262144 | tf_op jit(solution)/shard_map/all_to_all | solution.py:32
  17.1 24.2 %all-gather = bf16[512,128]{1,0:T(8,128)(2,1)S(1)} all-gather(bf16[128,128]{1,0:T(8,128)(2,1)} %param.7), channel_id=2, replica_groups=mesh['zl'=4,'y'=4,'c'=2,'zh'=4,'x'=4] {'zh'}, dimensions={0}, use_global_device_ids=true | all-gather | bytes 163840 | tf_op jit(solution)/shard_map/all_gather | solution.py:29
  41.3 0.0 all-to-all-done.2
  41.3 0.9 broadcast_in_dim.8
  42.2 4.8 %all-to-all-start = ((bf16[4,4,128,128]{3,2,1,0:T(8,128)(2,1)}), bf16[4,4,128,128]{3,2,1,0:T(8,128)(2,1)S(1)}, u32[]{:S(2)}, u32[]{:S(2)}) async-start(bf16[4,4,128,128]{3,2,1,0:T(8,128)(2,1)} %broadcast_in_dim.8), calls=%async_computation | async-start | bytes 1048576 | tf_op jit(solution)/shard_map/all_to_all | solution.py:32
  47.0 2.0 all-gather.1
  49.0 4.6 %all-to-all-done = bf16[4,4,128,128]{3,2,1,0:T(8,128)(2,1)S(1)} async-done(((bf16[4,4,128,128]{3,2,1,0:T(8,128)(2,1)}), bf16[4,4,128,128]{3,2,1,0:T(8,128)(2,1)S(1)}, u32[]{:S(2)}, u32[]{:S(2)}) %all-to-all-start) | async-done | bytes 524320 | tf_op jit(solution)/shard_map/all_to_all | solution.py:32
  53.7 0.0 copy-start.4
  53.7 0.0 copy-start.5
  53.7 4.8 %multiply_reduce_fusion.2 = (f32[2048]{0:T(1024)S(1)}, f32[2048,1024]{0,1:T(8,128)}) fusion(f32[1024]{0:T(1024)} %param.11, bf16[2048,128]{1,0:T(8,128)(2,1)S(1)} %bitcast.34, bf16[1024,128]{1,0:T(8,128)(2,1)S(1)} %bitcast.36), kind=kOutput, calls=%fused_computation.7 | convolution fusion | flops 543160320 | bytes 9187328 | tf_op jit(solution)/shard_map/dot_general | solution.py:13
  58.5 9.3 %psum.49 = f32[2048]{0:T(1024)S(1)} all-reduce(f32[2048]{0:T(1024)S(1)} %get-tuple-element.2), channel_id=1, replica_groups=mesh['zl'=4,'y'=4,'c'=2,'zh'=4,'x'=4] {'x'}, use_global_device_ids=true, to_apply=%region_1.0 | all-reduce | flops 2048 | bytes 16384 | tf_op jit(solution)/shard_map/psum | solution.py:21
  67.8 13.0 %psum.50 = f32[2048]{0:T(1024)S(1)} all-reduce(f32[2048]{0:T(1024)S(1)} %psum.49), channel_id=1, replica_groups=mesh['zl'=4,'y'=4,'c'=2,'zh'=4,'x'=4] {'zh'}, use_global_device_ids=true, to_apply=%region_2.0 | all-reduce | flops 2048 | bytes 16384 | tf_op jit(solution)/shard_map/psum | solution.py:21
  80.8 0.0 copy-done.2
  80.8 4.0 %multiply_reduce_fusion = f32[1024]{0:T(1024)S(1)} fusion(f32[2048,1024]{0,1:T(8,128)} %get-tuple-element.3, f32[2048]{0:T(1024)S(1)} %add_divide_fusion), kind=kLoop, calls=%fused_computation.2 | loop fusion | flops 4193280 | bytes 8400896 | tf_op jit(solution)/shard_map/reduce_sum | solution.py:88
  84.8 2.5 %psum.51 = f32[1024]{0:T(1024)S(1)} all-reduce(f32[1024]{0:T(1024)S(1)} %multiply_reduce_fusion), channel_id=1, replica_groups=mesh['zl'=4,'y'=4,'c'=2,'zh'=4,'x'=4] {'c'}, use_global_device_ids=true, to_apply=%region_4.0 | all-reduce | flops 1024 | bytes 8192 | tf_op jit(solution)/shard_map/psum | solution.py:21
  87.3 8.6 %psum.52 = f32[1024]{0:T(1024)S(1)} all-reduce(f32[1024]{0:T(1024)S(1)} %psum.51), channel_id=1, replica_groups=mesh['zl'=4,'y'=4,'c'=2,'zh'=4,'x'=4] {'y'}, use_global_device_ids=true, to_apply=%region_5.0 | all-reduce | flops 1024 | bytes 8192 | tf_op jit(solution)/shard_map/psum | solution.py:21
  95.8 9.1 %psum.53 = f32[1024]{0:T(1024)S(1)} all-reduce(f32[1024]{0:T(1024)S(1)} %psum.52), channel_id=1, replica_groups=mesh['zl'=4,'y'=4,'c'=2,'zh'=4,'x'=4] {'zl'}, use_global_device_ids=true, to_apply=%region_6.0 | all-reduce | flops 1024 | bytes 8192 | tf_op jit(solution)/shard_map/psum | solution.py:21
  104.9 0.0 copy-done.4
  104.9 0.0 copy-done.5
  104.9 0.0 copy-start
  104.9 5.1 %fusion.5 = f32[2048,128]{1,0:T(8,128)S(1)} fusion(bf16[1024,128]{1,0:T(8,128)(2,1)S(1)} %bitcast.37, f32[2048,1024]{0,1:T(8,128)} %get-tuple-element.3, f32[1024]{0:T(1024)S(1)} %rsqrt_multiply_fusion, f32[2048]{0:T(1024)S(1)} %add_divide_fusion), kind=kOutput, calls=%fused_computation.12 | convolution fusion | flops 541327360 | bytes 9711616 | tf_op jit(solution)/shard_map/dot_general | solution.py:94
  110.1 0.6 copy-done
  110.7 0.0 copy-start.3
  110.7 0.0 copy-start.1
  110.7 0.6 multiply_reduce_fusion.1
  111.3 9.0 %psum.54 = f32[2048]{0:T(1024)S(1)} all-reduce(f32[2048]{0:T(1024)S(1)} %multiply_reduce_fusion.1), channel_id=1, replica_groups=mesh['zl'=4,'y'=4,'c'=2,'zh'=4,'x'=4] {'x'}, use_global_device_ids=true, to_apply=%region_8.0 | all-reduce | flops 2048 | bytes 16384 | tf_op jit(solution)/shard_map/psum | solution.py:21
  120.3 15.0 %psum.55 = f32[2048]{0:T(1024)S(1)} all-reduce(f32[2048]{0:T(1024)S(1)} %psum.54), channel_id=1, replica_groups=mesh['zl'=4,'y'=4,'c'=2,'zh'=4,'x'=4] {'zh'}, use_global_device_ids=true, to_apply=%region_9.0 | all-reduce | flops 2048 | bytes 16384 | tf_op jit(solution)/shard_map/psum | solution.py:21
  135.4 0.0 copy-done.3
  135.4 0.0 copy-done.1
  135.4 5.7 %fusion = bf16[1024,2048]{1,0:T(8,128)(2,1)} fusion(f32[2048,1024]{0,1:T(8,128)} %get-tuple-element.3, f32[1024]{0:T(1024)S(1)} %rsqrt_multiply_fusion, f32[2048]{0:T(1024)S(1)} %add_divide_fusion, f32[1024]{0:T(1024)S(1)} %copy-done.1, f32[2048]{0:T(1024)S(1)} %negate_divide_fusion), kind=kLoop, calls=%fused_computation.1 | loop fusion | flops 12582912 | bytes 12607488 | tf_op jit(solution)/shard_map/convert_element_type | solution.py:112
  141.2 5.0 %fusion.8 = f32[2048,128]{1,0:T(8,128)S(1)} fusion(f32[2048,128]{1,0:T(8,128)S(1)} %fusion.5, bf16[1024,128]{1,0:T(8,128)(2,1)S(1)} %bitcast.38, f32[2048,1024]{0,1:T(8,128)} %get-tuple-element.3, f32[1024]{0:T(1024)S(1)} %copy-done.1, f32[2048]{0:T(1024)S(1)} %negate_divide_fusion), kind=kOutput, calls=%fused_computation.15 | convolution fusion | flops 541851648 | bytes 10760192 | tf_op jit(solution)/shard_map/dot_general | solution.py:81
  146.1 1.1 copy.19
  147.2 4.3 %all-to-all-start.3 = ((f32[1,4,4,128,128]{4,3,1,0,2:T(8,128)}), f32[1,4,4,128,128]{4,3,1,0,2:T(8,128)S(1)}, u32[]{:S(2)}, u32[]{:S(2)}) async-start(f32[1,4,4,128,128]{4,3,1,0,2:T(8,128)} %copy.19), calls=%async_computation.3 | async-start | bytes 2097152 | tf_op jit(solution)/shard_map/all_to_all | solution.py:65
  151.5 3.4 %fusion.10 = f32[4,4,2,32,128]{4,3,2,1,0:T(8,128)S(1)} fusion(bf16[4,4,2,32,2048]{4,3,2,1,0:T(8,128)(2,1)} %bitcast.33, bf16[2048,128,1,1,1]{1,0,4,3,2:T(8,128)(2,1)S(1)} %bitcast.35), kind=kOutput, calls=%fused_computation.27 | convolution fusion | flops 536870912 | bytes 5242880 | tf_op jit(solution)/shard_map/dot_general | solution.py:113
  155.0 1.9 collective-permute-start.2
  157.0 1.5 collective-permute-done.2
  158.5 0.7 copy.20
  159.2 1.8 all-to-all-done.3
  161.0 5.8 %all-to-all-start.4 = ((f32[1,4,4,32,128]{4,3,1,0,2:T(8,128)}), f32[1,4,4,32,128]{4,3,1,0,2:T(8,128)S(1)}, u32[]{:S(2)}, u32[]{:S(2)}) async-start(f32[1,4,4,32,128]{4,3,1,0,2:T(8,128)} %copy.20), calls=%async_computation.4 | async-start | bytes 524288 | tf_op jit(solution)/shard_map/all_to_all | solution.py:65
  166.7 0.1 reduce_sum.57
  166.8 7.3 %collective-permute-start = (f32[2,128,128]{2,1,0:T(8,128)S(1)}, f32[2,128,128]{2,1,0:T(8,128)S(1)}, u32[]{:S(2)}, u32[]{:S(2)}) collective-permute-start(f32[2,128,128]{2,1,0:T(8,128)S(1)} %constant_dynamic-slice_fusion.1), channel_id=1, source_target_pairs={{0,8},{4,12},{8,0},{12,4},{1,9},{5,13},{9,1},{13,5},{2,10},{6,14},... | collective-permute-start | bytes 393224 | tf_op jit(solution)/shard_map/ppermute | solution.py:55
  174.2 0.0 all-to-all-done.4
  174.2 0.6 reduce_sum.58
  174.8 3.6 %all-to-all-start.5 = ((f32[4,32,128]{2,1,0:T(8,128)}), f32[4,32,128]{2,1,0:T(8,128)S(1)}, u32[]{:S(2)}, u32[]{:S(2)}) async-start(f32[4,32,128]{2,1,0:T(8,128)} %reduce_sum.58), calls=%async_computation.5 | async-start | bytes 131072 | tf_op jit(solution)/shard_map/all_to_all | solution.py:65
  178.4 11.8 %collective-permute-done = f32[2,128,128]{2,1,0:T(8,128)S(1)} collective-permute-done((f32[2,128,128]{2,1,0:T(8,128)S(1)}, f32[2,128,128]{2,1,0:T(8,128)S(1)}, u32[]{:S(2)}, u32[]{:S(2)}) %collective-permute-start) | collective-permute-done | bytes 131104 | tf_op jit(solution)/shard_map/ppermute | solution.py:55
  190.3 1.9 collective-permute-start.1
  192.2 0.0 all-to-all-done.5
  192.2 0.6 reduce_sum.59
  192.8 7.5 %collective-permute-done.1 = f32[1,128,128]{2,1,0:T(8,128)S(1)} collective-permute-done((f32[1,128,128]{2,1,0:T(8,128)S(1)}, f32[1,128,128]{2,1,0:T(8,128)S(1)}, u32[]{:S(2)}, u32[]{:S(2)}) %collective-permute-start.1) | collective-permute-done | bytes 65568 | tf_op jit(solution)/shard_map/ppermute | solution.py:55
  200.4 0.6 add_bitcast_fusion
  (10 shorter events, 0.2 us)
Async XLA Ops:
  11.5 69.3 %copy-start.2 = (s32[2048]{0:T(1024)S(1)}, s32[2048]{0:T(1024)}, u32[]{:S(2)}) copy-start(s32[2048]{0:T(1024)} %param.9) | copy-start | bytes 24580
  12.2 29.1 %all-to-all-start.2 = ((bf16[4,4,32,128]{3,2,1,0:T(8,128)(2,1)}), bf16[4,4,32,128]{3,2,1,0:T(8,128)(2,1)S(1)}, u32[]{:S(2)}, u32[]{:S(2)}) async-start(bf16[4,4,32,128]{3,2,1,0:T(8,128)(2,1)} %broadcast_in_dim.10), calls=%async_computation.2 | async-start | bytes 262144 | tf_op jit(solution)/shard_map/all_to_all | solution.py:32
  42.2 11.4 %all-to-all-start = ((bf16[4,4,128,128]{3,2,1,0:T(8,128)(2,1)}), bf16[4,4,128,128]{3,2,1,0:T(8,128)(2,1)S(1)}, u32[]{:S(2)}, u32[]{:S(2)}) async-start(bf16[4,4,128,128]{3,2,1,0:T(8,128)(2,1)} %broadcast_in_dim.8), calls=%async_computation | async-start | bytes 1048576 | tf_op jit(solution)/shard_map/all_to_all | solution.py:32
  53.7 51.2 %copy-start.4 = (s32[1024]{0:T(1024)S(1)}, s32[1024]{0:T(1024)}, u32[]{:S(2)}) copy-start(s32[1024]{0:T(1024)} %param.10) | copy-start | bytes 12292
  53.7 51.2 %copy-start.5 = (f32[1024]{0:T(1024)S(1)}, f32[1024]{0:T(1024)}, u32[]{:S(2)}) copy-start(f32[1024]{0:T(1024)} %param.13) | copy-start | bytes 12292
  104.9 5.8 %copy-start = (f32[2048,1024]{0,1:T(8,128)S(1)}, f32[2048,1024]{0,1:T(8,128)}, u32[]{:S(2)}) copy-start(f32[2048,1024]{0,1:T(8,128)} %get-tuple-element.3) | copy-start | bytes 25165828
  110.7 24.7 %copy-start.3 = (f32[2048]{0:T(1024)S(1)}, f32[2048]{0:T(1024)}, u32[]{:S(2)}) copy-start(f32[2048]{0:T(1024)} %param.12) | copy-start | bytes 24580
  110.7 24.7 %copy-start.1 = (f32[1024]{0:T(1024)S(1)}, f32[1024]{0:T(1024)}, u32[]{:S(2)}) copy-start(f32[1024]{0:T(1024)} %param.11) | copy-start | bytes 12292
  147.2 13.8 %all-to-all-start.3 = ((f32[1,4,4,128,128]{4,3,1,0,2:T(8,128)}), f32[1,4,4,128,128]{4,3,1,0,2:T(8,128)S(1)}, u32[]{:S(2)}, u32[]{:S(2)}) async-start(f32[1,4,4,128,128]{4,3,1,0,2:T(8,128)} %copy.19), calls=%async_computation.3 | async-start | bytes 2097152 | tf_op jit(solution)/shard_map/all_to_all | solution.py:65
  155.0 3.4 %collective-permute-start.2 = (f32[4,4,32,128]{3,2,1,0:T(8,128)S(1)}, f32[4,4,32,128]{3,2,1,0:T(8,128)S(1)}, u32[]{:S(2)}, u32[]{:S(2)}) collective-permute-start(f32[4,4,32,128]{3,2,1,0:T(8,128)S(1)} %dynamic-slice_bitcast_fusion), channel_id=1, source_target_pairs={{0,16},{16,0},{1,17},{17,1},{2,18},{18,2},{3,19},{19,3},{4,20},{20... | collective-permute-start | bytes 786440 | tf_op jit(solution)/shard_map/ppermute | solution.py:121
  161.0 13.2 %all-to-all-start.4 = ((f32[1,4,4,32,128]{4,3,1,0,2:T(8,128)}), f32[1,4,4,32,128]{4,3,1,0,2:T(8,128)S(1)}, u32[]{:S(2)}, u32[]{:S(2)}) async-start(f32[1,4,4,32,128]{4,3,1,0,2:T(8,128)} %copy.20), calls=%async_computation.4 | async-start | bytes 524288 | tf_op jit(solution)/shard_map/all_to_all | solution.py:65
  166.8 23.4 %collective-permute-start = (f32[2,128,128]{2,1,0:T(8,128)S(1)}, f32[2,128,128]{2,1,0:T(8,128)S(1)}, u32[]{:S(2)}, u32[]{:S(2)}) collective-permute-start(f32[2,128,128]{2,1,0:T(8,128)S(1)} %constant_dynamic-slice_fusion.1), channel_id=1, source_target_pairs={{0,8},{4,12},{8,0},{12,4},{1,9},{5,13},{9,1},{13,5},{2,10},{6,14},... | collective-permute-start | bytes 393224 | tf_op jit(solution)/shard_map/ppermute | solution.py:55
  174.8 17.4 %all-to-all-start.5 = ((f32[4,32,128]{2,1,0:T(8,128)}), f32[4,32,128]{2,1,0:T(8,128)S(1)}, u32[]{:S(2)}, u32[]{:S(2)}) async-start(f32[4,32,128]{2,1,0:T(8,128)} %reduce_sum.58), calls=%async_computation.5 | async-start | bytes 131072 | tf_op jit(solution)/shard_map/all_to_all | solution.py:65
  190.3 10.1 %collective-permute-start.1 = (f32[1,128,128]{2,1,0:T(8,128)S(1)}, f32[1,128,128]{2,1,0:T(8,128)S(1)}, u32[]{:S(2)}, u32[]{:S(2)}) collective-permute-start(f32[1,128,128]{2,1,0:T(8,128)S(1)} %constant_dynamic-slice_fusion), channel_id=1, source_target_pairs={{0,4},{4,0},{8,12},{12,8},{1,5},{5,1},{9,13},{13,9},{2,6},{6,2},{1... | collective-permute-start | bytes 196616 | tf_op jit(solution)/shard_map/ppermute | solution.py:55
